TPU v7x, 256 devices: a whole 4x4x8 slice. The times are simulated.
256 devices in a mesh: section: 32 (over z_hi, y, core), tensor: 8 (over z_lo, x).
Axes of the slice: x: 4, y: 4, z: 8 (z_hi: 4, z_lo: 2; z = z_hi * 2 + z_lo), core: 2. Of those that a mesh axis runs over, the one named last changes fastest.
Arguments:
- acts: bfloat16 [32, 512, 3072], P('section', 'tensor'), may hold values from -6 to 6
- sides: bfloat16 [32, 512, 3072], P('section', 'tensor'), may hold values from -6 to 6
- gains: float32 [32, 3072], P('section'), may hold values from 0.1 to 1.9
- weights: bfloat16 [32, 6144, 3072], P('section', None, 'tensor'), may hold values from -0.078125 to 0.078125
- back_acts: bfloat16 [32, 512, 3072], P('section', 'tensor'), may hold values from -6 to 6
- back_sides: bfloat16 [32, 512, 3072], P('section', 'tensor'), may hold values from -6 to 6
- back_grads: bfloat16 [32, 512, 3072], P('section', 'tensor'), may hold values from -6 to 6
Outputs:
- received: bfloat16 [32, 512, 3072], P('section', 'tensor')
- mirrored: bfloat16 [32, 512, 3072], P('section', 'tensor')
- grad_received: bfloat16 [32, 512, 3072], P('section', 'tensor')
- weight_grads: bfloat16 [32, 6144, 3072], P('section', None, 'tensor')
- gain_grads: float32 [32, 3072], P('section')
All inputs are finite; a program needn't handle non-finite values.
Results may differ from a plain program's by a relative error of at most 0.015.
Values may be sent and summed in bfloat16 or wider, within the bound.
No kernel may reach another device: no remote copies, remote signals or barrier semaphores. Data moves between devices by JAX's collectives and lax.ppermute only.
A program may use at most 128 MiB of HBM per device.

v0:
```python
import jax
import jax.numpy as jnp
from jax import lax
from jax.sharding import PartitionSpec as P

epsilon = 1e-06
tanh_scale = 0.7978845608028654
cubic_term = 0.044715


def swapped(block, axis, apart):
    count = lax.axis_size(axis)
    route = []
    for low in range(count):
        high = low | 1 << apart
        if high != low and high < count:
            route += [(low, high), (high, low)]
    return lax.ppermute(block, axis, route)


def shifted(block, axis, distance):
    devices = range(lax.axis_size(axis))
    route = [((i - distance) % len(devices), i) for i in devices]
    return lax.ppermute(block, axis, route)


def gelu_value(inputs):
    inside = tanh_scale * (inputs + cubic_term * inputs * inputs * inputs)
    return 0.5 * inputs * (1.0 + jnp.tanh(inside))


def gelu_slope(inputs):
    inside = tanh_scale * (inputs + cubic_term * inputs * inputs * inputs)
    bent = jnp.tanh(inside)
    return 0.5 * (1.0 + bent) + 0.5 * inputs * (1.0 - bent * bent) * tanh_scale * (
        1.0 + 3.0 * cubic_term * inputs * inputs
    )


def normalize(rows_in, gain):
    xfloat = rows_in.astype(jnp.float32)
    rinv = lax.rsqrt(jnp.mean(xfloat * xfloat, axis=-1, keepdims=True) + epsilon)
    return (xfloat, rinv, (xfloat * rinv * gain).astype(jnp.bfloat16))


def mirror(payload):
    sections = lax.axis_size("section")
    levels = sections.bit_length() - 1
    for bit_idx in range(levels):
        payload = swapped(payload, "section", bit_idx)
    return payload


def on_device(acts, sides, gains, weights, back_acts, back_sides, back_grads):
    sections = lax.axis_size("section")
    middle = sections // 2
    section_idx = lax.axis_index("section")
    gain = gains[0]
    weight_all = weights[0]
    rows, width = acts[0].shape
    w_top = weight_all[:width]
    w_bottom = weight_all[width:]
    xfloat, rinv, normed = normalize(acts[0], gain)
    normed_all, side_all = (
        lax.all_gather(normed, "tensor", axis=0, tiled=True),
        lax.all_gather(sides[0], "tensor", axis=0, tiled=True),
    )
    hidden = jnp.dot(normed_all, w_top, preferred_element_type=jnp.float32) + jnp.dot(
        side_all, w_bottom, preferred_element_type=jnp.float32
    )
    update = lax.all_to_all(
        gelu_value(hidden).astype(jnp.bfloat16), "tensor", split_axis=0, concat_axis=1, tiled=True
    ).astype(jnp.float32)
    out_rows = (xfloat + update).astype(jnp.bfloat16)
    received = shifted(out_rows, "section", 1)
    bfloat, brinv, bnormed = normalize(back_acts[0], gain)
    bnormed_all, bside_all = (
        lax.all_gather(bnormed, "tensor", axis=0, tiled=True),
        lax.all_gather(back_sides[0], "tensor", axis=0, tiled=True),
    )
    bhidden = jnp.dot(bnormed_all, w_top, preferred_element_type=jnp.float32) + jnp.dot(
        bside_all, w_bottom, preferred_element_type=jnp.float32
    )
    grad_cols = lax.all_to_all(back_grads[0], "tensor", split_axis=1, concat_axis=0, tiled=True)
    dhidden = (grad_cols.astype(jnp.float32) * gelu_slope(bhidden)).astype(jnp.bfloat16)
    contract = (((0,), (0,)), ((), ()))
    grad_top = lax.dot_general(bnormed_all, dhidden, contract, preferred_element_type=jnp.float32)
    grad_bottom = lax.dot_general(bside_all, dhidden, contract, preferred_element_type=jnp.float32)
    weight_grads = jnp.concatenate([grad_top, grad_bottom], axis=0).astype(jnp.bfloat16)
    across = (((1,), (1,)), ((), ()))
    dfused = lax.psum_scatter(
        lax.dot_general(dhidden, weight_all, across, preferred_element_type=jnp.float32).astype(
            jnp.bfloat16
        ),
        "tensor",
        scatter_dimension=0,
        tiled=True,
    ).astype(jnp.float32)
    dnormed = dfused[:, :width]
    dside = dfused[:, width:].astype(jnp.bfloat16)
    gain_part = jnp.sum(dnormed * bfloat * brinv, axis=0)
    gain_grad = lax.psum(gain_part, "tensor")
    scaled = gain * dnormed
    dnorm_in = brinv * scaled - bfloat * brinv * brinv * brinv * jnp.mean(
        scaled * bfloat, axis=-1, keepdims=True
    )
    dx_rows = (back_grads[0].astype(jnp.float32) + dnorm_in).astype(jnp.bfloat16)
    grad_received = shifted(dx_rows, "section", -1)
    payload = jnp.where(section_idx < middle, out_rows, dside)
    mirrored = mirror(payload)
    return (
        received[None],
        mirrored[None],
        grad_received[None],
        weight_grads[None],
        gain_grad[None],
    )


def solution(mesh):
    placed = (
        P("section", "tensor", None),
        P("section", "tensor", None),
        P("section", None),
        P("section", None, "tensor"),
        P("section", "tensor", None),
        P("section", "tensor", None),
        P("section", "tensor", None),
    )
    return jax.shard_map(
        on_device,
        mesh=mesh,
        in_specs=placed,
        out_specs=(
            P("section", "tensor", None),
            P("section", "tensor", None),
            P("section", "tensor", None),
            P("section", None, "tensor"),
            P("section", None),
        ),
        check_vma=False,
    )
```

profile of v0, /device:TPU:32, one launch (start us, length us, event | category | flops | bytes accessed | tf_op | source)
XLA Modules:
  0.0 415.7 jit_solution(7512101617935437952)
XLA Ops:
  8.4 1.9 fusion.31
  12.9 5.8 %all-to-all-start.1 = ((bf16[64,8,384]{2,0,1:T(8,128)(2,1)}), bf16[64,8,384]{2,0,1:T(8,128)(2,1)S(1)}, u32[]{:S(2)}, u32[]{:S(2)}) async-start(bf16[64,8,384]{2,0,1:T(8,128)(2,1)} %copy.13), calls=%async_computation.1 | async-start | bytes 786432 | tf_op jit(solution)/shard_map/all_to_all | solution.py:84
  18.7 39.9 %all-gather.9.cloned.1.call-done = bf16[512,3072]{1,0:T(8,128)(2,1)} async-done(((bf16[64,3072]{1,0:T(8,128)(2,1)}), bf16[512,3072]{1,0:T(8,128)(2,1)}) %all-gather.9.cloned.1.call-update) | async-done | bytes 3145744 | tf_op jit(solution)/shard_map/all_gather | solution.py:78
  58.6 4.4 %fusion.10 = f32[512,384]{1,0:T(8,128)S(1)} fusion(bf16[512,3072]{1,0:T(8,128)(2,1)} %all-gather.9.cloned.1.call-done, bf16[1,6144,384]{2,1,0:T(8,128)(2,1)} %param.10), kind=kOutput, calls=%fused_computation.14 | convolution fusion | flops 1207959552 | bytes 6291456 | tf_op jit(solution)/shard_map/dot_general | solution.py:81
  63.0 43.7 %all-gather.13.cloned.1.call-done = bf16[1,512,3072]{2,1,0:T(8,128)(2,1)} async-done(((bf16[1,64,3072]{2,1,0:T(8,128)(2,1)}), bf16[1,512,3072]{2,1,0:T(8,128)(2,1)}) %all-gather.13.cloned.1.call-update) | async-done | bytes 3145744 | tf_op jit(solution)/shard_map/all_gather | solution.py:79
  106.7 4.9 %fusion.48 = bf16[512,384]{1,0:T(8,128)(2,1)S(1)} fusion(f32[512,384]{1,0:T(8,128)S(1)} %fusion.10, bf16[1,6144,384]{2,1,0:T(8,128)(2,1)} %param.10, bf16[1,512,3072]{2,1,0:T(8,128)(2,1)} %all-gather.13.cloned.1.call-done, bf16[64,8,384]{2,0,1:T(8,128)(2,1)S(1)} %all-to-all-done.1), kind=kOutput, calls=%fused_computation.55 | convolution fusion | flops 1212088320 | bytes 7077888 | tf_op jit(solution)/shard_map/dot_general | solution.py:81
  111.5 7.8 %convolution_convert_fusion = bf16[512,6144]{1,0:T(8,128)(2,1)} fusion(bf16[512,384]{1,0:T(8,128)(2,1)S(1)} %fusion.48, bf16[1,6144,384]{2,1,0:T(8,128)(2,1)} %param.10), kind=kOutput, calls=%fused_computation | convolution fusion | flops 2419064832 | bytes 11403264 | tf_op jit(solution)/shard_map/dot_general | solution.py:92
  120.5 74.3 %reduce-scatter.2.cloned.1.call-done = bf16[64,6144]{1,0:T(8,128)(2,1)} async-done(((bf16[512,6144]{1,0:T(8,128)(2,1)}), bf16[64,6144]{1,0:T(8,128)(2,1)}) %reduce-scatter.2.cloned.1.call-update) | async-done | bytes 786448 | tf_op jit(solution)/shard_map/reduce_scatter | solution.py:91
  196.1 2.2 fusion.36
  198.9 44.9 %all-gather.7.cloned.1.call-done = bf16[512,3072]{1,0:T(8,128)(2,1)} async-done(((bf16[64,3072]{1,0:T(8,128)(2,1)}), bf16[512,3072]{1,0:T(8,128)(2,1)}) %all-gather.7.cloned.1.call-update) | async-done | bytes 3145744 | tf_op jit(solution)/shard_map/all_gather | solution.py:65
  243.8 4.4 %fusion.12 = f32[512,384]{1,0:T(8,128)S(1)} fusion(bf16[512,3072]{1,0:T(8,128)(2,1)} %all-gather.7.cloned.1.call-done, bf16[1,6144,384]{2,1,0:T(8,128)(2,1)} %param.10), kind=kOutput, calls=%fused_computation.16 | convolution fusion | flops 1207959552 | bytes 6291456 | tf_op jit(solution)/shard_map/dot_general | solution.py:68
  248.2 43.6 %all-gather.11.cloned.1.call-done = bf16[1,512,3072]{2,1,0:T(8,128)(2,1)} async-done(((bf16[1,64,3072]{2,1,0:T(8,128)(2,1)}), bf16[1,512,3072]{2,1,0:T(8,128)(2,1)}) %all-gather.11.cloned.1.call-update) | async-done | bytes 3145744 | tf_op jit(solution)/shard_map/all_gather | solution.py:66
  291.8 5.3 %fusion.41 = bf16[512,384]{1,0:T(8,128)(2,1)} fusion(f32[512,384]{1,0:T(8,128)S(1)} %fusion.12, bf16[1,6144,384]{2,1,0:T(8,128)(2,1)} %param.10, bf16[1,512,3072]{2,1,0:T(8,128)(2,1)} %all-gather.11.cloned.1.call-done), kind=kOutput, calls=%fused_computation.48 | convolution fusion | flops 1209925632 | bytes 6684672 | tf_op jit(solution)/shard_map/dot_general | solution.py:68
  297.1 5.4 %all-to-all-start = ((bf16[8,64,384]{2,1,0:T(8,128)(2,1)}), bf16[8,64,384]{2,1,0:T(8,128)(2,1)S(1)}, u32[]{:S(2)}, u32[]{:S(2)}) async-start(bf16[8,64,384]{2,1,0:T(8,128)(2,1)} %bitcast.6), calls=%async_computation | async-start | bytes 786432 | tf_op jit(solution)/shard_map/all_to_all | solution.py:71
  302.5 6.5 %all-to-all-done = bf16[8,64,384]{2,1,0:T(8,128)(2,1)S(1)} async-done(((bf16[8,64,384]{2,1,0:T(8,128)(2,1)}), bf16[8,64,384]{2,1,0:T(8,128)(2,1)S(1)}, u32[]{:S(2)}, u32[]{:S(2)}) %all-to-all-start) | async-done | bytes 393248 | tf_op jit(solution)/shard_map/all_to_all | solution.py:71
  312.7 9.7 %collective-permute-done.2 = bf16[64,3072]{1,0:T(8,128)(2,1)S(1)} collective-permute-done((bf16[64,3072]{1,0:T(8,128)(2,1)S(1)}, bf16[64,3072]{1,0:T(8,128)(2,1)S(1)}, u32[]{:S(2)}, u32[]{:S(2)}) %collective-permute-start.2) | collective-permute-done | bytes 393248 | tf_op jit(solution)/shard_map/ppermute | solution.py:18
  322.3 3.0 collective-permute-start.3
  325.3 8.8 %collective-permute-done.3 = bf16[64,3072]{1,0:T(8,128)(2,1)S(1)} collective-permute-done((bf16[64,3072]{1,0:T(8,128)(2,1)S(1)}, bf16[64,3072]{1,0:T(8,128)(2,1)S(1)}, u32[]{:S(2)}, u32[]{:S(2)}) %collective-permute-start.3) | collective-permute-done | bytes 393248 | tf_op jit(solution)/shard_map/ppermute | solution.py:18
  334.1 2.5 collective-permute-start.4
  340.4 2.9 collective-permute-start.6
  343.3 8.8 %collective-permute-done.4 = bf16[64,3072]{1,0:T(8,128)(2,1)S(1)} collective-permute-done((bf16[64,3072]{1,0:T(8,128)(2,1)S(1)}, bf16[64,3072]{1,0:T(8,128)(2,1)S(1)}, u32[]{:S(2)}, u32[]{:S(2)}) %collective-permute-start.4) | collective-permute-done | bytes 393248 | tf_op jit(solution)/shard_map/ppermute | solution.py:18
  352.1 3.0 collective-permute-start.5
  355.1 2.7 pad_maximum_fusion
  357.8 49.1 %psum.7 = f32[1,3072]{1,0:T(1,128)} all-reduce(f32[1,3072]{1,0:T(1,128)S(1)} %bitcast.91), channel_id=1, replica_groups=mesh['section'=32,'tensor'=8] {'tensor'}, use_global_device_ids=true, to_apply=%region_5.0 | all-reduce | flops 3072 | bytes 24576 | tf_op jit(solution)/shard_map/psum | solution.py:102
  (48 shorter events, 16.4 us)
Async XLA Ops:
  7.2 51.4 %all-gather.9.cloned.1.call-start = ((), (), s32[]{:S(2)}) async-start(), calls=%async_computation.4 | async-start | bytes 3538944 | tf_op jit(solution)/shard_map/all_gather | solution.py:78
  10.3 96.3 %all-gather.13.cloned.1.call-start = ((), (), s32[]{:S(2)}) async-start(), calls=%async_computation.7 | async-start | bytes 3538944 | tf_op jit(solution)/shard_map/all_gather | solution.py:79
  12.9 50.0 %all-to-all-start.1 = ((bf16[64,8,384]{2,0,1:T(8,128)(2,1)}), bf16[64,8,384]{2,0,1:T(8,128)(2,1)S(1)}, u32[]{:S(2)}, u32[]{:S(2)}) async-start(bf16[64,8,384]{2,0,1:T(8,128)(2,1)} %copy.13), calls=%async_computation.1 | async-start | bytes 786432 | tf_op jit(solution)/shard_map/all_to_all | solution.py:84
  18.7 176.1 %reduce-scatter.2.cloned.1.call-start = ((), (), s32[]{:S(2)}) async-start(), calls=%async_computation.5 | async-start | bytes 7077888 | tf_op jit(solution)/shard_map/reduce_scatter | solution.py:91
  119.3 1.0 copy-start.1
  119.3 75.5 %copy-start = (bf16[1,64,3072]{2,1,0:T(8,128)(2,1)S(1)}, bf16[1,64,3072]{2,1,0:T(8,128)(2,1)}, u32[]{:S(2)}) copy-start(bf16[1,64,3072]{2,1,0:T(8,128)(2,1)} %param.11) | copy-start | bytes 1179652
  119.3 75.5 %copy-start.4 = (f32[1,3072]{1,0:T(1,128)S(1)}, f32[1,3072]{1,0:T(1,128)}, u32[]{:S(2)}) copy-start(f32[1,3072]{1,0:T(1,128)} %param.9) | copy-start | bytes 36868
  119.3 76.8 %copy-start.3 = (bf16[1,64,3072]{2,1,0:T(8,128)(2,1)S(1)}, bf16[1,64,3072]{2,1,0:T(8,128)(2,1)}, u32[]{:S(2)}) copy-start(bf16[1,64,3072]{2,1,0:T(8,128)(2,1)} %param.13) | copy-start | bytes 1179652
  119.4 124.5 %all-gather.7.cloned.1.call-start = ((), (), s32[]{:S(2)}) async-start(), calls=%async_computation.3 | async-start | bytes 3538944 | tf_op jit(solution)/shard_map/all_gather | solution.py:65
  198.3 93.4 %all-gather.11.cloned.1.call-start = ((), (), s32[]{:S(2)}) async-start(), calls=%async_computation.6 | async-start | bytes 3538944 | tf_op jit(solution)/shard_map/all_gather | solution.py:66
  297.1 12.1 %copy-start.2 = (bf16[64,6144]{1,0:T(8,128)(2,1)S(1)}, bf16[64,6144]{1,0:T(8,128)(2,1)}, u32[]{:S(2)}) copy-start(bf16[64,6144]{1,0:T(8,128)(2,1)} %reduce-scatter.2.cloned.1.call-done) | copy-start | bytes 2359300
  297.1 11.9 %all-to-all-start = ((bf16[8,64,384]{2,1,0:T(8,128)(2,1)}), bf16[8,64,384]{2,1,0:T(8,128)(2,1)S(1)}, u32[]{:S(2)}, u32[]{:S(2)}) async-start(bf16[8,64,384]{2,1,0:T(8,128)(2,1)} %bitcast.6), calls=%async_computation | async-start | bytes 786432 | tf_op jit(solution)/shard_map/all_to_all | solution.py:71
  309.0 27.6 %copy-start.6 = (bf16[1,512,3072]{2,1,0:T(8,128)(2,1)S(1)}, bf16[1,512,3072]{2,1,0:T(8,128)(2,1)}, u32[]{:S(2)}) copy-start(bf16[1,512,3072]{2,1,0:T(8,128)(2,1)} %all-gather.13.cloned.1.call-done) | copy-start | bytes 9437188
  309.3 29.2 %copy-start.5 = (bf16[512,3072]{1,0:T(8,128)(2,1)S(1)}, bf16[512,3072]{1,0:T(8,128)(2,1)}, u32[]{:S(2)}) copy-start(bf16[512,3072]{1,0:T(8,128)(2,1)} %all-gather.9.cloned.1.call-done) | copy-start | bytes 9437188
  309.4 1.8 collective-permute-start.1
  311.2 11.2 %collective-permute-start.2 = (bf16[64,3072]{1,0:T(8,128)(2,1)S(1)}, bf16[64,3072]{1,0:T(8,128)(2,1)S(1)}, u32[]{:S(2)}, u32[]{:S(2)}) collective-permute-start(bf16[64,3072]{1,0:T(8,128)(2,1)S(1)} %collective-permute-done.1), channel_id=1, source_target_pairs={{0,16},{16,0},{8,24},{24,8},{32,48},{48,32},{40,56},{56,40},{64,80... | collective-permute-start | bytes 1179656 | tf_op jit(solution)/shard_map/ppermute | solution.py:18
  322.3 11.8 %collective-permute-start.3 = (bf16[64,3072]{1,0:T(8,128)(2,1)S(1)}, bf16[64,3072]{1,0:T(8,128)(2,1)S(1)}, u32[]{:S(2)}, u32[]{:S(2)}) collective-permute-start(bf16[64,3072]{1,0:T(8,128)(2,1)S(1)} %collective-permute-done.2), channel_id=1, source_target_pairs={{0,32},{32,0},{8,40},{40,8},{16,48},{48,16},{24,56},{56,24},{64,96... | collective-permute-start | bytes 1179656 | tf_op jit(solution)/shard_map/ppermute | solution.py:18
  334.1 17.9 %collective-permute-start.4 = (bf16[64,3072]{1,0:T(8,128)(2,1)S(1)}, bf16[64,3072]{1,0:T(8,128)(2,1)S(1)}, u32[]{:S(2)}, u32[]{:S(2)}) collective-permute-start(bf16[64,3072]{1,0:T(8,128)(2,1)S(1)} %collective-permute-done.3), channel_id=1, source_target_pairs={{0,64},{64,0},{8,72},{72,8},{16,80},{80,16},{24,88},{88,24},{32,96... | collective-permute-start | bytes 1179656 | tf_op jit(solution)/shard_map/ppermute | solution.py:18
  340.4 66.5 %collective-permute-start.6 = (bf16[64,3072]{1,0:T(8,128)(2,1)S(1)}, bf16[64,3072]{1,0:T(8,128)(2,1)S(1)}, u32[]{:S(2)}, u32[]{:S(2)}) collective-permute-start(bf16[64,3072]{1,0:T(8,128)(2,1)S(1)} %get-tuple-element.9), channel_id=1, source_target_pairs={{8,0},{16,8},{24,16},{32,24},{40,32},{48,40},{56,48},{64,56},{72,6... | collective-permute-start | bytes 1179656 | tf_op jit(solution)/shard_map/ppermute | solution.py:24
  343.3 63.6 %collective-permute-start = (bf16[64,3072]{1,0:T(8,128)(2,1)S(1)}, bf16[64,3072]{1,0:T(8,128)(2,1)S(1)}, u32[]{:S(2)}, u32[]{:S(2)}) collective-permute-start(bf16[64,3072]{1,0:T(8,128)(2,1)S(1)} %get-tuple-element.8), channel_id=1, source_target_pairs={{248,0},{0,8},{8,16},{16,24},{24,32},{32,40},{40,48},{48,56},{56,6... | collective-permute-start | bytes 1179656 | tf_op jit(solution)/shard_map/ppermute | solution.py:24
  352.1 54.8 %collective-permute-start.5 = (bf16[64,3072]{1,0:T(8,128)(2,1)S(1)}, bf16[64,3072]{1,0:T(8,128)(2,1)S(1)}, u32[]{:S(2)}, u32[]{:S(2)}) collective-permute-start(bf16[64,3072]{1,0:T(8,128)(2,1)S(1)} %collective-permute-done.4), channel_id=1, source_target_pairs={{0,128},{128,0},{8,136},{136,8},{16,144},{144,16},{24,152},{152,24... | collective-permute-start | bytes 1179656 | tf_op jit(solution)/shard_map/ppermute | solution.py:18
Sparse Core Ops, SparseCore 0:
  10.5 48.0 all-gather.8
  60.3 46.2 all-gather.12
  119.5 75.2 reduce-scatter.1
  198.5 45.3 all-gather.6
  245.4 46.2 all-gather.10
where the time goes:
time: 421 us; the launch traced here: 416 us
  waiting for transfers between devices  283 us (67%)
  blocking collectives  49.1 us (12%)
  matrix products  30.5 us (7%)
  starting transfers between devices  24.4 us (6%)
  between operations  13.9 us (3%)
  other arithmetic  9.67 us (2%)
  local copies, waits for them, and re-layouts  5.07 us (1%)
    reduce_scatter x1, waiting for transfers between devices, on_device(): lax.psum_scatter(lax.dot_general(dhidden, weight_all, across, preferred_e...  74.3 us
    psum x1, blocking collectives, on_device(): gain_grad = lax.psum(gain_part, 'tensor')  49.1 us
    all_gather x1, waiting for transfers between devices, on_device(): lax.all_gather(normed, 'tensor', axis=0, tiled=True)  44.9 us
    all_gather x1, waiting for transfers between devices, on_device(): lax.all_gather(back_sides[0], 'tensor', axis=0, tiled=True)  43.7 us
    all_gather x1, waiting for transfers between devices, on_device(): lax.all_gather(sides[0], 'tensor', axis=0, tiled=True)  43.6 us
    all_gather x1, waiting for transfers between devices, on_device(): lax.all_gather(bnormed, 'tensor', axis=0, tiled=True)  39.9 us
    ppermute x5, waiting for transfers between devices, swapped(): return lax.ppermute(block, axis, route)  29 us
    ppermute x5, starting transfers between devices, swapped(): return lax.ppermute(block, axis, route)  10.2 us
  transfers between devices with their start and end apart: 14, of which 10 were waited for; matrix products, arithmetic and copies ran while one was open for 4% of the time, Pallas kernels for 0%

commit v1 on v0

v1 whole, which is shorter than its diff:
```python
import jax
import jax.numpy as jnp
from jax import lax
from jax.sharding import PartitionSpec as P

epsilon = 1e-06
tanh_scale = 0.7978845608028654
cubic_term = 0.044715


def shifted(block, axis, distance):
    devices = range(lax.axis_size(axis))
    route = [((i - distance) % len(devices), i) for i in devices]
    return lax.ppermute(block, axis, route)


def gelu_value(inputs):
    inside = tanh_scale * (inputs + cubic_term * inputs * inputs * inputs)
    return 0.5 * inputs * (1.0 + jnp.tanh(inside))


def gelu_slope(inputs):
    inside = tanh_scale * (inputs + cubic_term * inputs * inputs * inputs)
    bent = jnp.tanh(inside)
    return 0.5 * (1.0 + bent) + 0.5 * inputs * (1.0 - bent * bent) * tanh_scale * (
        1.0 + 3.0 * cubic_term * inputs * inputs
    )


def normalize(rows_in, gain):
    xfloat = rows_in.astype(jnp.float32)
    rinv = lax.rsqrt(jnp.mean(xfloat * xfloat, axis=-1, keepdims=True) + epsilon)
    return (xfloat, rinv, (xfloat * rinv * gain).astype(jnp.bfloat16))


def gathered(block, axis):
    count = lax.axis_size(axis)
    copies = jnp.broadcast_to(block[None], (count,) + block.shape)
    copies = copies.reshape(count * block.shape[0], block.shape[1])
    return lax.all_to_all(copies, axis, 0, 0, tiled=True)


def on_device(acts, sides, gains, weights, back_acts, back_sides, back_grads):
    sections = lax.axis_size("section")
    count = lax.axis_size("tensor")
    middle = sections // 2
    section_idx = lax.axis_index("section")
    gain = gains[0]
    weight_all = weights[0]
    rows, width = acts[0].shape

    xfloat, rinv, normed = normalize(acts[0], gain)
    joined_all = gathered(jnp.concatenate([normed, sides[0]], axis=1), "tensor")
    hidden = jnp.dot(joined_all, weight_all, preferred_element_type=jnp.float32)
    update = lax.all_to_all(
        gelu_value(hidden).astype(jnp.bfloat16), "tensor", split_axis=0, concat_axis=1, tiled=True
    ).astype(jnp.float32)
    out_rows = (xfloat + update).astype(jnp.bfloat16)
    received = shifted(out_rows, "section", 1)
    ahead = lax.ppermute(
        out_rows, "section", [(s, sections - 1 - s) for s in range(middle)]
    )

    raw_all = gathered(jnp.concatenate([back_acts[0], back_sides[0]], axis=1), "tensor")
    bfloat_all, brinv_all, bnormed_all = normalize(raw_all[:, :width], gain)
    bfused_all = jnp.concatenate([bnormed_all, raw_all[:, width:]], axis=1)
    bhidden = jnp.dot(bfused_all, weight_all, preferred_element_type=jnp.float32)
    grad_cols = lax.all_to_all(back_grads[0], "tensor", split_axis=1, concat_axis=0, tiled=True)
    dhidden = (grad_cols.astype(jnp.float32) * gelu_slope(bhidden)).astype(jnp.bfloat16)
    contract = (((0,), (0,)), ((), ()))
    weight_grads = lax.dot_general(
        bfused_all, dhidden, contract, preferred_element_type=jnp.float32
    ).astype(jnp.bfloat16)
    across = (((1,), (1,)), ((), ()))
    term = lax.dot_general(
        dhidden, weight_all, across, preferred_element_type=jnp.float32
    ).astype(jnp.bfloat16)
    gain_part = jnp.sum(term[:, :width].astype(jnp.float32) * bfloat_all * brinv_all, axis=0)
    part_hi = gain_part.astype(jnp.bfloat16)
    part_lo = (gain_part - part_hi.astype(jnp.float32)).astype(jnp.bfloat16)
    extra = jnp.concatenate([part_hi, part_lo])[None, None]
    send = jnp.concatenate(
        [term.reshape(count, rows, 2 * width), jnp.broadcast_to(extra, (count, 1, 2 * width))], axis=1
    ).reshape(count * (rows + 1), 2 * width)
    got = lax.all_to_all(send, "tensor", 0, 0, tiled=True).reshape(count, rows + 1, 2 * width)
    dfused = jnp.sum(got[:, :rows].astype(jnp.float32), axis=0)
    shares = got[:, rows].astype(jnp.float32)
    gain_grad = jnp.sum(shares[:, :width] + shares[:, width:], axis=0)
    dnormed = dfused[:, :width]
    dside = dfused[:, width:].astype(jnp.bfloat16)
    bfloat, brinv, _ = normalize(back_acts[0], gain)
    scaled = gain * dnormed
    dnorm_in = brinv * scaled - bfloat * brinv * brinv * brinv * jnp.mean(
        scaled * bfloat, axis=-1, keepdims=True
    )
    dx_rows = (back_grads[0].astype(jnp.float32) + dnorm_in).astype(jnp.bfloat16)
    grad_received = shifted(dx_rows, "section", -1)
    behind = lax.ppermute(
        dside, "section", [(s, sections - 1 - s) for s in range(middle, sections)]
    )
    mirrored = jnp.where(section_idx >= middle, ahead, behind)
    return (
        received[None],
        mirrored[None],
        grad_received[None],
        weight_grads[None],
        gain_grad[None],
    )


def solution(mesh):
    placed = (
        P("section", "tensor", None),
        P("section", "tensor", None),
        P("section", None),
        P("section", None, "tensor"),
        P("section", "tensor", None),
        P("section", "tensor", None),
        P("section", "tensor", None),
    )
    return jax.shard_map(
        on_device,
        mesh=mesh,
        in_specs=placed,
        out_specs=(
            P("section", "tensor", None),
            P("section", "tensor", None),
            P("section", "tensor", None),
            P("section", None, "tensor"),
            P("section", None),
        ),
        check_vma=False,
    )
```

time: 421 us -> 345 us (0.82)
  waiting for transfers between devices: 283 us -> 166 us
  blocking collectives: 49.1 us -> 75.8 us
  other arithmetic: 9.67 us -> 24.8 us
  between operations: 13.9 us -> 0.87 us
  starting transfers between devices: 24.4 us -> 37.2 us
  local copies, waits for them, and re-layouts: 5.07 us -> 9.67 us
  matrix products: 30.5 us -> 26 us
    all_gather x4 -> x0, waiting for transfers between devices: 172 us -> none  [the longest x1 44.9 us: on_device(): lax.all_gather(normed, 'tensor', axis=0, tiled=True)]
    all_to_all x0 -> x2, waiting for transfers between devices: none -> 147 us  [the longest x1 78.4 us: on_device(): lax.all_to_all(send, 'tensor', 0, 0, tiled=True)]
    all_to_all x0 -> x1, blocking collectives: none -> 75.8 us  [gathered(): return lax.all_to_all(copies, axis, 0, 0, tiled=True)]
    reduce_scatter x1 -> x0, waiting for transfers between devices: 74.3 us -> none  [on_device(): lax.psum_scatter(lax.dot_general(dhidden, weight_all, across, preferred_e...]
    psum x1 -> x0, blocking collectives: 49.1 us -> none  [on_device(): gain_grad = lax.psum(gain_part, 'tensor')]
    ppermute x5 -> x2, waiting for transfers between devices: 29 us -> 0.01 us  [the longest x1 0.01 us: on_device(): lax.ppermute(dside, 'section', [(s, sections - 1 - s) for s in range(midd...]
    ppermute x2, waiting for transfers between devices: 0.01 us -> 18.2 us  [shifted(): return lax.ppermute(block, axis, route)]
    all_to_all x0 -> x2, starting transfers between devices: none -> 12.4 us  [the longest x1 6.59 us: gathered(): return lax.all_to_all(copies, axis, 0, 0, tiled=True)]
  transfers between devices with their start and end apart: 14 -> 8, of which waited for: 10 -> 3; matrix products, arithmetic and copies ran while one was open for 4% -> 7% of each run, Pallas kernels for 0% -> 0%
where the time goes in v1:
time: 345 us; the launch traced here: 340 us
  waiting for transfers between devices  166 us (48%)
  blocking collectives  75.8 us (22%)
  starting transfers between devices  37.2 us (11%)
  matrix products  26 us (8%)
  other arithmetic  24.8 us (7%)
  local copies, waits for them, and re-layouts  9.67 us (3%)
    all_to_all x1, waiting for transfers between devices, on_device(): lax.all_to_all(send, 'tensor', 0, 0, tiled=True)  78.4 us
    all_to_all x1, blocking collectives, gathered(): return lax.all_to_all(copies, axis, 0, 0, tiled=True)  75.8 us
    all_to_all x1, waiting for transfers between devices, gathered(): return lax.all_to_all(copies, axis, 0, 0, tiled=True)  69 us
    ppermute x2, waiting for transfers between devices, shifted(): return lax.ppermute(block, axis, route)  18.2 us
    dot_general x1, matrix products, on_device(): lax.dot_general(bfused_all, dhidden, contract, preferred_element_type=jnp...  8.55 us
    ppermute x1, starting transfers between devices, on_device(): lax.ppermute(out_rows, 'section', [(s, sections - 1 - s) for s in range(m...  8.53 us
    dot_general x1, matrix products, on_device(): jnp.dot(bfused_all, weight_all, preferred_element_type=jnp.float32)  7.13 us
  transfers between devices with their start and end apart: 8, of which 3 were waited for; matrix products, arithmetic and copies ran while one was open for 7% of the time, Pallas kernels for 0%

profile of v1, /device:TPU:32, one launch (start us, length us, event | category | flops | bytes accessed | tf_op | source)
XLA Modules:
  0.0 339.9 jit_solution(16406312255095544041)
XLA Ops:
  1.8 3.4 broadcast_in_dim.18
  5.2 6.6 %all-to-all-start.3 = ((bf16[8,64,6144]{2,1,0:T(8,128)(2,1)}), bf16[8,64,6144]{2,1,0:T(8,128)(2,1)}, u32[]{:S(2)}, u32[]{:S(2)}) async-start(bf16[8,64,6144]{2,1,0:T(8,128)(2,1)} %broadcast_in_dim.18), calls=%async_computation.3 | async-start | bytes 12582912 | tf_op jit(solution)/shard_map/all_to_all | solution.py:40
  12.6 69.0 %all-to-all-done.3 = bf16[8,64,6144]{2,1,0:T(8,128)(2,1)} async-done(((bf16[8,64,6144]{2,1,0:T(8,128)(2,1)}), bf16[8,64,6144]{2,1,0:T(8,128)(2,1)}, u32[]{:S(2)}, u32[]{:S(2)}) %all-to-all-start.3) | async-done | bytes 6291488 | tf_op jit(solution)/shard_map/all_to_all | solution.py:40
  81.6 4.6 %all-to-all-start.2 = ((bf16[64,8,384]{2,0,1:T(8,128)(2,1)}), bf16[64,8,384]{2,0,1:T(8,128)(2,1)}, u32[]{:S(2)}, u32[]{:S(2)}) async-start(bf16[64,8,384]{2,0,1:T(8,128)(2,1)} %copy.13), calls=%async_computation.2 | async-start | bytes 786432 | tf_op jit(solution)/shard_map/all_to_all | solution.py:68
  86.2 2.6 fusion.1
  88.7 2.1 slice.38
  90.9 5.8 %fusion.3 = bf16[512,3072]{1,0:T(8,128)(2,1)} fusion(f32[3072]{0:T(1024)S(1)} %bitcast.65, f32[512]{0:T(512)S(1)} %add_rsqrt_fusion, bf16[512,6144]{1,0:T(8,128)(2,1)} %bitcast.13), kind=kLoop, calls=%fused_computation.10 | loop fusion | flops 6291456 | bytes 6305792 | tf_op jit(solution)/shard_map/convert_element_type | solution.py:33
  96.7 7.1 %fusion.22 = bf16[512,384]{1,0:T(8,128)(2,1)S(1)} fusion(bf16[1,6144,384]{2,1,0:T(8,128)(2,1)} %param.10, bf16[512,3072]{1,0:T(8,128)(2,1)S(1)} %slice.38, bf16[512,3072]{1,0:T(8,128)(2,1)} %fusion.3, bf16[64,8,384]{2,0,1:T(8,128)(2,1)} %all-to-all-done.2), kind=kOutput, calls=%fused_computation.39 | convolution fusion | flops 2432434176 | bytes 11796480 | tf_op jit(solution)/shard_map/dot_general | solution.py:67
  104.6 6.0 %convolution_convert_fusion = bf16[512,6144]{1,0:T(8,128)(2,1)S(1)} fusion(bf16[512,384]{1,0:T(8,128)(2,1)S(1)} %fusion.22, bf16[1,6144,384]{2,1,0:T(8,128)(2,1)} %param.10), kind=kOutput, calls=%fused_computation.4 | convolution fusion | flops 2419064832 | bytes 11403264 | tf_op jit(solution)/shard_map/dot_general | solution.py:75
  110.6 3.2 fusion.5
  114.0 3.5 %pad_maximum_fusion = bf16[8,65,6144]{2,1,0:T(8,128)(2,1)} fusion(bf16[8,1,6144]{2,1,0:T(2,128)(2,1)S(1)} %broadcast_in_dim.19, bf16[8,64,6144]{2,1,0:T(8,128)(2,1)S(1)} %bitcast.54), kind=kLoop, calls=%fused_computation.7 | loop fusion | flops 12779520 | bytes 12779520 | tf_op jit(solution)/shard_map/concatenate | solution.py:82
  117.5 5.8 %all-to-all-start.4 = ((bf16[8,65,6144]{2,1,0:T(8,128)(2,1)}), bf16[8,65,6144]{2,1,0:T(8,128)(2,1)}, u32[]{:S(2)}, u32[]{:S(2)}) async-start(bf16[8,65,6144]{2,1,0:T(8,128)(2,1)} %pad_maximum_fusion), calls=%async_computation.4 | async-start | bytes 14155776 | tf_op jit(solution)/shard_map/all_to_all | solution.py:85
  123.6 78.4 %all-to-all-done.4 = bf16[8,65,6144]{2,1,0:T(8,128)(2,1)} async-done(((bf16[8,65,6144]{2,1,0:T(8,128)(2,1)}), bf16[8,65,6144]{2,1,0:T(8,128)(2,1)}, u32[]{:S(2)}, u32[]{:S(2)}) %all-to-all-start.4) | async-done | bytes 6389792 | tf_op jit(solution)/shard_map/all_to_all | solution.py:85
  201.9 4.0 %convert_reduce_fusion = f32[64,6144]{1,0:T(8,128)S(1)} fusion(bf16[8,65,6144]{2,1,0:T(8,128)(2,1)} %all-to-all-done.4), kind=kLoop, calls=%fused_computation | loop fusion | flops 5898240 | bytes 7864320 | tf_op jit(solution)/shard_map/reduce_sum | solution.py:86
  206.2 1.2 fusion.29
  208.3 75.8 %all_to_all.50 = bf16[8,64,6144]{2,1,0:T(8,128)(2,1)S(1)} all-to-all(bf16[8,64,6144]{2,1,0:T(8,128)(2,1)S(1)} %broadcast_in_dim.16), channel_id=1, replica_groups=mesh['section'=32,'tensor'=8] {'tensor'}, dimensions={0} | all-to-all | bytes 12582912 | tf_op jit(solution)/shard_map/all_to_all | solution.py:40
  284.1 4.3 %fusion.15 = bf16[512,384]{1,0:T(8,128)(2,1)} fusion(bf16[512,6144]{1,0:T(8,128)(2,1)S(1)} %bitcast.55, bf16[1,6144,384]{2,1,0:T(8,128)(2,1)S(1)} %bitcast.70), kind=kOutput, calls=%fused_computation.32 | convolution fusion | flops 2417688576 | bytes 11403264 | tf_op jit(solution)/shard_map/dot_general | solution.py:54
  288.4 4.8 %all-to-all-start.1 = ((bf16[8,64,384]{2,1,0:T(8,128)(2,1)}), bf16[8,64,384]{2,1,0:T(8,128)(2,1)S(1)}, u32[]{:S(2)}, u32[]{:S(2)}) async-start(bf16[8,64,384]{2,1,0:T(8,128)(2,1)} %bitcast.6), calls=%async_computation.1 | async-start | bytes 786432 | tf_op jit(solution)/shard_map/all_to_all | solution.py:55
  293.2 8.6 %fusion = bf16[1,6144,384]{2,1,0:T(8,128)(2,1)} fusion(bf16[512,384]{1,0:T(8,128)(2,1)S(1)} %copy-done.8, bf16[512,3072]{1,0:T(8,128)(2,1)} %copy-done.2, bf16[512,3072]{1,0:T(8,128)(2,1)} %fusion.3), kind=kOutput, calls=%fused_computation.6 | convolution fusion | flops 2430861312 | bytes 11403264 | tf_op jit(solution)/shard_map/dot_general | solution.py:71
  301.8 5.5 %collective-permute-start.3 = (bf16[64,3072]{1,0:T(8,128)(2,1)S(1)}, bf16[64,3072]{1,0:T(8,128)(2,1)S(1)}, u32[]{:S(2)}, u32[]{:S(2)}) collective-permute-start(bf16[64,3072]{1,0:T(8,128)(2,1)S(1)} %copy-done.5), channel_id=1, source_target_pairs={{8,0},{16,8},{24,16},{32,24},{40,32},{48,40},{56,48},{64,56},{72,6... | collective-permute-start | bytes 1179656 | tf_op jit(solution)/shard_map/ppermute | solution.py:14
  307.3 1.3 collective-permute-start.2
  308.8 8.5 %collective-permute-start.1 = (bf16[64,3072]{1,0:T(8,128)(2,1)S(1)}, bf16[64,3072]{1,0:T(8,128)(2,1)S(1)}, u32[]{:S(2)}, u32[]{:S(2)}) collective-permute-start(bf16[64,3072]{1,0:T(8,128)(2,1)S(1)} %fusion.34), channel_id=1, source_target_pairs={{0,248},{8,240},{16,232},{24,224},{32,216},{40,208},{48,200},{56,1... | collective-permute-start | bytes 1179656 | tf_op jit(solution)/shard_map/ppermute | solution.py:60
  317.4 1.2 slice_convert_fusion.1
  319.4 18.2 %collective-permute-done = bf16[64,3072]{1,0:T(8,128)(2,1)S(1)} collective-permute-done((bf16[64,3072]{1,0:T(8,128)(2,1)S(1)}, bf16[64,3072]{1,0:T(8,128)(2,1)S(1)}, u32[]{:S(2)}, u32[]{:S(2)}) %collective-permute-start) | collective-permute-done | bytes 393248 | tf_op jit(solution)/shard_map/ppermute | solution.py:14
  (51 shorter events, 7.5 us)
Async XLA Ops:
  5.2 6.6 %copy-start.3 = (bf16[1,64,3072]{2,1,0:T(8,128)(2,1)S(1)}, bf16[1,64,3072]{2,1,0:T(8,128)(2,1)}, u32[]{:S(2)}) copy-start(bf16[1,64,3072]{2,1,0:T(8,128)(2,1)} %param.13) | copy-start | bytes 1179652
  5.2 76.4 %all-to-all-start.3 = ((bf16[8,64,6144]{2,1,0:T(8,128)(2,1)}), bf16[8,64,6144]{2,1,0:T(8,128)(2,1)}, u32[]{:S(2)}, u32[]{:S(2)}) async-start(bf16[8,64,6144]{2,1,0:T(8,128)(2,1)} %broadcast_in_dim.18), calls=%async_computation.3 | async-start | bytes 12582912 | tf_op jit(solution)/shard_map/all_to_all | solution.py:40
  11.8 79.1 %copy-start.6 = (f32[1,3072]{1,0:T(1,128)S(1)}, f32[1,3072]{1,0:T(1,128)}, u32[]{:S(2)}) copy-start(f32[1,3072]{1,0:T(1,128)} %param.9) | copy-start | bytes 36868
  81.6 15.1 %all-to-all-start.2 = ((bf16[64,8,384]{2,0,1:T(8,128)(2,1)}), bf16[64,8,384]{2,0,1:T(8,128)(2,1)}, u32[]{:S(2)}, u32[]{:S(2)}) async-start(bf16[64,8,384]{2,0,1:T(8,128)(2,1)} %copy.13), calls=%async_computation.2 | async-start | bytes 786432 | tf_op jit(solution)/shard_map/all_to_all | solution.py:68
  90.8 13.0 %copy-start.2 = (bf16[512,3072]{1,0:T(8,128)(2,1)}, bf16[512,3072]{1,0:T(8,128)(2,1)S(1)}, u32[]{:S(2)}) copy-start(bf16[512,3072]{1,0:T(8,128)(2,1)S(1)} %slice.38) | copy-start | bytes 9437188
  103.8 0.7 copy-start.7
  117.5 5.9 %copy-start = (bf16[1,64,3072]{2,1,0:T(8,128)(2,1)S(1)}, bf16[1,64,3072]{2,1,0:T(8,128)(2,1)}, u32[]{:S(2)}) copy-start(bf16[1,64,3072]{2,1,0:T(8,128)(2,1)} %param.7) | copy-start | bytes 1179652
  117.5 84.4 %all-to-all-start.4 = ((bf16[8,65,6144]{2,1,0:T(8,128)(2,1)}), bf16[8,65,6144]{2,1,0:T(8,128)(2,1)}, u32[]{:S(2)}, u32[]{:S(2)}) async-start(bf16[8,65,6144]{2,1,0:T(8,128)(2,1)} %pad_maximum_fusion), calls=%async_computation.4 | async-start | bytes 14155776 | tf_op jit(solution)/shard_map/all_to_all | solution.py:85
  123.4 82.6 %copy-start.1 = (bf16[1,64,3072]{2,1,0:T(8,128)(2,1)S(1)}, bf16[1,64,3072]{2,1,0:T(8,128)(2,1)}, u32[]{:S(2)}) copy-start(bf16[1,64,3072]{2,1,0:T(8,128)(2,1)} %param.11) | copy-start | bytes 1179652
  123.4 84.0 %copy-start.4 = (bf16[1,64,3072]{2,1,0:T(8,128)(2,1)S(1)}, bf16[1,64,3072]{2,1,0:T(8,128)(2,1)}, u32[]{:S(2)}) copy-start(bf16[1,64,3072]{2,1,0:T(8,128)(2,1)} %param.8) | copy-start | bytes 1179652
  207.5 76.6 %slice-start = ((s8[4718592]{0:T(1024)(128)(4,1)}), s8[524288]{0:T(1024)(128)(4,1)S(1)}, s32[]{:S(2)}) async-start(s8[4718592]{0:T(1024)(128)(4,1)} %bitcast.69), calls=%async_computation.5 | async-start | bytes 1048576
  208.3 75.8 %slice-start.1 = ((s8[4718592]{0:T(1024)(128)(4,1)}), s8[4194304]{0:T(1024)(128)(4,1)S(1)}, s32[]{:S(2)}) async-start(s8[4718592]{0:T(1024)(128)(4,1)} %bitcast.69), calls=%async_computation.6 | async-start | bytes 8388608
  284.1 9.1 %copy-start.8 = (bf16[512,384]{1,0:T(8,128)(2,1)S(1)}, bf16[512,384]{1,0:T(8,128)(2,1)}, u32[]{:S(2)}) copy-start(bf16[512,384]{1,0:T(8,128)(2,1)} %copy-done.7) | copy-start | bytes 1179652
  288.4 20.2 %all-to-all-start.1 = ((bf16[8,64,384]{2,1,0:T(8,128)(2,1)}), bf16[8,64,384]{2,1,0:T(8,128)(2,1)S(1)}, u32[]{:S(2)}, u32[]{:S(2)}) async-start(bf16[8,64,384]{2,1,0:T(8,128)(2,1)} %bitcast.6), calls=%async_computation.1 | async-start | bytes 786432 | tf_op jit(solution)/shard_map/all_to_all | solution.py:55
  293.2 8.6 %copy-start.5 = (bf16[64,3072]{1,0:T(8,128)(2,1)S(1)}, bf16[64,3072]{1,0:T(8,128)(2,1)}, u32[]{:S(2)}) copy-start(bf16[64,3072]{1,0:T(8,128)(2,1)} %get-tuple-element.9) | copy-start | bytes 1179652
  301.8 17.6 %collective-permute-start.3 = (bf16[64,3072]{1,0:T(8,128)(2,1)S(1)}, bf16[64,3072]{1,0:T(8,128)(2,1)S(1)}, u32[]{:S(2)}, u32[]{:S(2)}) collective-permute-start(bf16[64,3072]{1,0:T(8,128)(2,1)S(1)} %copy-done.5), channel_id=1, source_target_pairs={{8,0},{16,8},{24,16},{32,24},{40,32},{48,40},{56,48},{64,56},{72,6... | collective-permute-start | bytes 1179656 | tf_op jit(solution)/shard_map/ppermute | solution.py:14
  307.3 30.3 %collective-permute-start.2 = (bf16[64,3072]{1,0:T(8,128)(2,1)S(1)}, bf16[64,3072]{1,0:T(8,128)(2,1)S(1)}, u32[]{:S(2)}, u32[]{:S(2)}) collective-permute-start(bf16[64,3072]{1,0:T(8,128)(2,1)S(1)} %slice.62), channel_id=1, source_target_pairs={{128,120},{136,112},{144,104},{152,96},{160,88},{168,80},{176,72},... | collective-permute-start | bytes 1179656 | tf_op jit(solution)/shard_map/ppermute | solution.py:98
  308.8 28.8 %collective-permute-start.1 = (bf16[64,3072]{1,0:T(8,128)(2,1)S(1)}, bf16[64,3072]{1,0:T(8,128)(2,1)S(1)}, u32[]{:S(2)}, u32[]{:S(2)}) collective-permute-start(bf16[64,3072]{1,0:T(8,128)(2,1)S(1)} %fusion.34), channel_id=1, source_target_pairs={{0,248},{8,240},{16,232},{24,224},{32,216},{40,208},{48,200},{56,1... | collective-permute-start | bytes 1179656 | tf_op jit(solution)/shard_map/ppermute | solution.py:60
  317.3 20.2 %collective-permute-start = (bf16[64,3072]{1,0:T(8,128)(2,1)S(1)}, bf16[64,3072]{1,0:T(8,128)(2,1)S(1)}, u32[]{:S(2)}, u32[]{:S(2)}) collective-permute-start(bf16[64,3072]{1,0:T(8,128)(2,1)S(1)} %fusion.34), channel_id=1, source_target_pairs={{248,0},{0,8},{8,16},{16,24},{24,32},{32,40},{40,48},{48,56},{56,6... | collective-permute-start | bytes 1179656 | tf_op jit(solution)/shard_map/ppermute | solution.py:14

commit v2 on v1

--- a/solution.py
+++ b/solution.py
@@ -49,19 +49,11 @@
     weight_all = weights[0]
     rows, width = acts[0].shape
 
+    raw_all = gathered(jnp.concatenate([back_acts[0], back_sides[0]], axis=1), "tensor")
     xfloat, rinv, normed = normalize(acts[0], gain)
-    joined_all = gathered(jnp.concatenate([normed, sides[0]], axis=1), "tensor")
-    hidden = jnp.dot(joined_all, weight_all, preferred_element_type=jnp.float32)
-    update = lax.all_to_all(
-        gelu_value(hidden).astype(jnp.bfloat16), "tensor", split_axis=0, concat_axis=1, tiled=True
-    ).astype(jnp.float32)
-    out_rows = (xfloat + update).astype(jnp.bfloat16)
-    received = shifted(out_rows, "section", 1)
-    ahead = lax.ppermute(
-        out_rows, "section", [(s, sections - 1 - s) for s in range(middle)]
-    )
-
-    raw_all = gathered(jnp.concatenate([back_acts[0], back_sides[0]], axis=1), "tensor")
+    joined = jnp.concatenate([normed, sides[0]], axis=1)
+    raw_all, joined = lax.optimization_barrier((raw_all, joined))
+    joined_all = gathered(joined, "tensor")
     bfloat_all, brinv_all, bnormed_all = normalize(raw_all[:, :width], gain)
     bfused_all = jnp.concatenate([bnormed_all, raw_all[:, width:]], axis=1)
     bhidden = jnp.dot(bfused_all, weight_all, preferred_element_type=jnp.float32)
@@ -83,6 +75,17 @@
         [term.reshape(count, rows, 2 * width), jnp.broadcast_to(extra, (count, 1, 2 * width))], axis=1
     ).reshape(count * (rows + 1), 2 * width)
     got = lax.all_to_all(send, "tensor", 0, 0, tiled=True).reshape(count, rows + 1, 2 * width)
+
+    hidden = jnp.dot(joined_all, weight_all, preferred_element_type=jnp.float32)
+    update = lax.all_to_all(
+        gelu_value(hidden).astype(jnp.bfloat16), "tensor", split_axis=0, concat_axis=1, tiled=True
+    ).astype(jnp.float32)
+    out_rows = (xfloat + update).astype(jnp.bfloat16)
+    received = shifted(out_rows, "section", 1)
+    ahead = lax.ppermute(
+        out_rows, "section", [(s, sections - 1 - s) for s in range(middle)]
+    )
+
     dfused = jnp.sum(got[:, :rows].astype(jnp.float32), axis=0)
     shares = got[:, rows].astype(jnp.float32)
     gain_grad = jnp.sum(shares[:, :width] + shares[:, width:], axis=0)

time: 345 us -> 305 us (0.88)
  blocking collectives: 75.8 us -> 0 us
  waiting for transfers between devices: 166 us -> 200 us
  starting transfers between devices: 37.2 us -> 42.4 us
  local copies, waits for them, and re-layouts: 9.67 us -> 13.4 us
    all_to_all x1 -> x0, blocking collectives: 75.8 us -> none  [gathered(): return lax.all_to_all(copies, axis, 0, 0, tiled=True)]
    all_to_all x1 -> x2, waiting for transfers between devices: 69 us -> 114 us  [gathered(): return lax.all_to_all(copies, axis, 0, 0, tiled=True)]
    all_to_all x1, waiting for transfers between devices: 78.4 us -> 63.1 us  [on_device(): lax.all_to_all(send, 'tensor', 0, 0, tiled=True)]
    all_to_all x1, waiting for transfers between devices: 0.01 us -> 7.34 us  [on_device(): lax.all_to_all(back_grads[0], 'tensor', split_axis=1, concat_axis=0, tile...]
    all_to_all x1 -> x2, starting transfers between devices: 6.59 us -> 12.4 us  [gathered(): return lax.all_to_all(copies, axis, 0, 0, tiled=True)]
    dot_general x1, matrix products: 4.27 us -> 8.43 us  [on_device(): hidden = jnp.dot(joined_all, weight_all, preferred_element_type=jnp.float32)]
  transfers between devices with their start and end apart: 8 -> 9, of which waited for: 3 -> 6; matrix products, arithmetic and copies ran while one was open for 7% -> 15% of each run, Pallas kernels for 0% -> 0%
where the time goes in v2:
time: 305 us; the launch traced here: 302 us
  waiting for transfers between devices  200 us (66%)
  starting transfers between devices  42.4 us (14%)
  matrix products  23.6 us (8%)
  other arithmetic  21.5 us (7%)
  local copies, waits for them, and re-layouts  13.4 us (4%)
    all_to_all x2, waiting for transfers between devices, gathered(): return lax.all_to_all(copies, axis, 0, 0, tiled=True)  114 us
    all_to_all x1, waiting for transfers between devices, on_device(): lax.all_to_all(send, 'tensor', 0, 0, tiled=True)  63.1 us
    ppermute x2, waiting for transfers between devices, shifted(): return lax.ppermute(block, axis, route)  15.6 us
    all_to_all x2, starting transfers between devices, gathered(): return lax.all_to_all(copies, axis, 0, 0, tiled=True)  12.4 us
    dot_general x1, matrix products, on_device(): hidden = jnp.dot(joined_all, weight_all, preferred_element_type=jnp.float32)  8.43 us
    ppermute x1, starting transfers between devices, on_device(): lax.ppermute(out_rows, 'section', [(s, sections - 1 - s) for s in range(m...  7.87 us
    dot_general x1, matrix products, on_device(): lax.dot_general(bfused_all, dhidden, contract, preferred_element_type=jnp...  7.61 us
    all_to_all x1, waiting for transfers between devices, on_device(): lax.all_to_all(back_grads[0], 'tensor', split_axis=1, concat_axis=0, tile...  7.34 us
  transfers between devices with their start and end apart: 9, of which 6 were waited for; matrix products, arithmetic and copies ran while one was open for 15% of the time, Pallas kernels for 0%

profile of v2, /device:TPU:32, one launch (start us, length us, event | category | flops | bytes accessed | tf_op | source)
XLA Modules:
  0.0 301.6 jit_solution(8601807383127399153)
XLA Ops:
  1.8 3.4 %broadcast_in_dim.16 = bf16[8,64,6144]{2,1,0:T(8,128)(2,1)} broadcast(bf16[64,6144]{1,0:T(8,128)(2,1)S(1)} %pad_maximum_fusion.4), dimensions={1,2} | broadcast | bytes 7077888 | tf_op jit(solution)/shard_map/broadcast_in_dim | solution.py:38
  5.2 6.6 %all-to-all-start = ((bf16[8,64,6144]{2,1,0:T(8,128)(2,1)}), bf16[8,64,6144]{2,1,0:T(8,128)(2,1)}, u32[]{:S(2)}, u32[]{:S(2)}) async-start(bf16[8,64,6144]{2,1,0:T(8,128)(2,1)} %broadcast_in_dim.16), calls=%async_computation | async-start | bytes 12582912 | tf_op jit(solution)/shard_map/all_to_all | solution.py:40
  13.0 68.6 %all-to-all-done = bf16[8,64,6144]{2,1,0:T(8,128)(2,1)} async-done(((bf16[8,64,6144]{2,1,0:T(8,128)(2,1)}), bf16[8,64,6144]{2,1,0:T(8,128)(2,1)}, u32[]{:S(2)}, u32[]{:S(2)}) %all-to-all-start) | async-done | bytes 6291488 | tf_op jit(solution)/shard_map/all_to_all | solution.py:40
  81.7 4.2 %all-to-all-start.3 = ((bf16[64,8,384]{2,0,1:T(8,128)(2,1)}), bf16[64,8,384]{2,0,1:T(8,128)(2,1)S(1)}, u32[]{:S(2)}, u32[]{:S(2)}) async-start(bf16[64,8,384]{2,0,1:T(8,128)(2,1)} %copy.13), calls=%async_computation.3 | async-start | bytes 786432 | tf_op jit(solution)/shard_map/all_to_all | solution.py:60
  85.9 7.3 %all-to-all-done.3 = bf16[64,8,384]{2,0,1:T(8,128)(2,1)S(1)} async-done(((bf16[64,8,384]{2,0,1:T(8,128)(2,1)}), bf16[64,8,384]{2,0,1:T(8,128)(2,1)S(1)}, u32[]{:S(2)}, u32[]{:S(2)}) %all-to-all-start.3) | async-done | bytes 393248 | tf_op jit(solution)/shard_map/all_to_all | solution.py:60
  93.3 3.4 %broadcast_in_dim.17 = bf16[8,64,6144]{2,1,0:T(8,128)(2,1)} broadcast(bf16[64,6144]{1,0:T(8,128)(2,1)S(1)} %pad_maximum_fusion.5), dimensions={1,2} | broadcast | bytes 7077888 | tf_op jit(solution)/shard_map/broadcast_in_dim | solution.py:38
  96.7 5.9 %all-to-all-start.1 = ((bf16[8,64,6144]{2,1,0:T(8,128)(2,1)}), bf16[8,64,6144]{2,1,0:T(8,128)(2,1)}, u32[]{:S(2)}, u32[]{:S(2)}) async-start(bf16[8,64,6144]{2,1,0:T(8,128)(2,1)} %broadcast_in_dim.17), calls=%async_computation.1 | async-start | bytes 12582912 | tf_op jit(solution)/shard_map/all_to_all | solution.py:40
  102.6 2.2 slice.29
  104.8 2.7 fusion.1
  107.5 3.1 %fusion.3 = bf16[512,3072]{1,0:T(8,128)(2,1)S(1)} fusion(f32[3072]{0:T(1024)S(1)} %bitcast.65, f32[512]{0:T(512)S(1)} %add_rsqrt_fusion, bf16[512,6144]{1,0:T(8,128)(2,1)} %bitcast.3), kind=kLoop, calls=%fused_computation.10 | loop fusion | flops 6291456 | bytes 6305792 | tf_op jit(solution)/shard_map/convert_element_type | solution.py:33
  112.3 3.8 %fusion.22 = bf16[512,384]{1,0:T(8,128)(2,1)S(1)} fusion(bf16[1,6144,384]{2,1,0:T(8,128)(2,1)S(1)} %bitcast.70, bf16[512,3072]{1,0:T(8,128)(2,1)S(1)} %slice.29, bf16[512,3072]{1,0:T(8,128)(2,1)S(1)} %fusion.3, bf16[64,8,384]{2,0,1:T(8,128)(2,1)S(1)} %copy-done.6), kind=kOutput, calls=%fused_computation.39 | convolution fusion | flops 2432434176 | bytes 11796480 | tf_op jit(solution)/shard_map/dot_general | solution.py:59
  116.1 3.7 %convolution_convert_fusion = bf16[512,6144]{1,0:T(8,128)(2,1)S(1)} fusion(bf16[512,384]{1,0:T(8,128)(2,1)S(1)} %fusion.22, bf16[1,6144,384]{2,1,0:T(8,128)(2,1)S(1)} %bitcast.70), kind=kOutput, calls=%fused_computation.4 | convolution fusion | flops 2419064832 | bytes 11403264 | tf_op jit(solution)/shard_map/dot_general | solution.py:67
  119.9 3.2 %fusion.5 = f32[3072]{0:T(1024)S(1)} fusion(bf16[512,6144]{1,0:T(8,128)(2,1)S(1)} %convolution_convert_fusion, f32[512]{0:T(512)S(1)} %add_rsqrt_fusion, bf16[512,6144]{1,0:T(8,128)(2,1)} %bitcast.3), kind=kLoop, calls=%fused_computation.12 | loop fusion | flops 7861248 | bytes 6305792 | tf_op jit(solution)/shard_map/reduce_sum | solution.py:70
  123.2 3.5 %pad_maximum_fusion = bf16[8,65,6144]{2,1,0:T(8,128)(2,1)} fusion(bf16[8,1,6144]{2,1,0:T(2,128)(2,1)S(1)} %broadcast_in_dim.19, bf16[8,64,6144]{2,1,0:T(8,128)(2,1)S(1)} %bitcast.54), kind=kLoop, calls=%fused_computation.7 | loop fusion | flops 12779520 | bytes 12779520 | tf_op jit(solution)/shard_map/concatenate | solution.py:74
  126.8 45.0 %all-to-all-done.1 = bf16[8,64,6144]{2,1,0:T(8,128)(2,1)} async-done(((bf16[8,64,6144]{2,1,0:T(8,128)(2,1)}), bf16[8,64,6144]{2,1,0:T(8,128)(2,1)}, u32[]{:S(2)}, u32[]{:S(2)}) %all-to-all-start.1) | async-done | bytes 6291488 | tf_op jit(solution)/shard_map/all_to_all | solution.py:40
  171.7 5.3 %all-to-all-start.4 = ((bf16[8,65,6144]{2,1,0:T(8,128)(2,1)}), bf16[8,65,6144]{2,1,0:T(8,128)(2,1)}, u32[]{:S(2)}, u32[]{:S(2)}) async-start(bf16[8,65,6144]{2,1,0:T(8,128)(2,1)} %pad_maximum_fusion), calls=%async_computation.4 | async-start | bytes 14155776 | tf_op jit(solution)/shard_map/all_to_all | solution.py:77
  177.0 7.6 %fusion = bf16[1,6144,384]{2,1,0:T(8,128)(2,1)} fusion(bf16[512,384]{1,0:T(8,128)(2,1)} %copy-done.9, bf16[512,3072]{1,0:T(8,128)(2,1)S(1)} %slice.29, bf16[512,3072]{1,0:T(8,128)(2,1)} %copy-done.2), kind=kOutput, calls=%fused_computation.6 | convolution fusion | flops 2430861312 | bytes 11403264 | tf_op jit(solution)/shard_map/dot_general | solution.py:63
  184.6 8.4 %fusion.15 = bf16[512,384]{1,0:T(8,128)(2,1)} fusion(bf16[512,6144]{1,0:T(8,128)(2,1)} %bitcast.7, bf16[1,6144,384]{2,1,0:T(8,128)(2,1)} %param.10), kind=kOutput, calls=%fused_computation.32 | convolution fusion | flops 2417688576 | bytes 11403264 | tf_op jit(solution)/shard_map/dot_general | solution.py:79
  193.0 63.1 %all-to-all-done.4 = bf16[8,65,6144]{2,1,0:T(8,128)(2,1)} async-done(((bf16[8,65,6144]{2,1,0:T(8,128)(2,1)}), bf16[8,65,6144]{2,1,0:T(8,128)(2,1)}, u32[]{:S(2)}, u32[]{:S(2)}) %all-to-all-start.4) | async-done | bytes 6389792 | tf_op jit(solution)/shard_map/all_to_all | solution.py:77
  256.1 4.2 %all-to-all-start.2 = ((bf16[8,64,384]{2,1,0:T(8,128)(2,1)}), bf16[8,64,384]{2,1,0:T(8,128)(2,1)S(1)}, u32[]{:S(2)}, u32[]{:S(2)}) async-start(bf16[8,64,384]{2,1,0:T(8,128)(2,1)} %bitcast.9), calls=%async_computation.2 | async-start | bytes 786432 | tf_op jit(solution)/shard_map/all_to_all | solution.py:80
  260.3 4.1 %convert_reduce_fusion = f32[64,6144]{1,0:T(8,128)S(1)} fusion(bf16[8,65,6144]{2,1,0:T(8,128)(2,1)} %all-to-all-done.4), kind=kLoop, calls=%fused_computation | loop fusion | flops 5898240 | bytes 7864320 | tf_op jit(solution)/shard_map/reduce_sum | solution.py:89
  266.4 7.2 %collective-permute-start.3 = (bf16[64,3072]{1,0:T(8,128)(2,1)S(1)}, bf16[64,3072]{1,0:T(8,128)(2,1)S(1)}, u32[]{:S(2)}, u32[]{:S(2)}) collective-permute-start(bf16[64,3072]{1,0:T(8,128)(2,1)S(1)} %fusion.29), channel_id=1, source_target_pairs={{8,0},{16,8},{24,16},{32,24},{40,32},{48,40},{56,48},{64,56},{72,6... | collective-permute-start | bytes 1179656 | tf_op jit(solution)/shard_map/ppermute | solution.py:14
  273.8 7.9 %collective-permute-start.1 = (bf16[64,3072]{1,0:T(8,128)(2,1)S(1)}, bf16[64,3072]{1,0:T(8,128)(2,1)S(1)}, u32[]{:S(2)}, u32[]{:S(2)}) collective-permute-start(bf16[64,3072]{1,0:T(8,128)(2,1)S(1)} %fusion.34), channel_id=1, source_target_pairs={{0,248},{8,240},{16,232},{24,224},{32,216},{40,208},{48,200},{56,1... | collective-permute-start | bytes 1179656 | tf_op jit(solution)/shard_map/ppermute | solution.py:85
  284.1 15.1 %collective-permute-done = bf16[64,3072]{1,0:T(8,128)(2,1)S(1)} collective-permute-done((bf16[64,3072]{1,0:T(8,128)(2,1)S(1)}, bf16[64,3072]{1,0:T(8,128)(2,1)S(1)}, u32[]{:S(2)}, u32[]{:S(2)}) %collective-permute-start) | collective-permute-done | bytes 393248 | tf_op jit(solution)/shard_map/ppermute | solution.py:14
  (55 shorter events, 11.2 us)
Async XLA Ops:
  5.2 6.6 %copy-start.3 = (bf16[1,64,3072]{2,1,0:T(8,128)(2,1)S(1)}, bf16[1,64,3072]{2,1,0:T(8,128)(2,1)}, u32[]{:S(2)}) copy-start(bf16[1,64,3072]{2,1,0:T(8,128)(2,1)} %param.13) | copy-start | bytes 1179652
  5.2 7.5 %copy-start.1 = (bf16[1,64,3072]{2,1,0:T(8,128)(2,1)S(1)}, bf16[1,64,3072]{2,1,0:T(8,128)(2,1)}, u32[]{:S(2)}) copy-start(bf16[1,64,3072]{2,1,0:T(8,128)(2,1)} %param.7) | copy-start | bytes 1179652
  5.2 7.7 %copy-start.8 = (f32[1,3072]{1,0:T(1,128)S(1)}, f32[1,3072]{1,0:T(1,128)}, u32[]{:S(2)}) copy-start(f32[1,3072]{1,0:T(1,128)} %param.9) | copy-start | bytes 36868
  5.2 80.6 %copy-start.7 = (bf16[1,64,3072]{2,1,0:T(8,128)(2,1)S(1)}, bf16[1,64,3072]{2,1,0:T(8,128)(2,1)}, u32[]{:S(2)}) copy-start(bf16[1,64,3072]{2,1,0:T(8,128)(2,1)} %param.8) | copy-start | bytes 1179652
  5.2 76.4 %all-to-all-start = ((bf16[8,64,6144]{2,1,0:T(8,128)(2,1)}), bf16[8,64,6144]{2,1,0:T(8,128)(2,1)}, u32[]{:S(2)}, u32[]{:S(2)}) async-start(bf16[8,64,6144]{2,1,0:T(8,128)(2,1)} %broadcast_in_dim.16), calls=%async_computation | async-start | bytes 12582912 | tf_op jit(solution)/shard_map/all_to_all | solution.py:40
  81.7 11.6 %all-to-all-start.3 = ((bf16[64,8,384]{2,0,1:T(8,128)(2,1)}), bf16[64,8,384]{2,0,1:T(8,128)(2,1)S(1)}, u32[]{:S(2)}, u32[]{:S(2)}) async-start(bf16[64,8,384]{2,0,1:T(8,128)(2,1)} %copy.13), calls=%async_computation.3 | async-start | bytes 786432 | tf_op jit(solution)/shard_map/all_to_all | solution.py:60
  93.3 3.5 %copy-start.5 = (bf16[64,8,384]{2,0,1:T(8,128)(2,1)}, bf16[64,8,384]{2,0,1:T(8,128)(2,1)S(1)}, u32[]{:S(2)}) copy-start(bf16[64,8,384]{2,0,1:T(8,128)(2,1)S(1)} %all-to-all-done.3) | copy-start | bytes 1179652
  96.7 75.0 %all-to-all-start.1 = ((bf16[8,64,6144]{2,1,0:T(8,128)(2,1)}), bf16[8,64,6144]{2,1,0:T(8,128)(2,1)}, u32[]{:S(2)}, u32[]{:S(2)}) async-start(bf16[8,64,6144]{2,1,0:T(8,128)(2,1)} %broadcast_in_dim.17), calls=%async_computation.1 | async-start | bytes 12582912 | tf_op jit(solution)/shard_map/all_to_all | solution.py:40
  102.6 9.7 %slice-start = ((s8[4718592]{0:T(1024)(128)(4,1)}), s8[4194304]{0:T(1024)(128)(4,1)S(1)}, s32[]{:S(2)}) async-start(s8[4718592]{0:T(1024)(128)(4,1)} %bitcast.69), calls=%async_computation.5 | async-start | bytes 8388608
  104.8 7.4 %copy-start.6 = (bf16[64,8,384]{2,0,1:T(8,128)(2,1)S(1)}, bf16[64,8,384]{2,0,1:T(8,128)(2,1)}, u32[]{:S(2)}) copy-start(bf16[64,8,384]{2,0,1:T(8,128)(2,1)} %copy-done.5) | copy-start | bytes 1179652
  104.8 7.4 %slice-start.1 = ((s8[4718592]{0:T(1024)(128)(4,1)}), s8[524288]{0:T(1024)(128)(4,1)S(1)}, s32[]{:S(2)}) async-start(s8[4718592]{0:T(1024)(128)(4,1)} %bitcast.69), calls=%async_computation.6 | async-start | bytes 1048576
  110.6 1.7 copy-start.2
  116.1 7.0 %copy-start.9 = (bf16[512,384]{1,0:T(8,128)(2,1)}, bf16[512,384]{1,0:T(8,128)(2,1)S(1)}, u32[]{:S(2)}) copy-start(bf16[512,384]{1,0:T(8,128)(2,1)S(1)} %fusion.22) | copy-start | bytes 1179652
  171.7 84.4 %all-to-all-start.4 = ((bf16[8,65,6144]{2,1,0:T(8,128)(2,1)}), bf16[8,65,6144]{2,1,0:T(8,128)(2,1)}, u32[]{:S(2)}, u32[]{:S(2)}) async-start(bf16[8,65,6144]{2,1,0:T(8,128)(2,1)} %pad_maximum_fusion), calls=%async_computation.4 | async-start | bytes 14155776 | tf_op jit(solution)/shard_map/all_to_all | solution.py:77
  193.0 71.4 %copy-start = (bf16[1,64,3072]{2,1,0:T(8,128)(2,1)S(1)}, bf16[1,64,3072]{2,1,0:T(8,128)(2,1)}, u32[]{:S(2)}) copy-start(bf16[1,64,3072]{2,1,0:T(8,128)(2,1)} %param.11) | copy-start | bytes 1179652
  193.0 73.0 %copy-start.4 = (bf16[1,64,3072]{2,1,0:T(8,128)(2,1)S(1)}, bf16[1,64,3072]{2,1,0:T(8,128)(2,1)}, u32[]{:S(2)}) copy-start(bf16[1,64,3072]{2,1,0:T(8,128)(2,1)} %param.13) | copy-start | bytes 1179652
  256.1 17.4 %all-to-all-start.2 = ((bf16[8,64,384]{2,1,0:T(8,128)(2,1)}), bf16[8,64,384]{2,1,0:T(8,128)(2,1)S(1)}, u32[]{:S(2)}, u32[]{:S(2)}) async-start(bf16[8,64,384]{2,1,0:T(8,128)(2,1)} %bitcast.9), calls=%async_computation.2 | async-start | bytes 786432 | tf_op jit(solution)/shard_map/all_to_all | solution.py:80
  264.7 34.6 %collective-permute-start.2 = (bf16[64,3072]{1,0:T(8,128)(2,1)S(1)}, bf16[64,3072]{1,0:T(8,128)(2,1)S(1)}, u32[]{:S(2)}, u32[]{:S(2)}) collective-permute-start(bf16[64,3072]{1,0:T(8,128)(2,1)S(1)} %slice.60), channel_id=1, source_target_pairs={{128,120},{136,112},{144,104},{152,96},{160,88},{168,80},{176,72},... | collective-permute-start | bytes 1179656 | tf_op jit(solution)/shard_map/ppermute | solution.py:101
  266.4 17.8 %collective-permute-start.3 = (bf16[64,3072]{1,0:T(8,128)(2,1)S(1)}, bf16[64,3072]{1,0:T(8,128)(2,1)S(1)}, u32[]{:S(2)}, u32[]{:S(2)}) collective-permute-start(bf16[64,3072]{1,0:T(8,128)(2,1)S(1)} %fusion.29), channel_id=1, source_target_pairs={{8,0},{16,8},{24,16},{32,24},{40,32},{48,40},{56,48},{64,56},{72,6... | collective-permute-start | bytes 1179656 | tf_op jit(solution)/shard_map/ppermute | solution.py:14
  273.7 25.6 %collective-permute-start = (bf16[64,3072]{1,0:T(8,128)(2,1)S(1)}, bf16[64,3072]{1,0:T(8,128)(2,1)S(1)}, u32[]{:S(2)}, u32[]{:S(2)}) collective-permute-start(bf16[64,3072]{1,0:T(8,128)(2,1)S(1)} %fusion.34), channel_id=1, source_target_pairs={{248,0},{0,8},{8,16},{16,24},{24,32},{32,40},{40,48},{48,56},{56,6... | collective-permute-start | bytes 1179656 | tf_op jit(solution)/shard_map/ppermute | solution.py:14
  273.8 25.5 %collective-permute-start.1 = (bf16[64,3072]{1,0:T(8,128)(2,1)S(1)}, bf16[64,3072]{1,0:T(8,128)(2,1)S(1)}, u32[]{:S(2)}, u32[]{:S(2)}) collective-permute-start(bf16[64,3072]{1,0:T(8,128)(2,1)S(1)} %fusion.34), channel_id=1, source_target_pairs={{0,248},{8,240},{16,232},{24,224},{32,216},{40,208},{48,200},{56,1... | collective-permute-start | bytes 1179656 | tf_op jit(solution)/shard_map/ppermute | solution.py:85

commit v3 on v2

--- a/solution.py
+++ b/solution.py
@@ -33,11 +33,14 @@
     return (xfloat, rinv, (xfloat * rinv * gain).astype(jnp.bfloat16))
 
 
-def gathered(block, axis):
-    count = lax.axis_size(axis)
-    copies = jnp.broadcast_to(block[None], (count,) + block.shape)
-    copies = copies.reshape(count * block.shape[0], block.shape[1])
-    return lax.all_to_all(copies, axis, 0, 0, tiled=True)
+def spread(block, count):
+    return jnp.broadcast_to(block[None], (count,) + block.shape)
+
+
+def exchange(chunks, axis):
+    count, rows, cols = chunks.shape
+    got = lax.all_to_all(chunks.reshape(count * rows, cols), axis, 0, 0, tiled=True)
+    return got.reshape(count, rows, cols)
 
 
 def on_device(acts, sides, gains, weights, back_acts, back_sides, back_grads):
@@ -48,16 +51,23 @@
     gain = gains[0]
     weight_all = weights[0]
     rows, width = acts[0].shape
+    block_cols = weight_all.shape[1]
+    lanes = 128
+    gain_rows = 2 * width // lanes
 
-    raw_all = gathered(jnp.concatenate([back_acts[0], back_sides[0]], axis=1), "tensor")
-    xfloat, rinv, normed = normalize(acts[0], gain)
-    joined = jnp.concatenate([normed, sides[0]], axis=1)
-    raw_all, joined = lax.optimization_barrier((raw_all, joined))
-    joined_all = gathered(joined, "tensor")
+    grad_blocks = back_grads[0].reshape(rows, count, block_cols).transpose(1, 0, 2)
+    raw = jnp.concatenate([back_acts[0], back_sides[0]], axis=1)
+    got_b = exchange(jnp.concatenate([spread(raw, count), grad_blocks], axis=2), "tensor")
+    xfloat, _, normed = normalize(acts[0], gain)
+    chunks_f = spread(jnp.concatenate([normed, sides[0]], axis=1), count)
+    got_b, chunks_f = lax.optimization_barrier((got_b, chunks_f))
+    joined_all = exchange(chunks_f, "tensor").reshape(count * rows, 2 * width)
+
+    raw_all = got_b[:, :, : 2 * width].reshape(count * rows, 2 * width)
+    grad_cols = got_b[:, :, 2 * width :].reshape(count * rows, block_cols)
     bfloat_all, brinv_all, bnormed_all = normalize(raw_all[:, :width], gain)
     bfused_all = jnp.concatenate([bnormed_all, raw_all[:, width:]], axis=1)
     bhidden = jnp.dot(bfused_all, weight_all, preferred_element_type=jnp.float32)
-    grad_cols = lax.all_to_all(back_grads[0], "tensor", split_axis=1, concat_axis=0, tiled=True)
     dhidden = (grad_cols.astype(jnp.float32) * gelu_slope(bhidden)).astype(jnp.bfloat16)
     contract = (((0,), (0,)), ((), ()))
     weight_grads = lax.dot_general(
@@ -70,25 +80,28 @@
     gain_part = jnp.sum(term[:, :width].astype(jnp.float32) * bfloat_all * brinv_all, axis=0)
     part_hi = gain_part.astype(jnp.bfloat16)
     part_lo = (gain_part - part_hi.astype(jnp.float32)).astype(jnp.bfloat16)
-    extra = jnp.concatenate([part_hi, part_lo])[None, None]
-    send = jnp.concatenate(
-        [term.reshape(count, rows, 2 * width), jnp.broadcast_to(extra, (count, 1, 2 * width))], axis=1
-    ).reshape(count * (rows + 1), 2 * width)
-    got = lax.all_to_all(send, "tensor", 0, 0, tiled=True).reshape(count, rows + 1, 2 * width)
+    gain_tile = jnp.concatenate([part_hi, part_lo]).reshape(gain_rows, lanes)
+    gain_tile = jnp.pad(gain_tile, ((0, rows - gain_rows), (0, 0)))
 
     hidden = jnp.dot(joined_all, weight_all, preferred_element_type=jnp.float32)
-    update = lax.all_to_all(
-        gelu_value(hidden).astype(jnp.bfloat16), "tensor", split_axis=0, concat_axis=1, tiled=True
-    ).astype(jnp.float32)
-    out_rows = (xfloat + update).astype(jnp.bfloat16)
+    update = gelu_value(hidden).astype(jnp.bfloat16)
+
+    chunks = jnp.concatenate(
+        [
+            term.reshape(count, rows, 2 * width),
+            update.reshape(count, rows, block_cols),
+            jnp.broadcast_to(gain_tile[None], (count, rows, lanes)),
+        ],
+        axis=2,
+    )
+    got = exchange(chunks, "tensor")
+    dfused = jnp.sum(got[:, :, : 2 * width].astype(jnp.float32), axis=0)
+    update_rows = got[:, :, 2 * width : 2 * width + block_cols].transpose(1, 0, 2).reshape(rows, width)
+    shares = got[:, :gain_rows, 2 * width + block_cols :].reshape(count, 2 * width).astype(jnp.float32)
+    gain_grad = jnp.sum(shares[:, :width] + shares[:, width:], axis=0)
+
+    out_rows = (xfloat + update_rows.astype(jnp.float32)).astype(jnp.bfloat16)
     received = shifted(out_rows, "section", 1)
-    ahead = lax.ppermute(
-        out_rows, "section", [(s, sections - 1 - s) for s in range(middle)]
-    )
-
-    dfused = jnp.sum(got[:, :rows].astype(jnp.float32), axis=0)
-    shares = got[:, rows].astype(jnp.float32)
-    gain_grad = jnp.sum(shares[:, :width] + shares[:, width:], axis=0)
     dnormed = dfused[:, :width]
     dside = dfused[:, width:].astype(jnp.bfloat16)
     bfloat, brinv, _ = normalize(back_acts[0], gain)
@@ -98,10 +111,8 @@
     )
     dx_rows = (back_grads[0].astype(jnp.float32) + dnorm_in).astype(jnp.bfloat16)
     grad_received = shifted(dx_rows, "section", -1)
-    behind = lax.ppermute(
-        dside, "section", [(s, sections - 1 - s) for s in range(middle, sections)]
-    )
-    mirrored = jnp.where(section_idx >= middle, ahead, behind)
+    payload = jnp.where(section_idx < middle, out_rows, dside)
+    mirrored = lax.ppermute(payload, "section", [(s, sections - 1 - s) for s in range(sections)])
     return (
         received[None],
         mirrored[None],

time: 305 us -> 309 us (1.013); the launches traced: 302 us -> 309 us
  waiting for transfers between devices: 200 us -> 219 us
  starting transfers between devices: 42.4 us -> 25.5 us
  local copies, waits for them, and re-layouts: 13.4 us -> 17.1 us
    all_to_all x5 -> x3, waiting for transfers between devices: 184 us -> 201 us  [exchange(): lax.all_to_all(chunks.reshape(count * rows, cols), axis, 0, 0, tiled=True)]
    ppermute x2 -> x1, waiting for transfers between devices: 0.01 us -> 11 us  [on_device(): lax.ppermute(payload, 'section', [(s, sections - 1 - s) for s in range(se...]
    all_to_all x5 -> x3, starting transfers between devices: 26.1 us -> 17.1 us  [exchange(): lax.all_to_all(chunks.reshape(count * rows, cols), axis, 0, 0, tiled=True)]
    ppermute x2 -> x1, starting transfers between devices: 9.15 us -> 0.87 us  [on_device(): lax.ppermute(payload, 'section', [(s, sections - 1 - s) for s in range(se...]
    ppermute x2, waiting for transfers between devices: 15.6 us -> 7.69 us  [shifted(): return lax.ppermute(block, axis, route)]
    concatenate x4 -> x5, other arithmetic: 4.75 us -> 10.7 us  [the longest x1 6.18 us: on_device(): jnp.concatenate([spread(raw, count), grad_blocks], axis=2)]
    slice x1 -> x2, local copies, waits for them, and re-layouts: 0.04 us -> 4.23 us  [the longest x1 3.19 us: on_device(): raw_all = got_b[:, :, :2 * width].reshape(count * rows, 2 * width)]
  transfers between devices with their start and end apart: 9 -> 6, of which waited for: 6 -> 6; matrix products, arithmetic and copies ran while one was open for 15% -> 8% of each run, Pallas kernels for 0% -> 0%
where the time goes in v3:
time: 309 us
  waiting for transfers between devices  219 us (71%)
  starting transfers between devices  25.5 us (8%)
  matrix products  23.9 us (8%)
  other arithmetic  22.1 us (7%)
  local copies, waits for them, and re-layouts  17.1 us (6%)
    all_to_all x3, waiting for transfers between devices, exchange(): lax.all_to_all(chunks.reshape(count * rows, cols), axis, 0, 0, tiled=True)  201 us
    all_to_all x3, starting transfers between devices, exchange(): lax.all_to_all(chunks.reshape(count * rows, cols), axis, 0, 0, tiled=True)  17.1 us
    ppermute x1, waiting for transfers between devices, on_device(): lax.ppermute(payload, 'section', [(s, sections - 1 - s) for s in range(se...  11 us
    dot_general x1, matrix products, on_device(): hidden = jnp.dot(joined_all, weight_all, preferred_element_type=jnp.float32)  7.83 us
    ppermute x2, waiting for transfers between devices, shifted(): return lax.ppermute(block, axis, route)  7.69 us
    ppermute x2, starting transfers between devices, shifted(): return lax.ppermute(block, axis, route)  7.53 us
    broadcast_in_dim x2, local copies, waits for them, and re-layouts, spread(): return jnp.broadcast_to(block[None], (count,) + block.shape)  6.78 us
    dot_general x1, matrix products, on_device(): lax.dot_general(bfused_all, dhidden, contract, preferred_element_type=jnp...  6.4 us
  transfers between devices with their start and end apart: 6, of which 6 were waited for; matrix products, arithmetic and copies ran while one was open for 8% of the time, Pallas kernels for 0%

profile of v3, /device:TPU:32, one launch (start us, length us, event | category | flops | bytes accessed | tf_op | source)
XLA Modules:
  0.0 308.7 jit_solution(15070564088048789913)
XLA Ops:
  1.7 1.2 pad_maximum_fusion.5
  2.9 3.4 %broadcast_in_dim.16 = bf16[8,64,6144]{2,1,0:T(8,128)(2,1)} broadcast(bf16[64,6144]{1,0:T(8,128)(2,1)S(1)} %pad_maximum_fusion.5), dimensions={1,2} | broadcast | bytes 7077888 | tf_op jit(solution)/shard_map/broadcast_in_dim | solution.py:37
  6.3 6.2 %pad_maximum_fusion.1 = bf16[8,64,6528]{2,1,0:T(8,128)(2,1)} fusion(bf16[8,64,384]{2,1,0:T(8,128)(2,1)S(1)} %bitcast.66, bf16[8,64,6144]{2,1,0:T(8,128)(2,1)} %broadcast_in_dim.16), kind=kLoop, calls=%fused_computation.8 | loop fusion | flops 13369344 | bytes 13369344 | tf_op jit(solution)/shard_map/concatenate | solution.py:60
  12.5 6.6 %all-to-all-start = ((bf16[8,64,6528]{2,1,0:T(8,128)(2,1)}), bf16[8,64,6528]{2,1,0:T(8,128)(2,1)}, u32[]{:S(2)}, u32[]{:S(2)}) async-start(bf16[8,64,6528]{2,1,0:T(8,128)(2,1)} %pad_maximum_fusion.1), calls=%async_computation | async-start | bytes 13369344 | tf_op jit(solution)/shard_map/all_to_all | solution.py:42
  19.6 73.6 %all-to-all-done = bf16[8,64,6528]{2,1,0:T(8,128)(2,1)} async-done(((bf16[8,64,6528]{2,1,0:T(8,128)(2,1)}), bf16[8,64,6528]{2,1,0:T(8,128)(2,1)}, u32[]{:S(2)}, u32[]{:S(2)}) %all-to-all-start) | async-done | bytes 6684704 | tf_op jit(solution)/shard_map/all_to_all | solution.py:42
  93.1 3.4 %broadcast_in_dim.17 = bf16[8,64,6144]{2,1,0:T(8,128)(2,1)} broadcast(bf16[64,6144]{1,0:T(8,128)(2,1)S(1)} %pad_maximum_fusion.6), dimensions={1,2} | broadcast | bytes 7077888 | tf_op jit(solution)/shard_map/broadcast_in_dim | solution.py:37
  96.5 5.2 %all-to-all-start.1 = ((bf16[8,64,6144]{2,1,0:T(8,128)(2,1)}), bf16[8,64,6144]{2,1,0:T(8,128)(2,1)}, u32[]{:S(2)}, u32[]{:S(2)}) async-start(bf16[8,64,6144]{2,1,0:T(8,128)(2,1)} %broadcast_in_dim.17), calls=%async_computation.1 | async-start | bytes 12582912 | tf_op jit(solution)/shard_map/all_to_all | solution.py:42
  102.8 3.2 %slice.38 = bf16[8,64,6144]{2,1,0:T(8,128)(2,1)S(1)} slice(bf16[8,64,6528]{2,1,0:T(8,128)(2,1)} %all-to-all-done), slice={[0:8], [0:64], [0:6144]} | slice | bytes 12582912 | tf_op jit(solution)/shard_map/slice | solution.py:66
  107.0 1.3 fusion.3
  109.4 3.4 %fusion.9 = f32[512,384]{1,0:T(8,128)S(1)} fusion(bf16[1,6144,384]{2,1,0:T(8,128)(2,1)S(1)} %bitcast.84, bf16[512,3072]{1,0:T(8,128)(2,1)S(1)} %slice.50, bf16[512,3072]{1,0:T(8,128)(2,1)S(1)} %fusion.3), kind=kOutput, calls=%fused_computation.18 | convolution fusion | flops 2428502016 | bytes 11796480 | tf_op jit(solution)/shard_map/dot_general | solution.py:70
  112.8 6.3 %convolution_convert_fusion = bf16[512,6144]{1,0:T(8,128)(2,1)S(1)} fusion(bf16[1,6144,384]{2,1,0:T(8,128)(2,1)} %param.10, f32[512,384]{1,0:T(8,128)S(1)} %fusion.9, bf16[512,384]{1,0:T(8,128)(2,1)S(1)} %bitcast.70), kind=kOutput, calls=%fused_computation.4 | convolution fusion | flops 2422996992 | bytes 12189696 | tf_op jit(solution)/shard_map/dot_general | solution.py:77
  119.1 1.5 fusion.5
  120.6 1.1 copy-done
  121.8 50.7 %all-to-all-done.1 = bf16[8,64,6144]{2,1,0:T(8,128)(2,1)} async-done(((bf16[8,64,6144]{2,1,0:T(8,128)(2,1)}), bf16[8,64,6144]{2,1,0:T(8,128)(2,1)}, u32[]{:S(2)}, u32[]{:S(2)}) %all-to-all-start.1) | async-done | bytes 6291488 | tf_op jit(solution)/shard_map/all_to_all | solution.py:42
  172.4 7.8 %fusion.22 = bf16[512,384]{1,0:T(8,128)(2,1)S(1)} fusion(bf16[512,6144]{1,0:T(8,128)(2,1)} %bitcast.11, bf16[1,6144,384]{2,1,0:T(8,128)(2,1)} %param.10), kind=kOutput, calls=%fused_computation.40 | convolution fusion | flops 2417688576 | bytes 11403264 | tf_op jit(solution)/shard_map/dot_general | solution.py:86
  180.3 3.3 %pad_maximum_fusion = bf16[8,64,6656]{2,1,0:T(8,128)(2,1)} fusion(bf16[8,64,128]{2,1,0:T(8,128)(2,1)S(1)} %broadcast_in_dim.18, bf16[8,64,384]{2,1,0:T(8,128)(2,1)S(1)} %bitcast.77, bf16[8,64,6144]{2,1,0:T(8,128)(2,1)S(1)} %bitcast.63), kind=kLoop, calls=%fused_computation.7 | loop fusion | flops 20447232 | bytes 13631488 | tf_op jit(solution)/shard_map/concatenate | solution.py:89
  183.6 5.2 %all-to-all-start.2 = ((bf16[8,64,6656]{2,1,0:T(8,128)(2,1)}), bf16[8,64,6656]{2,1,0:T(8,128)(2,1)}, u32[]{:S(2)}, u32[]{:S(2)}) async-start(bf16[8,64,6656]{2,1,0:T(8,128)(2,1)} %pad_maximum_fusion), calls=%async_computation.2 | async-start | bytes 13631488 | tf_op jit(solution)/shard_map/all_to_all | solution.py:42
  188.9 76.3 %all-to-all-done.2 = bf16[8,64,6656]{2,1,0:T(8,128)(2,1)} async-done(((bf16[8,64,6656]{2,1,0:T(8,128)(2,1)}), bf16[8,64,6656]{2,1,0:T(8,128)(2,1)}, u32[]{:S(2)}, u32[]{:S(2)}) %all-to-all-start.2) | async-done | bytes 6815776 | tf_op jit(solution)/shard_map/all_to_all | solution.py:42
  266.3 4.2 %convert_reduce_fusion = f32[64,6144]{1,0:T(8,128)S(1)} fusion(bf16[8,64,6656]{2,1,0:T(8,128)(2,1)} %all-to-all-done.2), kind=kLoop, calls=%fused_computation | loop fusion | flops 5898240 | bytes 7864320 | tf_op jit(solution)/shard_map/reduce_sum | solution.py:98
  271.2 7.5 %collective-permute-start.2 = (bf16[64,3072]{1,0:T(8,128)(2,1)S(1)}, bf16[64,3072]{1,0:T(8,128)(2,1)S(1)}, u32[]{:S(2)}, u32[]{:S(2)}) collective-permute-start(bf16[64,3072]{1,0:T(8,128)(2,1)S(1)} %fusion.29), channel_id=1, source_target_pairs={{8,0},{16,8},{24,16},{32,24},{40,32},{48,40},{56,48},{64,56},{72,6... | collective-permute-start | bytes 1179656 | tf_op jit(solution)/shard_map/ppermute | solution.py:14
  279.8 6.4 %fusion = bf16[1,6144,384]{2,1,0:T(8,128)(2,1)} fusion(bf16[512,3072]{1,0:T(8,128)(2,1)S(1)} %copy-done.5, bf16[512,3072]{1,0:T(8,128)(2,1)S(1)} %copy-done.7, f32[512,384]{1,0:T(8,128)S(1)} %fusion.9, bf16[512,384]{1,0:T(8,128)(2,1)S(1)} %bitcast.71), kind=kOutput, calls=%fused_computation.6 | convolution fusion | flops 2434793472 | bytes 12189696 | tf_op jit(solution)/shard_map/dot_general | solution.py:73
  287.8 3.5 %collective-permute-done.2 = bf16[64,3072]{1,0:T(8,128)(2,1)S(1)} collective-permute-done((bf16[64,3072]{1,0:T(8,128)(2,1)S(1)}, bf16[64,3072]{1,0:T(8,128)(2,1)S(1)}, u32[]{:S(2)}, u32[]{:S(2)}) %collective-permute-start.2) | collective-permute-done | bytes 393248 | tf_op jit(solution)/shard_map/ppermute | solution.py:14
  291.3 11.0 %collective-permute-done.1 = bf16[64,3072]{1,0:T(8,128)(2,1)S(1)} collective-permute-done((bf16[64,3072]{1,0:T(8,128)(2,1)S(1)}, bf16[64,3072]{1,0:T(8,128)(2,1)S(1)}, u32[]{:S(2)}, u32[]{:S(2)}) %collective-permute-start.1) | collective-permute-done | bytes 393248 | tf_op jit(solution)/shard_map/ppermute | solution.py:115
  302.2 4.2 %collective-permute-done = bf16[64,3072]{1,0:T(8,128)(2,1)S(1)} collective-permute-done((bf16[64,3072]{1,0:T(8,128)(2,1)S(1)}, bf16[64,3072]{1,0:T(8,128)(2,1)S(1)}, u32[]{:S(2)}, u32[]{:S(2)}) %collective-permute-start) | collective-permute-done | bytes 393248 | tf_op jit(solution)/shard_map/ppermute | solution.py:14
  (53 shorter events, 11.4 us)
Async XLA Ops:
  12.5 6.6 %copy-start.3 = (bf16[1,64,3072]{2,1,0:T(8,128)(2,1)S(1)}, bf16[1,64,3072]{2,1,0:T(8,128)(2,1)}, u32[]{:S(2)}) copy-start(bf16[1,64,3072]{2,1,0:T(8,128)(2,1)} %param.7) | copy-start | bytes 1179652
  12.5 6.8 %copy-start.10 = (f32[1,3072]{1,0:T(1,128)S(1)}, f32[1,3072]{1,0:T(1,128)}, u32[]{:S(2)}) copy-start(f32[1,3072]{1,0:T(1,128)} %param.9) | copy-start | bytes 36868
  12.5 7.0 %copy-start.9 = (bf16[1,64,3072]{2,1,0:T(8,128)(2,1)S(1)}, bf16[1,64,3072]{2,1,0:T(8,128)(2,1)}, u32[]{:S(2)}) copy-start(bf16[1,64,3072]{2,1,0:T(8,128)(2,1)} %param.8) | copy-start | bytes 1179652
  12.5 80.6 %all-to-all-start = ((bf16[8,64,6528]{2,1,0:T(8,128)(2,1)}), bf16[8,64,6528]{2,1,0:T(8,128)(2,1)}, u32[]{:S(2)}, u32[]{:S(2)}) async-start(bf16[8,64,6528]{2,1,0:T(8,128)(2,1)} %pad_maximum_fusion.1), calls=%async_computation | async-start | bytes 13369344 | tf_op jit(solution)/shard_map/all_to_all | solution.py:42
  96.5 75.9 %all-to-all-start.1 = ((bf16[8,64,6144]{2,1,0:T(8,128)(2,1)}), bf16[8,64,6144]{2,1,0:T(8,128)(2,1)}, u32[]{:S(2)}, u32[]{:S(2)}) async-start(bf16[8,64,6144]{2,1,0:T(8,128)(2,1)} %broadcast_in_dim.17), calls=%async_computation.1 | async-start | bytes 12582912 | tf_op jit(solution)/shard_map/all_to_all | solution.py:42
  106.0 3.3 %slice-start = ((s8[4718592]{0:T(1024)(128)(4,1)}), s8[4194304]{0:T(1024)(128)(4,1)S(1)}, s32[]{:S(2)}) async-start(s8[4718592]{0:T(1024)(128)(4,1)} %bitcast.83), calls=%async_computation.3 | async-start | bytes 8388608
  106.3 6.6 %copy-start.4 = (bf16[512,3072]{1,0:T(8,128)(2,1)}, bf16[512,3072]{1,0:T(8,128)(2,1)S(1)}, u32[]{:S(2)}) copy-start(bf16[512,3072]{1,0:T(8,128)(2,1)S(1)} %slice.50) | copy-start | bytes 9437188
  106.3 3.1 %slice-start.1 = ((s8[4718592]{0:T(1024)(128)(4,1)}), s8[524288]{0:T(1024)(128)(4,1)S(1)}, s32[]{:S(2)}) async-start(s8[4718592]{0:T(1024)(128)(4,1)} %bitcast.83), calls=%async_computation.4 | async-start | bytes 1048576
  109.4 3.4 %copy-start.6 = (bf16[512,3072]{1,0:T(8,128)(2,1)}, bf16[512,3072]{1,0:T(8,128)(2,1)S(1)}, u32[]{:S(2)}) copy-start(bf16[512,3072]{1,0:T(8,128)(2,1)S(1)} %fusion.3) | copy-start | bytes 9437188
  119.1 2.7 copy-start
  172.4 7.9 %copy-start.1 = (bf16[512,6144]{1,0:T(8,128)(2,1)S(1)}, bf16[512,6144]{1,0:T(8,128)(2,1)}, u32[]{:S(2)}) copy-start(bf16[512,6144]{1,0:T(8,128)(2,1)} %copy-done) | copy-start | bytes 18874372
  183.6 81.6 %all-to-all-start.2 = ((bf16[8,64,6656]{2,1,0:T(8,128)(2,1)}), bf16[8,64,6656]{2,1,0:T(8,128)(2,1)}, u32[]{:S(2)}, u32[]{:S(2)}) async-start(bf16[8,64,6656]{2,1,0:T(8,128)(2,1)} %pad_maximum_fusion), calls=%async_computation.2 | async-start | bytes 13631488 | tf_op jit(solution)/shard_map/all_to_all | solution.py:42
  188.9 81.7 %copy-start.2 = (bf16[1,64,3072]{2,1,0:T(8,128)(2,1)S(1)}, bf16[1,64,3072]{2,1,0:T(8,128)(2,1)}, u32[]{:S(2)}) copy-start(bf16[1,64,3072]{2,1,0:T(8,128)(2,1)} %param.11) | copy-start | bytes 1179652
  188.9 82.0 %copy-start.8 = (bf16[1,64,3072]{2,1,0:T(8,128)(2,1)S(1)}, bf16[1,64,3072]{2,1,0:T(8,128)(2,1)}, u32[]{:S(2)}) copy-start(bf16[1,64,3072]{2,1,0:T(8,128)(2,1)} %param.13) | copy-start | bytes 1179652
  266.3 13.4 %copy-start.5 = (bf16[512,3072]{1,0:T(8,128)(2,1)S(1)}, bf16[512,3072]{1,0:T(8,128)(2,1)}, u32[]{:S(2)}) copy-start(bf16[512,3072]{1,0:T(8,128)(2,1)} %copy-done.4) | copy-start | bytes 9437188
  266.3 13.4 %copy-start.7 = (bf16[512,3072]{1,0:T(8,128)(2,1)S(1)}, bf16[512,3072]{1,0:T(8,128)(2,1)}, u32[]{:S(2)}) copy-start(bf16[512,3072]{1,0:T(8,128)(2,1)} %copy-done.6) | copy-start | bytes 9437188
  271.2 20.1 %collective-permute-start.2 = (bf16[64,3072]{1,0:T(8,128)(2,1)S(1)}, bf16[64,3072]{1,0:T(8,128)(2,1)S(1)}, u32[]{:S(2)}, u32[]{:S(2)}) collective-permute-start(bf16[64,3072]{1,0:T(8,128)(2,1)S(1)} %fusion.29), channel_id=1, source_target_pairs={{8,0},{16,8},{24,16},{32,24},{40,32},{48,40},{56,48},{64,56},{72,6... | collective-permute-start | bytes 1179656 | tf_op jit(solution)/shard_map/ppermute | solution.py:14
  278.8 23.4 %collective-permute-start.1 = (bf16[64,3072]{1,0:T(8,128)(2,1)S(1)}, bf16[64,3072]{1,0:T(8,128)(2,1)S(1)}, u32[]{:S(2)}, u32[]{:S(2)}) collective-permute-start(bf16[64,3072]{1,0:T(8,128)(2,1)S(1)} %get-tuple-element.11), channel_id=1, source_target_pairs={{0,248},{8,240},{16,232},{24,224},{32,216},{40,208},{48,200},{56,1... | collective-permute-start | bytes 1179656 | tf_op jit(solution)/shard_map/ppermute | solution.py:115
  279.7 26.8 %collective-permute-start = (bf16[64,3072]{1,0:T(8,128)(2,1)S(1)}, bf16[64,3072]{1,0:T(8,128)(2,1)S(1)}, u32[]{:S(2)}, u32[]{:S(2)}) collective-permute-start(bf16[64,3072]{1,0:T(8,128)(2,1)S(1)} %get-tuple-element.12), channel_id=1, source_target_pairs={{248,0},{0,8},{8,16},{16,24},{24,32},{32,40},{40,48},{48,56},{56,6... | collective-permute-start | bytes 1179656 | tf_op jit(solution)/shard_map/ppermute | solution.py:14

commit v4 on v3

--- a/solution.py
+++ b/solution.py
@@ -86,24 +86,31 @@
     hidden = jnp.dot(joined_all, weight_all, preferred_element_type=jnp.float32)
     update = gelu_value(hidden).astype(jnp.bfloat16)
 
-    chunks = jnp.concatenate(
+    chunks_a = jnp.concatenate(
+        [term[:, width:].reshape(count, rows, width), update.reshape(count, rows, block_cols)], axis=2
+    )
+    chunks_a, weight_grads = lax.optimization_barrier((chunks_a, weight_grads))
+    got_a = exchange(chunks_a, "tensor")
+    dside = jnp.sum(got_a[:, :, :width].astype(jnp.float32), axis=0).astype(jnp.bfloat16)
+    update_rows = got_a[:, :, width:].transpose(1, 0, 2).reshape(rows, width)
+    out_rows = (xfloat + update_rows.astype(jnp.float32)).astype(jnp.bfloat16)
+    received = shifted(out_rows, "section", 1)
+    payload = jnp.where(section_idx < middle, out_rows, dside)
+    mirrored = lax.ppermute(payload, "section", [(s, sections - 1 - s) for s in range(sections)])
+
+    chunks_b = jnp.concatenate(
         [
-            term.reshape(count, rows, 2 * width),
-            update.reshape(count, rows, block_cols),
+            term[:, :width].reshape(count, rows, width),
             jnp.broadcast_to(gain_tile[None], (count, rows, lanes)),
         ],
         axis=2,
     )
-    got = exchange(chunks, "tensor")
-    dfused = jnp.sum(got[:, :, : 2 * width].astype(jnp.float32), axis=0)
-    update_rows = got[:, :, 2 * width : 2 * width + block_cols].transpose(1, 0, 2).reshape(rows, width)
-    shares = got[:, :gain_rows, 2 * width + block_cols :].reshape(count, 2 * width).astype(jnp.float32)
+    got_a, chunks_b = lax.optimization_barrier((got_a, chunks_b))
+    got_b2 = exchange(chunks_b, "tensor")
+    dnormed = jnp.sum(got_b2[:, :, :width].astype(jnp.float32), axis=0)
+    shares = got_b2[:, :gain_rows, width:].reshape(count, 2 * width).astype(jnp.float32)
     gain_grad = jnp.sum(shares[:, :width] + shares[:, width:], axis=0)
 
-    out_rows = (xfloat + update_rows.astype(jnp.float32)).astype(jnp.bfloat16)
-    received = shifted(out_rows, "section", 1)
-    dnormed = dfused[:, :width]
-    dside = dfused[:, width:].astype(jnp.bfloat16)
     bfloat, brinv, _ = normalize(back_acts[0], gain)
     scaled = gain * dnormed
     dnorm_in = brinv * scaled - bfloat * brinv * brinv * brinv * jnp.mean(
@@ -111,8 +118,6 @@
     )
     dx_rows = (back_grads[0].astype(jnp.float32) + dnorm_in).astype(jnp.bfloat16)
     grad_received = shifted(dx_rows, "section", -1)
-    payload = jnp.where(section_idx < middle, out_rows, dside)
-    mirrored = lax.ppermute(payload, "section", [(s, sections - 1 - s) for s in range(sections)])
     return (
         received[None],
         mirrored[None],

time: 309 us -> 302 us (0.977)
  waiting for transfers between devices: 219 us -> 192 us
  starting transfers between devices: 25.5 us -> 35.7 us
  local copies, waits for them, and re-layouts: 17.1 us -> 21.9 us
    all_to_all x3 -> x4, waiting for transfers between devices: 201 us -> 185 us  [exchange(): lax.all_to_all(chunks.reshape(count * rows, cols), axis, 0, 0, tiled=True)]
    ppermute x1, waiting for transfers between devices: 11 us -> 0.01 us  [on_device(): lax.ppermute(payload, 'section', [(s, sections - 1 - s) for s in range(se...]
    ppermute x1, starting transfers between devices: 0.87 us -> 7.26 us  [on_device(): lax.ppermute(payload, 'section', [(s, sections - 1 - s) for s in range(se...]
    all_to_all x3 -> x4, starting transfers between devices: 17.1 us -> 21 us  [exchange(): lax.all_to_all(chunks.reshape(count * rows, cols), axis, 0, 0, tiled=True)]
    unnamed x31 -> x29, local copies, waits for them, and re-layouts: 5.68 us -> 8.32 us
  transfers between devices with their start and end apart: 6 -> 7, of which waited for: 6 -> 5; matrix products, arithmetic and copies ran while one was open for 8% -> 13% of each run, Pallas kernels for 0% -> 0%
where the time goes in v4:
time: 302 us; the launch traced here: 299 us
  waiting for transfers between devices  192 us (64%)
  starting transfers between devices  35.7 us (12%)
  other arithmetic  24.4 us (8%)
  matrix products  23.8 us (8%)
  local copies, waits for them, and re-layouts  21.9 us (7%)
    all_to_all x4, waiting for transfers between devices, exchange(): lax.all_to_all(chunks.reshape(count * rows, cols), axis, 0, 0, tiled=True)  185 us
    all_to_all x4, starting transfers between devices, exchange(): lax.all_to_all(chunks.reshape(count * rows, cols), axis, 0, 0, tiled=True)  21 us
    unnamed x29, local copies, waits for them, and re-layouts  8.32 us
    ppermute x2, waiting for transfers between devices, shifted(): return lax.ppermute(block, axis, route)  7.75 us
    dot_general x1, matrix products, on_device(): hidden = jnp.dot(joined_all, weight_all, preferred_element_type=jnp.float32)  7.68 us
    ppermute x2, starting transfers between devices, shifted(): return lax.ppermute(block, axis, route)  7.49 us
    ppermute x1, starting transfers between devices, on_device(): lax.ppermute(payload, 'section', [(s, sections - 1 - s) for s in range(se...  7.26 us
    broadcast_in_dim x2, local copies, waits for them, and re-layouts, spread(): return jnp.broadcast_to(block[None], (count,) + block.shape)  6.79 us
  transfers between devices with their start and end apart: 7, of which 5 were waited for; matrix products, arithmetic and copies ran while one was open for 13% of the time, Pallas kernels for 0%

profile of v4, /device:TPU:32, one launch (start us, length us, event | category | flops | bytes accessed | tf_op | source)
XLA Modules:
  0.0 299.0 jit_solution(17104577902542001586)
XLA Ops:
  2.9 3.4 %broadcast_in_dim.16 = bf16[8,64,6144]{2,1,0:T(8,128)(2,1)} broadcast(bf16[64,6144]{1,0:T(8,128)(2,1)S(1)} %pad_maximum_fusion.6), dimensions={1,2} | broadcast | bytes 7077888 | tf_op jit(solution)/shard_map/broadcast_in_dim | solution.py:37
  6.3 6.1 %pad_maximum_fusion = bf16[8,64,6528]{2,1,0:T(8,128)(2,1)} fusion(bf16[8,64,384]{2,1,0:T(8,128)(2,1)S(1)} %bitcast.67, bf16[8,64,6144]{2,1,0:T(8,128)(2,1)} %broadcast_in_dim.16), kind=kLoop, calls=%fused_computation.5 | loop fusion | flops 13369344 | bytes 13369344 | tf_op jit(solution)/shard_map/concatenate | solution.py:60
  12.4 6.7 %all-to-all-start = ((bf16[8,64,6528]{2,1,0:T(8,128)(2,1)}), bf16[8,64,6528]{2,1,0:T(8,128)(2,1)}, u32[]{:S(2)}, u32[]{:S(2)}) async-start(bf16[8,64,6528]{2,1,0:T(8,128)(2,1)} %pad_maximum_fusion), calls=%async_computation | async-start | bytes 13369344 | tf_op jit(solution)/shard_map/all_to_all | solution.py:42
  19.6 73.5 %all-to-all-done = bf16[8,64,6528]{2,1,0:T(8,128)(2,1)} async-done(((bf16[8,64,6528]{2,1,0:T(8,128)(2,1)}), bf16[8,64,6528]{2,1,0:T(8,128)(2,1)}, u32[]{:S(2)}, u32[]{:S(2)}) %all-to-all-start) | async-done | bytes 6684704 | tf_op jit(solution)/shard_map/all_to_all | solution.py:42
  93.0 3.4 %broadcast_in_dim.17 = bf16[8,64,6144]{2,1,0:T(8,128)(2,1)} broadcast(bf16[64,6144]{1,0:T(8,128)(2,1)S(1)} %pad_maximum_fusion.7), dimensions={1,2} | broadcast | bytes 7077888 | tf_op jit(solution)/shard_map/broadcast_in_dim | solution.py:37
  96.5 5.2 %all-to-all-start.1 = ((bf16[8,64,6144]{2,1,0:T(8,128)(2,1)}), bf16[8,64,6144]{2,1,0:T(8,128)(2,1)}, u32[]{:S(2)}, u32[]{:S(2)}) async-start(bf16[8,64,6144]{2,1,0:T(8,128)(2,1)} %broadcast_in_dim.17), calls=%async_computation.1 | async-start | bytes 12582912 | tf_op jit(solution)/shard_map/all_to_all | solution.py:42
  102.7 3.2 %slice.38 = bf16[8,64,6144]{2,1,0:T(8,128)(2,1)S(1)} slice(bf16[8,64,6528]{2,1,0:T(8,128)(2,1)} %all-to-all-done), slice={[0:8], [0:64], [0:6144]} | slice | bytes 12582912 | tf_op jit(solution)/shard_map/slice | solution.py:66
  108.2 2.2 slice-done
  110.5 3.4 %fusion.8 = f32[512,384]{1,0:T(8,128)S(1)} fusion(bf16[1,6144,384]{2,1,0:T(8,128)(2,1)S(1)} %bitcast.85, bf16[512,3072]{1,0:T(8,128)(2,1)S(1)} %slice.50, bf16[512,3072]{1,0:T(8,128)(2,1)S(1)} %fusion.2), kind=kOutput, calls=%fused_computation.16 | convolution fusion | flops 2428502016 | bytes 11796480 | tf_op jit(solution)/shard_map/dot_general | solution.py:70
  114.8 6.2 %convolution_convert_fusion = bf16[512,6144]{1,0:T(8,128)(2,1)S(1)} fusion(bf16[1,6144,384]{2,1,0:T(8,128)(2,1)} %param.10, f32[512,384]{1,0:T(8,128)S(1)} %fusion.8, bf16[512,384]{1,0:T(8,128)(2,1)S(1)} %bitcast.75), kind=kOutput, calls=%fused_computation.3 | convolution fusion | flops 2422996992 | bytes 12189696 | tf_op jit(solution)/shard_map/dot_general | solution.py:77
  121.1 2.2 fusion.66
  124.6 6.5 %convolution_convert_fusion.1 = bf16[6144,384]{1,0:T(8,128)(2,1)} fusion(bf16[512,3072]{1,0:T(8,128)(2,1)S(1)} %slice.50, bf16[512,3072]{1,0:T(8,128)(2,1)S(1)} %fusion.2, f32[512,384]{1,0:T(8,128)S(1)} %copy-done.9, bf16[512,384]{1,0:T(8,128)(2,1)S(1)} %bitcast.76), kind=kOutput, calls=%fused_computation.4 | convolution fusion | flops 2434793472 | bytes 12189696 | tf_op jit(solution)/shard_map/dot_general | solution.py:73
  131.1 41.3 %all-to-all-done.1 = bf16[8,64,6144]{2,1,0:T(8,128)(2,1)} async-done(((bf16[8,64,6144]{2,1,0:T(8,128)(2,1)}), bf16[8,64,6144]{2,1,0:T(8,128)(2,1)}, u32[]{:S(2)}, u32[]{:S(2)}) %all-to-all-start.1) | async-done | bytes 6291488 | tf_op jit(solution)/shard_map/all_to_all | solution.py:42
  172.4 7.7 %fusion.21 = bf16[512,384]{1,0:T(8,128)(2,1)S(1)} fusion(bf16[512,6144]{1,0:T(8,128)(2,1)} %bitcast.11, bf16[1,6144,384]{2,1,0:T(8,128)(2,1)} %param.10), kind=kOutput, calls=%fused_computation.41 | convolution fusion | flops 2417688576 | bytes 11403264 | tf_op jit(solution)/shard_map/dot_general | solution.py:86
  180.1 2.1 pad_maximum_fusion.4
  182.1 4.2 %all-to-all-start.2 = ((bf16[8,64,3456]{2,1,0:T(8,128)(2,1)}), bf16[8,64,3456]{2,1,0:T(8,128)(2,1)S(1)}, u32[]{:S(2)}, u32[]{:S(2)}) async-start(bf16[8,64,3456]{2,1,0:T(8,128)(2,1)} %pad_maximum_fusion.4), calls=%async_computation.2 | async-start | bytes 7077888 | tf_op jit(solution)/shard_map/all_to_all | solution.py:42
  186.3 4.3 %fusion.4 = f32[3072]{0:T(1024)S(1)} fusion(f32[512]{0:T(512)S(1)} %add_rsqrt_fusion, bf16[512,6144]{1,0:T(8,128)(2,1)} %bitcast.62, bf16[512,6144]{1,0:T(8,128)(2,1)} %copy-done.1), kind=kLoop, calls=%fused_computation.10 | loop fusion | flops 7861248 | bytes 6305792 | tf_op jit(solution)/shard_map/reduce_sum | solution.py:80
  192.7 34.7 %all-to-all-done.2 = bf16[8,64,3456]{2,1,0:T(8,128)(2,1)S(1)} async-done(((bf16[8,64,3456]{2,1,0:T(8,128)(2,1)}), bf16[8,64,3456]{2,1,0:T(8,128)(2,1)S(1)}, u32[]{:S(2)}, u32[]{:S(2)}) %all-to-all-start.2) | async-done | bytes 3538976 | tf_op jit(solution)/shard_map/all_to_all | solution.py:42
  227.4 4.9 %all-to-all-start.3 = ((bf16[8,64,3200]{2,1,0:T(8,128)(2,1)}), bf16[8,64,3200]{2,1,0:T(8,128)(2,1)}, u32[]{:S(2)}, u32[]{:S(2)}) async-start(bf16[8,64,3200]{2,1,0:T(8,128)(2,1)} %pad_maximum_fusion.5), calls=%async_computation.3 | async-start | bytes 6553600 | tf_op jit(solution)/shard_map/all_to_all | solution.py:42
  233.5 7.3 %collective-permute-start.1 = (bf16[64,3072]{1,0:T(8,128)(2,1)S(1)}, bf16[64,3072]{1,0:T(8,128)(2,1)S(1)}, u32[]{:S(2)}, u32[]{:S(2)}) collective-permute-start(bf16[64,3072]{1,0:T(8,128)(2,1)S(1)} %get-tuple-element.19), channel_id=1, source_target_pairs={{0,248},{8,240},{16,232},{24,224},{32,216},{40,208},{48,200},{56,1... | collective-permute-start | bytes 1179656 | tf_op jit(solution)/shard_map/ppermute | solution.py:99
  241.8 35.1 %all-to-all-done.3 = bf16[8,64,3200]{2,1,0:T(8,128)(2,1)} async-done(((bf16[8,64,3200]{2,1,0:T(8,128)(2,1)}), bf16[8,64,3200]{2,1,0:T(8,128)(2,1)}, u32[]{:S(2)}, u32[]{:S(2)}) %all-to-all-start.3) | async-done | bytes 3276832 | tf_op jit(solution)/shard_map/all_to_all | solution.py:42
  276.8 2.5 convert_reduce_fusion
  281.0 6.4 %collective-permute-start.2 = (bf16[64,3072]{1,0:T(8,128)(2,1)S(1)}, bf16[64,3072]{1,0:T(8,128)(2,1)S(1)}, u32[]{:S(2)}, u32[]{:S(2)}) collective-permute-start(bf16[64,3072]{1,0:T(8,128)(2,1)S(1)} %fusion.28), channel_id=1, source_target_pairs={{8,0},{16,8},{24,16},{32,24},{40,32},{48,40},{56,48},{64,56},{72,6... | collective-permute-start | bytes 1179656 | tf_op jit(solution)/shard_map/ppermute | solution.py:14
  289.0 7.7 %collective-permute-done.2 = bf16[64,3072]{1,0:T(8,128)(2,1)S(1)} collective-permute-done((bf16[64,3072]{1,0:T(8,128)(2,1)S(1)}, bf16[64,3072]{1,0:T(8,128)(2,1)S(1)}, u32[]{:S(2)}, u32[]{:S(2)}) %collective-permute-start.2) | collective-permute-done | bytes 393248 | tf_op jit(solution)/shard_map/ppermute | solution.py:14
  (56 shorter events, 18.0 us)
Async XLA Ops:
  12.4 6.7 %copy-start.3 = (bf16[1,64,3072]{2,1,0:T(8,128)(2,1)S(1)}, bf16[1,64,3072]{2,1,0:T(8,128)(2,1)}, u32[]{:S(2)}) copy-start(bf16[1,64,3072]{2,1,0:T(8,128)(2,1)} %param.7) | copy-start | bytes 1179652
  12.4 6.9 %copy-start.7 = (f32[1,3072]{1,0:T(1,128)S(1)}, f32[1,3072]{1,0:T(1,128)}, u32[]{:S(2)}) copy-start(f32[1,3072]{1,0:T(1,128)} %param.9) | copy-start | bytes 36868
  12.4 7.1 %copy-start.6 = (bf16[1,64,3072]{2,1,0:T(8,128)(2,1)S(1)}, bf16[1,64,3072]{2,1,0:T(8,128)(2,1)}, u32[]{:S(2)}) copy-start(bf16[1,64,3072]{2,1,0:T(8,128)(2,1)} %param.8) | copy-start | bytes 1179652
  12.4 80.6 %all-to-all-start = ((bf16[8,64,6528]{2,1,0:T(8,128)(2,1)}), bf16[8,64,6528]{2,1,0:T(8,128)(2,1)}, u32[]{:S(2)}, u32[]{:S(2)}) async-start(bf16[8,64,6528]{2,1,0:T(8,128)(2,1)} %pad_maximum_fusion), calls=%async_computation | async-start | bytes 13369344 | tf_op jit(solution)/shard_map/all_to_all | solution.py:42
  96.5 75.9 %all-to-all-start.1 = ((bf16[8,64,6144]{2,1,0:T(8,128)(2,1)}), bf16[8,64,6144]{2,1,0:T(8,128)(2,1)}, u32[]{:S(2)}, u32[]{:S(2)}) async-start(bf16[8,64,6144]{2,1,0:T(8,128)(2,1)} %broadcast_in_dim.17), calls=%async_computation.1 | async-start | bytes 12582912 | tf_op jit(solution)/shard_map/all_to_all | solution.py:42
  105.9 15.1 %copy-start = (bf16[8,64,6144]{2,1,0:T(8,128)(2,1)}, bf16[8,64,6144]{2,1,0:T(8,128)(2,1)S(1)}, u32[]{:S(2)}) copy-start(bf16[8,64,6144]{2,1,0:T(8,128)(2,1)S(1)} %slice.38) | copy-start | bytes 18874372
  105.9 4.5 %slice-start = ((s8[4718592]{0:T(1024)(128)(4,1)}), s8[4194304]{0:T(1024)(128)(4,1)S(1)}, s32[]{:S(2)}) async-start(s8[4718592]{0:T(1024)(128)(4,1)} %bitcast.84), calls=%async_computation.4 | async-start | bytes 8388608
  106.2 4.3 %slice-start.1 = ((s8[4718592]{0:T(1024)(128)(4,1)}), s8[524288]{0:T(1024)(128)(4,1)S(1)}, s32[]{:S(2)}) async-start(s8[4718592]{0:T(1024)(128)(4,1)} %bitcast.84), calls=%async_computation.5 | async-start | bytes 1048576
  113.9 0.9 copy-start.8
  121.0 3.5 %copy-start.1 = (bf16[512,6144]{1,0:T(8,128)(2,1)}, bf16[512,6144]{1,0:T(8,128)(2,1)S(1)}, u32[]{:S(2)}) copy-start(bf16[512,6144]{1,0:T(8,128)(2,1)S(1)} %convolution_convert_fusion) | copy-start | bytes 18874372
  121.1 3.5 %copy-start.9 = (f32[512,384]{1,0:T(8,128)S(1)}, f32[512,384]{1,0:T(8,128)}, u32[]{:S(2)}) copy-start(f32[512,384]{1,0:T(8,128)} %copy-done.8) | copy-start | bytes 2359300
  182.1 45.3 %all-to-all-start.2 = ((bf16[8,64,3456]{2,1,0:T(8,128)(2,1)}), bf16[8,64,3456]{2,1,0:T(8,128)(2,1)S(1)}, u32[]{:S(2)}, u32[]{:S(2)}) async-start(bf16[8,64,3456]{2,1,0:T(8,128)(2,1)} %pad_maximum_fusion.4), calls=%async_computation.2 | async-start | bytes 7077888 | tf_op jit(solution)/shard_map/all_to_all | solution.py:42
  186.3 4.4 %copy-start.2 = (bf16[512,3072]{1,0:T(8,128)(2,1)S(1)}, bf16[512,3072]{1,0:T(8,128)(2,1)}, u32[]{:S(2)}) copy-start(bf16[512,3072]{1,0:T(8,128)(2,1)} %get-tuple-element.21) | copy-start | bytes 9437188
  227.4 49.5 %all-to-all-start.3 = ((bf16[8,64,3200]{2,1,0:T(8,128)(2,1)}), bf16[8,64,3200]{2,1,0:T(8,128)(2,1)}, u32[]{:S(2)}, u32[]{:S(2)}) async-start(bf16[8,64,3200]{2,1,0:T(8,128)(2,1)} %pad_maximum_fusion.5), calls=%async_computation.3 | async-start | bytes 6553600 | tf_op jit(solution)/shard_map/all_to_all | solution.py:42
  232.3 1.0 copy-start.4
  232.8 46.5 %copy-start.5 = (bf16[1,64,3072]{2,1,0:T(8,128)(2,1)S(1)}, bf16[1,64,3072]{2,1,0:T(8,128)(2,1)}, u32[]{:S(2)}) copy-start(bf16[1,64,3072]{2,1,0:T(8,128)(2,1)} %param.11) | copy-start | bytes 1179652
  233.5 54.0 %collective-permute-start.1 = (bf16[64,3072]{1,0:T(8,128)(2,1)S(1)}, bf16[64,3072]{1,0:T(8,128)(2,1)S(1)}, u32[]{:S(2)}, u32[]{:S(2)}) collective-permute-start(bf16[64,3072]{1,0:T(8,128)(2,1)S(1)} %get-tuple-element.19), channel_id=1, source_target_pairs={{0,248},{8,240},{16,232},{24,224},{32,216},{40,208},{48,200},{56,1... | collective-permute-start | bytes 1179656 | tf_op jit(solution)/shard_map/ppermute | solution.py:99
  240.7 46.7 %collective-permute-start = (bf16[64,3072]{1,0:T(8,128)(2,1)S(1)}, bf16[64,3072]{1,0:T(8,128)(2,1)S(1)}, u32[]{:S(2)}, u32[]{:S(2)}) collective-permute-start(bf16[64,3072]{1,0:T(8,128)(2,1)S(1)} %get-tuple-element.20), channel_id=1, source_target_pairs={{248,0},{0,8},{8,16},{16,24},{24,32},{32,40},{40,48},{48,56},{56,6... | collective-permute-start | bytes 1179656 | tf_op jit(solution)/shard_map/ppermute | solution.py:14
  281.0 15.8 %collective-permute-start.2 = (bf16[64,3072]{1,0:T(8,128)(2,1)S(1)}, bf16[64,3072]{1,0:T(8,128)(2,1)S(1)}, u32[]{:S(2)}, u32[]{:S(2)}) collective-permute-start(bf16[64,3072]{1,0:T(8,128)(2,1)S(1)} %fusion.28), channel_id=1, source_target_pairs={{8,0},{16,8},{24,16},{32,24},{40,32},{48,40},{56,48},{64,56},{72,6... | collective-permute-start | bytes 1179656 | tf_op jit(solution)/shard_map/ppermute | solution.py:14

commit v5 on v3

--- a/solution.py
+++ b/solution.py
@@ -83,27 +83,18 @@
     gain_tile = jnp.concatenate([part_hi, part_lo]).reshape(gain_rows, lanes)
     gain_tile = jnp.pad(gain_tile, ((0, rows - gain_rows), (0, 0)))
 
-    hidden = jnp.dot(joined_all, weight_all, preferred_element_type=jnp.float32)
-    update = gelu_value(hidden).astype(jnp.bfloat16)
-
-    chunks = jnp.concatenate(
+    chunks_a = jnp.concatenate(
         [
-            term.reshape(count, rows, 2 * width),
-            update.reshape(count, rows, block_cols),
+            term[:, :width].reshape(count, rows, width),
             jnp.broadcast_to(gain_tile[None], (count, rows, lanes)),
         ],
         axis=2,
     )
-    got = exchange(chunks, "tensor")
-    dfused = jnp.sum(got[:, :, : 2 * width].astype(jnp.float32), axis=0)
-    update_rows = got[:, :, 2 * width : 2 * width + block_cols].transpose(1, 0, 2).reshape(rows, width)
-    shares = got[:, :gain_rows, 2 * width + block_cols :].reshape(count, 2 * width).astype(jnp.float32)
+    chunks_a, weight_grads = lax.optimization_barrier((chunks_a, weight_grads))
+    got_a = exchange(chunks_a, "tensor")
+    dnormed = jnp.sum(got_a[:, :, :width].astype(jnp.float32), axis=0)
+    shares = got_a[:, :gain_rows, width:].reshape(count, 2 * width).astype(jnp.float32)
     gain_grad = jnp.sum(shares[:, :width] + shares[:, width:], axis=0)
-
-    out_rows = (xfloat + update_rows.astype(jnp.float32)).astype(jnp.bfloat16)
-    received = shifted(out_rows, "section", 1)
-    dnormed = dfused[:, :width]
-    dside = dfused[:, width:].astype(jnp.bfloat16)
     bfloat, brinv, _ = normalize(back_acts[0], gain)
     scaled = gain * dnormed
     dnorm_in = brinv * scaled - bfloat * brinv * brinv * brinv * jnp.mean(
@@ -111,6 +102,19 @@
     )
     dx_rows = (back_grads[0].astype(jnp.float32) + dnorm_in).astype(jnp.bfloat16)
     grad_received = shifted(dx_rows, "section", -1)
+
+    hidden = jnp.dot(joined_all, weight_all, preferred_element_type=jnp.float32)
+    update = gelu_value(hidden).astype(jnp.bfloat16)
+
+    chunks_b = jnp.concatenate(
+        [term[:, width:].reshape(count, rows, width), update.reshape(count, rows, block_cols)], axis=2
+    )
+    got_a, chunks_b = lax.optimization_barrier((got_a, chunks_b))
+    got_b2 = exchange(chunks_b, "tensor")
+    dside = jnp.sum(got_b2[:, :, :width].astype(jnp.float32), axis=0).astype(jnp.bfloat16)
+    update_rows = got_b2[:, :, width:].transpose(1, 0, 2).reshape(rows, width)
+    out_rows = (xfloat + update_rows.astype(jnp.float32)).astype(jnp.bfloat16)
+    received = shifted(out_rows, "section", 1)
     payload = jnp.where(section_idx < middle, out_rows, dside)
     mirrored = lax.ppermute(payload, "section", [(s, sections - 1 - s) for s in range(sections)])
     return (

time: 309 us -> 301 us (0.974)
  waiting for transfers between devices: 219 us -> 198 us
  starting transfers between devices: 25.5 us -> 34.4 us
  local copies, waits for them, and re-layouts: 17.1 us -> 20.2 us
    all_to_all x3 -> x4, waiting for transfers between devices: 201 us -> 173 us  [exchange(): lax.all_to_all(chunks.reshape(count * rows, cols), axis, 0, 0, tiled=True)]
    ppermute x1, waiting for transfers between devices: 11 us -> 18.9 us  [on_device(): lax.ppermute(payload, 'section', [(s, sections - 1 - s) for s in range(se...]
    ppermute x1, starting transfers between devices: 0.87 us -> 6.24 us  [on_device(): lax.ppermute(payload, 'section', [(s, sections - 1 - s) for s in range(se...]
    all_to_all x3 -> x4, starting transfers between devices: 17.1 us -> 20.2 us  [exchange(): lax.all_to_all(chunks.reshape(count * rows, cols), axis, 0, 0, tiled=True)]
    unnamed x31 -> x21, local copies, waits for them, and re-layouts: 5.68 us -> 6.65 us
  transfers between devices with their start and end apart: 6 -> 7, of which waited for: 6 -> 6; matrix products, arithmetic and copies ran while one was open for 8% -> 16% of each run, Pallas kernels for 0% -> 0%
where the time goes in v5:
time: 301 us; the launch traced here: 300 us
  waiting for transfers between devices  198 us (66%)
  starting transfers between devices  34.4 us (11%)
  matrix products  24 us (8%)
  other arithmetic  23.4 us (8%)
  local copies, waits for them, and re-layouts  20.2 us (7%)
    all_to_all x4, waiting for transfers between devices, exchange(): lax.all_to_all(chunks.reshape(count * rows, cols), axis, 0, 0, tiled=True)  173 us
    all_to_all x4, starting transfers between devices, exchange(): lax.all_to_all(chunks.reshape(count * rows, cols), axis, 0, 0, tiled=True)  20.2 us
    ppermute x1, waiting for transfers between devices, on_device(): lax.ppermute(payload, 'section', [(s, sections - 1 - s) for s in range(se...  18.9 us
    ppermute x2, starting transfers between devices, shifted(): return lax.ppermute(block, axis, route)  7.96 us
    dot_general x1, matrix products, on_device(): hidden = jnp.dot(joined_all, weight_all, preferred_element_type=jnp.float32)  7.82 us
    broadcast_in_dim x2, local copies, waits for them, and re-layouts, spread(): return jnp.broadcast_to(block[None], (count,) + block.shape)  6.79 us
    unnamed x21, local copies, waits for them, and re-layouts  6.65 us
    dot_general x1, matrix products, on_device(): lax.dot_general(bfused_all, dhidden, contract, preferred_element_type=jnp...  6.5 us
  transfers between devices with their start and end apart: 7, of which 6 were waited for; matrix products, arithmetic and copies ran while one was open for 16% of the time, Pallas kernels for 0%

profile of v5, /device:TPU:32, one launch (start us, length us, event | category | flops | bytes accessed | tf_op | source)
XLA Modules:
  0.0 300.3 jit_solution(11622819493743625441)
XLA Ops:
  2.9 3.4 %broadcast_in_dim.16 = bf16[8,64,6144]{2,1,0:T(8,128)(2,1)} broadcast(bf16[64,6144]{1,0:T(8,128)(2,1)S(1)} %pad_maximum_fusion.6), dimensions={1,2} | broadcast | bytes 7077888 | tf_op jit(solution)/shard_map/broadcast_in_dim | solution.py:37
  6.3 6.1 %pad_maximum_fusion = bf16[8,64,6528]{2,1,0:T(8,128)(2,1)} fusion(bf16[8,64,384]{2,1,0:T(8,128)(2,1)S(1)} %bitcast.67, bf16[8,64,6144]{2,1,0:T(8,128)(2,1)} %broadcast_in_dim.16), kind=kLoop, calls=%fused_computation.5 | loop fusion | flops 13369344 | bytes 13369344 | tf_op jit(solution)/shard_map/concatenate | solution.py:60
  12.4 6.7 %all-to-all-start = ((bf16[8,64,6528]{2,1,0:T(8,128)(2,1)}), bf16[8,64,6528]{2,1,0:T(8,128)(2,1)}, u32[]{:S(2)}, u32[]{:S(2)}) async-start(bf16[8,64,6528]{2,1,0:T(8,128)(2,1)} %pad_maximum_fusion), calls=%async_computation | async-start | bytes 13369344 | tf_op jit(solution)/shard_map/all_to_all | solution.py:42
  19.5 73.5 %all-to-all-done = bf16[8,64,6528]{2,1,0:T(8,128)(2,1)} async-done(((bf16[8,64,6528]{2,1,0:T(8,128)(2,1)}), bf16[8,64,6528]{2,1,0:T(8,128)(2,1)}, u32[]{:S(2)}, u32[]{:S(2)}) %all-to-all-start) | async-done | bytes 6684704 | tf_op jit(solution)/shard_map/all_to_all | solution.py:42
  93.1 3.4 %broadcast_in_dim.17 = bf16[8,64,6144]{2,1,0:T(8,128)(2,1)} broadcast(bf16[64,6144]{1,0:T(8,128)(2,1)S(1)} %pad_maximum_fusion.7), dimensions={1,2} | broadcast | bytes 7077888 | tf_op jit(solution)/shard_map/broadcast_in_dim | solution.py:37
  96.5 5.2 %all-to-all-start.2 = ((bf16[8,64,6144]{2,1,0:T(8,128)(2,1)}), bf16[8,64,6144]{2,1,0:T(8,128)(2,1)}, u32[]{:S(2)}, u32[]{:S(2)}) async-start(bf16[8,64,6144]{2,1,0:T(8,128)(2,1)} %broadcast_in_dim.17), calls=%async_computation.2 | async-start | bytes 12582912 | tf_op jit(solution)/shard_map/all_to_all | solution.py:42
  102.7 3.2 %slice.38 = bf16[8,64,6144]{2,1,0:T(8,128)(2,1)S(1)} slice(bf16[8,64,6528]{2,1,0:T(8,128)(2,1)} %all-to-all-done), slice={[0:8], [0:64], [0:6144]} | slice | bytes 12582912 | tf_op jit(solution)/shard_map/slice | solution.py:66
  108.3 3.4 %fusion.8 = f32[512,384]{1,0:T(8,128)S(1)} fusion(bf16[1,6144,384]{2,1,0:T(8,128)(2,1)S(1)} %bitcast.84, bf16[512,3072]{1,0:T(8,128)(2,1)S(1)} %slice.50, bf16[512,3072]{1,0:T(8,128)(2,1)S(1)} %fusion.2), kind=kOutput, calls=%fused_computation.16 | convolution fusion | flops 2428502016 | bytes 11796480 | tf_op jit(solution)/shard_map/dot_general | solution.py:70
  111.7 6.3 %convolution_convert_fusion = bf16[512,6144]{1,0:T(8,128)(2,1)S(1)} fusion(bf16[1,6144,384]{2,1,0:T(8,128)(2,1)} %param.10, f32[512,384]{1,0:T(8,128)S(1)} %fusion.8, bf16[512,384]{1,0:T(8,128)(2,1)S(1)} %bitcast.72), kind=kOutput, calls=%fused_computation.3 | convolution fusion | flops 2422996992 | bytes 12189696 | tf_op jit(solution)/shard_map/dot_general | solution.py:77
  119.5 2.1 fusion.66
  123.6 6.5 %convolution_convert_fusion.1 = bf16[6144,384]{1,0:T(8,128)(2,1)} fusion(bf16[512,3072]{1,0:T(8,128)(2,1)S(1)} %slice.50, bf16[512,3072]{1,0:T(8,128)(2,1)S(1)} %fusion.2, f32[512,384]{1,0:T(8,128)S(1)} %fusion.8, bf16[512,384]{1,0:T(8,128)(2,1)S(1)} %bitcast.73), kind=kOutput, calls=%fused_computation.4 | convolution fusion | flops 2434793472 | bytes 12189696 | tf_op jit(solution)/shard_map/dot_general | solution.py:73
  130.1 42.3 %all-to-all-done.2 = bf16[8,64,6144]{2,1,0:T(8,128)(2,1)} async-done(((bf16[8,64,6144]{2,1,0:T(8,128)(2,1)}), bf16[8,64,6144]{2,1,0:T(8,128)(2,1)}, u32[]{:S(2)}, u32[]{:S(2)}) %all-to-all-start.2) | async-done | bytes 6291488 | tf_op jit(solution)/shard_map/all_to_all | solution.py:42
  172.4 4.2 %all-to-all-start.1 = ((bf16[8,64,3200]{2,1,0:T(8,128)(2,1)}), bf16[8,64,3200]{2,1,0:T(8,128)(2,1)S(1)}, u32[]{:S(2)}, u32[]{:S(2)}) async-start(bf16[8,64,3200]{2,1,0:T(8,128)(2,1)} %pad_maximum_fusion.5), calls=%async_computation.1 | async-start | bytes 6553600 | tf_op jit(solution)/shard_map/all_to_all | solution.py:42
  176.6 7.8 %fusion.21 = bf16[512,384]{1,0:T(8,128)(2,1)S(1)} fusion(bf16[512,6144]{1,0:T(8,128)(2,1)} %bitcast.13, bf16[1,6144,384]{2,1,0:T(8,128)(2,1)} %param.10), kind=kOutput, calls=%fused_computation.41 | convolution fusion | flops 2417688576 | bytes 11403264 | tf_op jit(solution)/shard_map/dot_general | solution.py:106
  184.4 2.1 pad_maximum_fusion.4
  186.4 28.4 %all-to-all-done.1 = bf16[8,64,3200]{2,1,0:T(8,128)(2,1)S(1)} async-done(((bf16[8,64,3200]{2,1,0:T(8,128)(2,1)}), bf16[8,64,3200]{2,1,0:T(8,128)(2,1)S(1)}, u32[]{:S(2)}, u32[]{:S(2)}) %all-to-all-start.1) | async-done | bytes 3276832 | tf_op jit(solution)/shard_map/all_to_all | solution.py:42
  216.6 4.2 %all-to-all-start.3 = ((bf16[8,64,3456]{2,1,0:T(8,128)(2,1)}), bf16[8,64,3456]{2,1,0:T(8,128)(2,1)S(1)}, u32[]{:S(2)}, u32[]{:S(2)}) async-start(bf16[8,64,3456]{2,1,0:T(8,128)(2,1)} %pad_maximum_fusion.4), calls=%async_computation.3 | async-start | bytes 7077888 | tf_op jit(solution)/shard_map/all_to_all | solution.py:42
  220.8 2.5 convert_reduce_fusion
  224.6 2.2 fusion.28
  226.8 7.2 %collective-permute-start.2 = (bf16[64,3072]{1,0:T(8,128)(2,1)}, bf16[64,3072]{1,0:T(8,128)(2,1)}, u32[]{:S(2)}, u32[]{:S(2)}) collective-permute-start(bf16[64,3072]{1,0:T(8,128)(2,1)} %fusion.28), channel_id=1, source_target_pairs={{8,0},{16,8},{24,16},{32,24},{40,32},{48,40},{56,48},{64,56},{72,6... | collective-permute-start | bytes 1179656 | tf_op jit(solution)/shard_map/ppermute | solution.py:14
  233.9 29.2 %all-to-all-done.3 = bf16[8,64,3456]{2,1,0:T(8,128)(2,1)S(1)} async-done(((bf16[8,64,3456]{2,1,0:T(8,128)(2,1)}), bf16[8,64,3456]{2,1,0:T(8,128)(2,1)S(1)}, u32[]{:S(2)}, u32[]{:S(2)}) %all-to-all-start.3) | async-done | bytes 3538976 | tf_op jit(solution)/shard_map/all_to_all | solution.py:42
  264.3 6.2 %collective-permute-start.1 = (bf16[64,3072]{1,0:T(8,128)(2,1)S(1)}, bf16[64,3072]{1,0:T(8,128)(2,1)S(1)}, u32[]{:S(2)}, u32[]{:S(2)}) collective-permute-start(bf16[64,3072]{1,0:T(8,128)(2,1)S(1)} %get-tuple-element.17), channel_id=1, source_target_pairs={{0,248},{8,240},{16,232},{24,224},{32,216},{40,208},{48,200},{56,1... | collective-permute-start | bytes 1179656 | tf_op jit(solution)/shard_map/ppermute | solution.py:119
  273.0 18.9 %collective-permute-done.1 = bf16[64,3072]{1,0:T(8,128)(2,1)S(1)} collective-permute-done((bf16[64,3072]{1,0:T(8,128)(2,1)S(1)}, bf16[64,3072]{1,0:T(8,128)(2,1)S(1)}, u32[]{:S(2)}, u32[]{:S(2)}) %collective-permute-start.1) | collective-permute-done | bytes 393248 | tf_op jit(solution)/shard_map/ppermute | solution.py:119
  291.9 5.2 %collective-permute-done = bf16[64,3072]{1,0:T(8,128)(2,1)S(1)} collective-permute-done((bf16[64,3072]{1,0:T(8,128)(2,1)S(1)}, bf16[64,3072]{1,0:T(8,128)(2,1)S(1)}, u32[]{:S(2)}, u32[]{:S(2)}) %collective-permute-start) | collective-permute-done | bytes 393248 | tf_op jit(solution)/shard_map/ppermute | solution.py:14
  (48 shorter events, 19.3 us)
Async XLA Ops:
  12.4 6.7 %copy-start.2 = (bf16[1,64,3072]{2,1,0:T(8,128)(2,1)S(1)}, bf16[1,64,3072]{2,1,0:T(8,128)(2,1)}, u32[]{:S(2)}) copy-start(bf16[1,64,3072]{2,1,0:T(8,128)(2,1)} %param.7) | copy-start | bytes 1179652
  12.4 6.9 %copy-start.5 = (f32[1,3072]{1,0:T(1,128)S(1)}, f32[1,3072]{1,0:T(1,128)}, u32[]{:S(2)}) copy-start(f32[1,3072]{1,0:T(1,128)} %param.9) | copy-start | bytes 36868
  12.4 7.0 %copy-start.4 = (bf16[1,64,3072]{2,1,0:T(8,128)(2,1)S(1)}, bf16[1,64,3072]{2,1,0:T(8,128)(2,1)}, u32[]{:S(2)}) copy-start(bf16[1,64,3072]{2,1,0:T(8,128)(2,1)} %param.8) | copy-start | bytes 1179652
  12.4 80.6 %all-to-all-start = ((bf16[8,64,6528]{2,1,0:T(8,128)(2,1)}), bf16[8,64,6528]{2,1,0:T(8,128)(2,1)}, u32[]{:S(2)}, u32[]{:S(2)}) async-start(bf16[8,64,6528]{2,1,0:T(8,128)(2,1)} %pad_maximum_fusion), calls=%async_computation | async-start | bytes 13369344 | tf_op jit(solution)/shard_map/all_to_all | solution.py:42
  96.5 75.9 %all-to-all-start.2 = ((bf16[8,64,6144]{2,1,0:T(8,128)(2,1)}), bf16[8,64,6144]{2,1,0:T(8,128)(2,1)}, u32[]{:S(2)}, u32[]{:S(2)}) async-start(bf16[8,64,6144]{2,1,0:T(8,128)(2,1)} %broadcast_in_dim.17), calls=%async_computation.2 | async-start | bytes 12582912 | tf_op jit(solution)/shard_map/all_to_all | solution.py:42
  105.9 2.3 slice-start
  106.2 2.1 slice-start.1
  172.4 42.5 %all-to-all-start.1 = ((bf16[8,64,3200]{2,1,0:T(8,128)(2,1)}), bf16[8,64,3200]{2,1,0:T(8,128)(2,1)S(1)}, u32[]{:S(2)}, u32[]{:S(2)}) async-start(bf16[8,64,3200]{2,1,0:T(8,128)(2,1)} %pad_maximum_fusion.5), calls=%async_computation.1 | async-start | bytes 6553600 | tf_op jit(solution)/shard_map/all_to_all | solution.py:42
  176.6 7.8 %copy-start.1 = (bf16[512,3072]{1,0:T(8,128)(2,1)S(1)}, bf16[512,3072]{1,0:T(8,128)(2,1)}, u32[]{:S(2)}) copy-start(bf16[512,3072]{1,0:T(8,128)(2,1)} %get-tuple-element.21) | copy-start | bytes 9437188
  214.8 1.7 copy-start
  216.6 46.6 %all-to-all-start.3 = ((bf16[8,64,3456]{2,1,0:T(8,128)(2,1)}), bf16[8,64,3456]{2,1,0:T(8,128)(2,1)S(1)}, u32[]{:S(2)}, u32[]{:S(2)}) async-start(bf16[8,64,3456]{2,1,0:T(8,128)(2,1)} %pad_maximum_fusion.4), calls=%async_computation.3 | async-start | bytes 7077888 | tf_op jit(solution)/shard_map/all_to_all | solution.py:42
  226.8 46.2 %collective-permute-start.2 = (bf16[64,3072]{1,0:T(8,128)(2,1)}, bf16[64,3072]{1,0:T(8,128)(2,1)}, u32[]{:S(2)}, u32[]{:S(2)}) collective-permute-start(bf16[64,3072]{1,0:T(8,128)(2,1)} %fusion.28), channel_id=1, source_target_pairs={{8,0},{16,8},{24,16},{32,24},{40,32},{48,40},{56,48},{64,56},{72,6... | collective-permute-start | bytes 1179656 | tf_op jit(solution)/shard_map/ppermute | solution.py:14
  263.2 1.0 copy-start.3
  264.3 27.6 %collective-permute-start.1 = (bf16[64,3072]{1,0:T(8,128)(2,1)S(1)}, bf16[64,3072]{1,0:T(8,128)(2,1)S(1)}, u32[]{:S(2)}, u32[]{:S(2)}) collective-permute-start(bf16[64,3072]{1,0:T(8,128)(2,1)S(1)} %get-tuple-element.17), channel_id=1, source_target_pairs={{0,248},{8,240},{16,232},{24,224},{32,216},{40,208},{48,200},{56,1... | collective-permute-start | bytes 1179656 | tf_op jit(solution)/shard_map/ppermute | solution.py:119
  270.5 26.5 %collective-permute-start = (bf16[64,3072]{1,0:T(8,128)(2,1)S(1)}, bf16[64,3072]{1,0:T(8,128)(2,1)S(1)}, u32[]{:S(2)}, u32[]{:S(2)}) collective-permute-start(bf16[64,3072]{1,0:T(8,128)(2,1)S(1)} %get-tuple-element.18), channel_id=1, source_target_pairs={{248,0},{0,8},{8,16},{16,24},{24,32},{32,40},{40,48},{48,56},{56,6... | collective-permute-start | bytes 1179656 | tf_op jit(solution)/shard_map/ppermute | solution.py:14

commit v6 on v5

--- a/solution.py
+++ b/solution.py
@@ -33,8 +33,9 @@
     return (xfloat, rinv, (xfloat * rinv * gain).astype(jnp.bfloat16))
 
 
-def spread(block, count):
-    return jnp.broadcast_to(block[None], (count,) + block.shape)
+def spread(pieces):
+    block = jnp.concatenate(pieces, axis=1)
+    return jnp.broadcast_to(block[None], (lax.axis_size("tensor"),) + block.shape)
 
 
 def exchange(chunks, axis):
@@ -55,11 +56,15 @@
     lanes = 128
     gain_rows = 2 * width // lanes
 
+    keep = lax.broadcasted_iota(jnp.int32, (count, 1, 1), 0) + section_idx >= 0
     grad_blocks = back_grads[0].reshape(rows, count, block_cols).transpose(1, 0, 2)
-    raw = jnp.concatenate([back_acts[0], back_sides[0]], axis=1)
-    got_b = exchange(jnp.concatenate([spread(raw, count), grad_blocks], axis=2), "tensor")
+    grad_blocks = jnp.pad(grad_blocks, ((0, 0), (0, 0), (2 * width, 0)))
+    raw_pad = jnp.zeros((rows, block_cols), jnp.bfloat16)
+    is_raw = lax.broadcasted_iota(jnp.int32, (1, 1, 2 * width + block_cols), 2) < 2 * width + 0 * section_idx
+    chunks_b = jnp.where(is_raw, spread([back_acts[0], back_sides[0], raw_pad]), grad_blocks)
+    got_b = exchange(chunks_b, "tensor")
     xfloat, _, normed = normalize(acts[0], gain)
-    chunks_f = spread(jnp.concatenate([normed, sides[0]], axis=1), count)
+    chunks_f = jnp.where(keep, spread([normed, sides[0]]), jnp.zeros((), jnp.bfloat16))
     got_b, chunks_f = lax.optimization_barrier((got_b, chunks_f))
     joined_all = exchange(chunks_f, "tensor").reshape(count * rows, 2 * width)
 

time: 301 us -> 292 us (0.970)
  local copies, waits for them, and re-layouts: 20.2 us -> 13.4 us
    broadcast_in_dim x2 -> x1, local copies, waits for them, and re-layouts: 6.79 us -> 0.01 us  [on_device(): raw_pad = jnp.zeros((rows, block_cols), jnp.bfloat16)]
    select_n x0 -> x2, other arithmetic: none -> 6.51 us  [the longest x1 3.33 us: on_device(): jnp.where(is_raw, spread([back_acts[0], back_sides[0], raw_pad]), grad_bl...]
    concatenate x3 -> x2, other arithmetic: 7.36 us -> 1.31 us  [spread(): block = jnp.concatenate(pieces, axis=1)]
    unnamed x21 -> x25, local copies, waits for them, and re-layouts: 6.65 us -> 6.67 us
  transfers between devices with their start and end apart: 7 -> 7, of which waited for: 6 -> 6; matrix products, arithmetic and copies ran while one was open for 16% -> 17% of each run, Pallas kernels for 0% -> 0%
where the time goes in v6:
time: 292 us; the launch traced here: 291 us
  waiting for transfers between devices  195 us (67%)
  starting transfers between devices  34.3 us (12%)
  matrix products  24 us (8%)
  other arithmetic  22.9 us (8%)
  local copies, waits for them, and re-layouts  13.4 us (5%)
    all_to_all x4, waiting for transfers between devices, exchange(): lax.all_to_all(chunks.reshape(count * rows, cols), axis, 0, 0, tiled=True)  171 us
    all_to_all x4, starting transfers between devices, exchange(): lax.all_to_all(chunks.reshape(count * rows, cols), axis, 0, 0, tiled=True)  20.2 us
    ppermute x1, waiting for transfers between devices, on_device(): lax.ppermute(payload, 'section', [(s, sections - 1 - s) for s in range(se...  18.9 us
    ppermute x2, starting transfers between devices, shifted(): return lax.ppermute(block, axis, route)  7.92 us
    dot_general x1, matrix products, on_device(): hidden = jnp.dot(joined_all, weight_all, preferred_element_type=jnp.float32)  7.82 us
    unnamed x25, local copies, waits for them, and re-layouts  6.67 us
    dot_general x1, matrix products, on_device(): lax.dot_general(bfused_all, dhidden, contract, preferred_element_type=jnp...  6.5 us
    dot_general x1, matrix products, on_device(): lax.dot_general(dhidden, weight_all, across, preferred_element_type=jnp.f...  6.25 us
  transfers between devices with their start and end apart: 7, of which 6 were waited for; matrix products, arithmetic and copies ran while one was open for 17% of the time, Pallas kernels for 0%

profile of v6, /device:TPU:32, one launch (start us, length us, event | category | flops | bytes accessed | tf_op | source)
XLA Modules:
  0.0 290.8 jit_solution(4387298660775127184)
XLA Ops:
  3.0 3.3 %pad_select_fusion = bf16[8,64,6528]{2,1,0:T(8,128)(2,1)} fusion(bf16[8,64,384]{2,1,0:T(8,128)(2,1)S(1)} %bitcast.67, pred[6528]{0:T(1024)(128)(4,1)S(1)} %iota_compare_fusion.1, bf16[64,6528]{1,0:T(8,128)(2,1)S(1)} %maximum_maximum_fusion), kind=kLoop, calls=%fused_computation.5 | loop fusion | flops 3342336 | bytes 7920000 | tf_op jit(solution)/shard_map/jit(_where)/select_n | solution.py:64
  6.4 6.6 %all-to-all-start = ((bf16[8,64,6528]{2,1,0:T(8,128)(2,1)}), bf16[8,64,6528]{2,1,0:T(8,128)(2,1)}, u32[]{:S(2)}, u32[]{:S(2)}) async-start(bf16[8,64,6528]{2,1,0:T(8,128)(2,1)} %pad_select_fusion), calls=%async_computation | async-start | bytes 13369344 | tf_op jit(solution)/shard_map/all_to_all | solution.py:43
  13.5 3.2 %broadcast_select_fusion = bf16[8,64,6144]{2,1,0:T(8,128)(2,1)} fusion(pred[8]{0:T(512)(128)(4,1)S(1)} %add_compare_fusion, bf16[64,6144]{1,0:T(8,128)(2,1)S(1)} %pad_maximum_fusion.5), kind=kLoop, calls=%fused_computation.13 | loop fusion | flops 3145728 | bytes 7077896 | tf_op jit(solution)/shard_map/jit(_where)/select_n | solution.py:67
  16.6 70.4 %all-to-all-done = bf16[8,64,6528]{2,1,0:T(8,128)(2,1)} async-done(((bf16[8,64,6528]{2,1,0:T(8,128)(2,1)}), bf16[8,64,6528]{2,1,0:T(8,128)(2,1)}, u32[]{:S(2)}, u32[]{:S(2)}) %all-to-all-start) | async-done | bytes 6684704 | tf_op jit(solution)/shard_map/all_to_all | solution.py:43
  87.0 5.2 %all-to-all-start.2 = ((bf16[8,64,6144]{2,1,0:T(8,128)(2,1)}), bf16[8,64,6144]{2,1,0:T(8,128)(2,1)}, u32[]{:S(2)}, u32[]{:S(2)}) async-start(bf16[8,64,6144]{2,1,0:T(8,128)(2,1)} %broadcast_select_fusion), calls=%async_computation.2 | async-start | bytes 12582912 | tf_op jit(solution)/shard_map/all_to_all | solution.py:43
  93.3 3.2 %slice.38 = bf16[8,64,6144]{2,1,0:T(8,128)(2,1)S(1)} slice(bf16[8,64,6528]{2,1,0:T(8,128)(2,1)} %all-to-all-done), slice={[0:8], [0:64], [0:6144]} | slice | bytes 12582912 | tf_op jit(solution)/shard_map/slice | solution.py:71
  98.8 3.4 %fusion.8 = f32[512,384]{1,0:T(8,128)S(1)} fusion(bf16[1,6144,384]{2,1,0:T(8,128)(2,1)S(1)} %bitcast.84, bf16[512,3072]{1,0:T(8,128)(2,1)S(1)} %slice.50, bf16[512,3072]{1,0:T(8,128)(2,1)S(1)} %fusion.2), kind=kOutput, calls=%fused_computation.17 | convolution fusion | flops 2428502016 | bytes 11796480 | tf_op jit(solution)/shard_map/dot_general | solution.py:75
  102.3 6.3 %convolution_convert_fusion = bf16[512,6144]{1,0:T(8,128)(2,1)S(1)} fusion(bf16[1,6144,384]{2,1,0:T(8,128)(2,1)} %param.10, f32[512,384]{1,0:T(8,128)S(1)} %fusion.8, bf16[512,384]{1,0:T(8,128)(2,1)S(1)} %bitcast.72), kind=kOutput, calls=%fused_computation.3 | convolution fusion | flops 2422996992 | bytes 12189696 | tf_op jit(solution)/shard_map/dot_general | solution.py:82
  110.0 2.1 fusion.66
  112.2 2.0 pad_maximum_fusion.4
  114.2 6.5 %convolution_convert_fusion.1 = bf16[6144,384]{1,0:T(8,128)(2,1)} fusion(bf16[512,3072]{1,0:T(8,128)(2,1)S(1)} %slice.50, bf16[512,3072]{1,0:T(8,128)(2,1)S(1)} %fusion.2, f32[512,384]{1,0:T(8,128)S(1)} %fusion.8, bf16[512,384]{1,0:T(8,128)(2,1)S(1)} %bitcast.73), kind=kOutput, calls=%fused_computation.4 | convolution fusion | flops 2434793472 | bytes 12189696 | tf_op jit(solution)/shard_map/dot_general | solution.py:78
  120.7 42.2 %all-to-all-done.2 = bf16[8,64,6144]{2,1,0:T(8,128)(2,1)} async-done(((bf16[8,64,6144]{2,1,0:T(8,128)(2,1)}), bf16[8,64,6144]{2,1,0:T(8,128)(2,1)}, u32[]{:S(2)}, u32[]{:S(2)}) %all-to-all-start.2) | async-done | bytes 6291488 | tf_op jit(solution)/shard_map/all_to_all | solution.py:43
  162.9 4.2 %all-to-all-start.1 = ((bf16[8,64,3200]{2,1,0:T(8,128)(2,1)}), bf16[8,64,3200]{2,1,0:T(8,128)(2,1)S(1)}, u32[]{:S(2)}, u32[]{:S(2)}) async-start(bf16[8,64,3200]{2,1,0:T(8,128)(2,1)} %pad_maximum_fusion.4), calls=%async_computation.1 | async-start | bytes 6553600 | tf_op jit(solution)/shard_map/all_to_all | solution.py:43
  167.1 7.8 %fusion.21 = bf16[512,384]{1,0:T(8,128)(2,1)S(1)} fusion(bf16[512,6144]{1,0:T(8,128)(2,1)} %bitcast.13, bf16[1,6144,384]{2,1,0:T(8,128)(2,1)} %param.10), kind=kOutput, calls=%fused_computation.43 | convolution fusion | flops 2417688576 | bytes 11403264 | tf_op jit(solution)/shard_map/dot_general | solution.py:111
  174.9 2.1 pad_maximum_fusion.3
  177.0 28.4 %all-to-all-done.1 = bf16[8,64,3200]{2,1,0:T(8,128)(2,1)S(1)} async-done(((bf16[8,64,3200]{2,1,0:T(8,128)(2,1)}), bf16[8,64,3200]{2,1,0:T(8,128)(2,1)S(1)}, u32[]{:S(2)}, u32[]{:S(2)}) %all-to-all-start.1) | async-done | bytes 3276832 | tf_op jit(solution)/shard_map/all_to_all | solution.py:43
  207.1 4.2 %all-to-all-start.3 = ((bf16[8,64,3456]{2,1,0:T(8,128)(2,1)}), bf16[8,64,3456]{2,1,0:T(8,128)(2,1)S(1)}, u32[]{:S(2)}, u32[]{:S(2)}) async-start(bf16[8,64,3456]{2,1,0:T(8,128)(2,1)} %pad_maximum_fusion.3), calls=%async_computation.3 | async-start | bytes 7077888 | tf_op jit(solution)/shard_map/all_to_all | solution.py:43
  211.3 2.6 convert_reduce_fusion
  216.3 7.1 %collective-permute-start.2 = (bf16[64,3072]{1,0:T(8,128)(2,1)}, bf16[64,3072]{1,0:T(8,128)(2,1)}, u32[]{:S(2)}, u32[]{:S(2)}) collective-permute-start(bf16[64,3072]{1,0:T(8,128)(2,1)} %fusion.28), channel_id=1, source_target_pairs={{8,0},{16,8},{24,16},{32,24},{40,32},{48,40},{56,48},{64,56},{72,6... | collective-permute-start | bytes 1179656 | tf_op jit(solution)/shard_map/ppermute | solution.py:14
  223.4 30.3 %all-to-all-done.3 = bf16[8,64,3456]{2,1,0:T(8,128)(2,1)S(1)} async-done(((bf16[8,64,3456]{2,1,0:T(8,128)(2,1)}), bf16[8,64,3456]{2,1,0:T(8,128)(2,1)S(1)}, u32[]{:S(2)}, u32[]{:S(2)}) %all-to-all-start.3) | async-done | bytes 3538976 | tf_op jit(solution)/shard_map/all_to_all | solution.py:43
  254.8 6.2 %collective-permute-start.1 = (bf16[64,3072]{1,0:T(8,128)(2,1)S(1)}, bf16[64,3072]{1,0:T(8,128)(2,1)S(1)}, u32[]{:S(2)}, u32[]{:S(2)}) collective-permute-start(bf16[64,3072]{1,0:T(8,128)(2,1)S(1)} %get-tuple-element.17), channel_id=1, source_target_pairs={{0,248},{8,240},{16,232},{24,224},{32,216},{40,208},{48,200},{56,1... | collective-permute-start | bytes 1179656 | tf_op jit(solution)/shard_map/ppermute | solution.py:124
  263.5 18.9 %collective-permute-done.1 = bf16[64,3072]{1,0:T(8,128)(2,1)S(1)} collective-permute-done((bf16[64,3072]{1,0:T(8,128)(2,1)S(1)}, bf16[64,3072]{1,0:T(8,128)(2,1)S(1)}, u32[]{:S(2)}, u32[]{:S(2)}) %collective-permute-start.1) | collective-permute-done | bytes 393248 | tf_op jit(solution)/shard_map/ppermute | solution.py:124
  282.4 5.2 %collective-permute-done = bf16[64,3072]{1,0:T(8,128)(2,1)S(1)} collective-permute-done((bf16[64,3072]{1,0:T(8,128)(2,1)S(1)}, bf16[64,3072]{1,0:T(8,128)(2,1)S(1)}, u32[]{:S(2)}, u32[]{:S(2)}) %collective-permute-start) | collective-permute-done | bytes 393248 | tf_op jit(solution)/shard_map/ppermute | solution.py:14
  289.1 1.8 copy.26
  (55 shorter events, 16.8 us)
Async XLA Ops:
  6.4 6.6 %copy-start.3 = (bf16[1,64,3072]{2,1,0:T(8,128)(2,1)S(1)}, bf16[1,64,3072]{2,1,0:T(8,128)(2,1)}, u32[]{:S(2)}) copy-start(bf16[1,64,3072]{2,1,0:T(8,128)(2,1)} %param.7) | copy-start | bytes 1179652
  6.4 6.8 %copy-start.7 = (f32[1,3072]{1,0:T(1,128)S(1)}, f32[1,3072]{1,0:T(1,128)}, u32[]{:S(2)}) copy-start(f32[1,3072]{1,0:T(1,128)} %param.9) | copy-start | bytes 36868
  6.4 7.0 %copy-start.6 = (bf16[1,64,3072]{2,1,0:T(8,128)(2,1)S(1)}, bf16[1,64,3072]{2,1,0:T(8,128)(2,1)}, u32[]{:S(2)}) copy-start(bf16[1,64,3072]{2,1,0:T(8,128)(2,1)} %param.8) | copy-start | bytes 1179652
  6.4 80.6 %all-to-all-start = ((bf16[8,64,6528]{2,1,0:T(8,128)(2,1)}), bf16[8,64,6528]{2,1,0:T(8,128)(2,1)}, u32[]{:S(2)}, u32[]{:S(2)}) async-start(bf16[8,64,6528]{2,1,0:T(8,128)(2,1)} %pad_select_fusion), calls=%async_computation | async-start | bytes 13369344 | tf_op jit(solution)/shard_map/all_to_all | solution.py:43
  87.0 75.9 %all-to-all-start.2 = ((bf16[8,64,6144]{2,1,0:T(8,128)(2,1)}), bf16[8,64,6144]{2,1,0:T(8,128)(2,1)}, u32[]{:S(2)}, u32[]{:S(2)}) async-start(bf16[8,64,6144]{2,1,0:T(8,128)(2,1)} %broadcast_select_fusion), calls=%async_computation.2 | async-start | bytes 12582912 | tf_op jit(solution)/shard_map/all_to_all | solution.py:43
  96.5 2.3 slice-start
  96.8 2.1 slice-start.1
  162.9 42.5 %all-to-all-start.1 = ((bf16[8,64,3200]{2,1,0:T(8,128)(2,1)}), bf16[8,64,3200]{2,1,0:T(8,128)(2,1)S(1)}, u32[]{:S(2)}, u32[]{:S(2)}) async-start(bf16[8,64,3200]{2,1,0:T(8,128)(2,1)} %pad_maximum_fusion.4), calls=%async_computation.1 | async-start | bytes 6553600 | tf_op jit(solution)/shard_map/all_to_all | solution.py:43
  167.1 7.8 %copy-start.1 = (bf16[512,3072]{1,0:T(8,128)(2,1)S(1)}, bf16[512,3072]{1,0:T(8,128)(2,1)}, u32[]{:S(2)}) copy-start(bf16[512,3072]{1,0:T(8,128)(2,1)} %get-tuple-element.21) | copy-start | bytes 9437188
  205.4 1.7 copy-start
  207.1 46.6 %all-to-all-start.3 = ((bf16[8,64,3456]{2,1,0:T(8,128)(2,1)}), bf16[8,64,3456]{2,1,0:T(8,128)(2,1)S(1)}, u32[]{:S(2)}, u32[]{:S(2)}) async-start(bf16[8,64,3456]{2,1,0:T(8,128)(2,1)} %pad_maximum_fusion.3), calls=%async_computation.3 | async-start | bytes 7077888 | tf_op jit(solution)/shard_map/all_to_all | solution.py:43
  211.3 3.9 %copy-start.2 = (bf16[1,64,3072]{2,1,0:T(8,128)(2,1)S(1)}, bf16[1,64,3072]{2,1,0:T(8,128)(2,1)}, u32[]{:S(2)}) copy-start(bf16[1,64,3072]{2,1,0:T(8,128)(2,1)} %param.11) | copy-start | bytes 1179652
  211.3 3.9 %copy-start.5 = (bf16[1,64,3072]{2,1,0:T(8,128)(2,1)S(1)}, bf16[1,64,3072]{2,1,0:T(8,128)(2,1)}, u32[]{:S(2)}) copy-start(bf16[1,64,3072]{2,1,0:T(8,128)(2,1)} %param.13) | copy-start | bytes 1179652
  216.3 47.2 %collective-permute-start.2 = (bf16[64,3072]{1,0:T(8,128)(2,1)}, bf16[64,3072]{1,0:T(8,128)(2,1)}, u32[]{:S(2)}, u32[]{:S(2)}) collective-permute-start(bf16[64,3072]{1,0:T(8,128)(2,1)} %fusion.28), channel_id=1, source_target_pairs={{8,0},{16,8},{24,16},{32,24},{40,32},{48,40},{56,48},{64,56},{72,6... | collective-permute-start | bytes 1179656 | tf_op jit(solution)/shard_map/ppermute | solution.py:14
  253.7 1.0 copy-start.4
  254.8 27.5 %collective-permute-start.1 = (bf16[64,3072]{1,0:T(8,128)(2,1)S(1)}, bf16[64,3072]{1,0:T(8,128)(2,1)S(1)}, u32[]{:S(2)}, u32[]{:S(2)}) collective-permute-start(bf16[64,3072]{1,0:T(8,128)(2,1)S(1)} %get-tuple-element.17), channel_id=1, source_target_pairs={{0,248},{8,240},{16,232},{24,224},{32,216},{40,208},{48,200},{56,1... | collective-permute-start | bytes 1179656 | tf_op jit(solution)/shard_map/ppermute | solution.py:124
  261.0 26.5 %collective-permute-start = (bf16[64,3072]{1,0:T(8,128)(2,1)S(1)}, bf16[64,3072]{1,0:T(8,128)(2,1)S(1)}, u32[]{:S(2)}, u32[]{:S(2)}) collective-permute-start(bf16[64,3072]{1,0:T(8,128)(2,1)S(1)} %get-tuple-element.18), channel_id=1, source_target_pairs={{248,0},{0,8},{8,16},{16,24},{24,32},{32,40},{40,48},{48,56},{56,6... | collective-permute-start | bytes 1179656 | tf_op jit(solution)/shard_map/ppermute | solution.py:14

commit v7 on v6

--- a/solution.py
+++ b/solution.py
@@ -75,9 +75,6 @@
     bhidden = jnp.dot(bfused_all, weight_all, preferred_element_type=jnp.float32)
     dhidden = (grad_cols.astype(jnp.float32) * gelu_slope(bhidden)).astype(jnp.bfloat16)
     contract = (((0,), (0,)), ((), ()))
-    weight_grads = lax.dot_general(
-        bfused_all, dhidden, contract, preferred_element_type=jnp.float32
-    ).astype(jnp.bfloat16)
     across = (((1,), (1,)), ((), ()))
     term = lax.dot_general(
         dhidden, weight_all, across, preferred_element_type=jnp.float32
@@ -95,7 +92,6 @@
         ],
         axis=2,
     )
-    chunks_a, weight_grads = lax.optimization_barrier((chunks_a, weight_grads))
     got_a = exchange(chunks_a, "tensor")
     dnormed = jnp.sum(got_a[:, :, :width].astype(jnp.float32), axis=0)
     shares = got_a[:, :gain_rows, width:].reshape(count, 2 * width).astype(jnp.float32)
@@ -122,6 +118,10 @@
     received = shifted(out_rows, "section", 1)
     payload = jnp.where(section_idx < middle, out_rows, dside)
     mirrored = lax.ppermute(payload, "section", [(s, sections - 1 - s) for s in range(sections)])
+    got_b2, bfused_all, dhidden = lax.optimization_barrier((got_b2, bfused_all, dhidden))
+    weight_grads = lax.dot_general(
+        bfused_all, dhidden, contract, preferred_element_type=jnp.float32
+    ).astype(jnp.bfloat16)
     return (
         received[None],
         mirrored[None],

time: 292 us -> 292 us (level)
  other arithmetic: 22.9 us -> 28 us
    ppermute x2, waiting for transfers between devices: 5.19 us -> 33.1 us  [shifted(): return lax.ppermute(block, axis, route)]
    all_to_all x4, waiting for transfers between devices: 171 us -> 147 us  [exchange(): lax.all_to_all(chunks.reshape(count * rows, cols), axis, 0, 0, tiled=True)]
    ppermute x1, waiting for transfers between devices: 18.9 us -> 13.2 us  [on_device(): lax.ppermute(payload, 'section', [(s, sections - 1 - s) for s in range(se...]
    concatenate x0 -> x1, other arithmetic: none -> 3.25 us  [on_device(): bfused_all = jnp.concatenate([bnormed_all, raw_all[:, width:]], axis=1)]
    unnamed x25 -> x35, local copies, waits for them, and re-layouts: 6.67 us -> 6.98 us
where the time goes in v7:
time: 292 us
  waiting for transfers between devices  194 us (66%)
  starting transfers between devices  33.7 us (12%)
  other arithmetic  28 us (10%)
  matrix products  21.7 us (7%)
  local copies, waits for them, and re-layouts  13.7 us (5%)
    all_to_all x4, waiting for transfers between devices, exchange(): lax.all_to_all(chunks.reshape(count * rows, cols), axis, 0, 0, tiled=True)  147 us
    ppermute x2, waiting for transfers between devices, shifted(): return lax.ppermute(block, axis, route)  33.1 us
    all_to_all x4, starting transfers between devices, exchange(): lax.all_to_all(chunks.reshape(count * rows, cols), axis, 0, 0, tiled=True)  20.2 us
    ppermute x1, waiting for transfers between devices, on_device(): lax.ppermute(payload, 'section', [(s, sections - 1 - s) for s in range(se...  13.2 us
    dot_general x1, matrix products, on_device(): hidden = jnp.dot(joined_all, weight_all, preferred_element_type=jnp.float32)  7.82 us
    ppermute x2, starting transfers between devices, shifted(): return lax.ppermute(block, axis, route)  7.21 us
    unnamed x35, local copies, waits for them, and re-layouts  6.98 us
    ppermute x1, starting transfers between devices, on_device(): lax.ppermute(payload, 'section', [(s, sections - 1 - s) for s in range(se...  6.21 us
  transfers between devices with their start and end apart: 7, of which 6 were waited for; matrix products, arithmetic and copies ran while one was open for 17% of the time, Pallas kernels for 0%

profile of v7, /device:TPU:32, one launch (start us, length us, event | category | flops | bytes accessed | tf_op | source)
XLA Modules:
  0.0 291.5 jit_solution(3934697613847327497)
XLA Ops:
  3.0 3.3 %pad_select_fusion = bf16[8,64,6528]{2,1,0:T(8,128)(2,1)} fusion(bf16[8,64,384]{2,1,0:T(8,128)(2,1)S(1)} %bitcast.73, pred[6528]{0:T(1024)(128)(4,1)S(1)} %iota_compare_fusion.1, bf16[64,6528]{1,0:T(8,128)(2,1)S(1)} %maximum_maximum_fusion), kind=kLoop, calls=%fused_computation.6 | loop fusion | flops 3342336 | bytes 7920000 | tf_op jit(solution)/shard_map/jit(_where)/select_n | solution.py:64
  6.3 6.6 %all-to-all-start = ((bf16[8,64,6528]{2,1,0:T(8,128)(2,1)}), bf16[8,64,6528]{2,1,0:T(8,128)(2,1)}, u32[]{:S(2)}, u32[]{:S(2)}) async-start(bf16[8,64,6528]{2,1,0:T(8,128)(2,1)} %pad_select_fusion), calls=%async_computation | async-start | bytes 13369344 | tf_op jit(solution)/shard_map/all_to_all | solution.py:43
  13.4 3.2 %broadcast_select_fusion = bf16[8,64,6144]{2,1,0:T(8,128)(2,1)} fusion(pred[8]{0:T(512)(128)(4,1)S(1)} %add_compare_fusion, bf16[64,6144]{1,0:T(8,128)(2,1)S(1)} %pad_maximum_fusion.3), kind=kLoop, calls=%fused_computation.14 | loop fusion | flops 3145728 | bytes 7077896 | tf_op jit(solution)/shard_map/jit(_where)/select_n | solution.py:67
  16.7 70.3 %all-to-all-done = bf16[8,64,6528]{2,1,0:T(8,128)(2,1)} async-done(((bf16[8,64,6528]{2,1,0:T(8,128)(2,1)}), bf16[8,64,6528]{2,1,0:T(8,128)(2,1)}, u32[]{:S(2)}, u32[]{:S(2)}) %all-to-all-start) | async-done | bytes 6684704 | tf_op jit(solution)/shard_map/all_to_all | solution.py:43
  87.0 5.3 %all-to-all-start.2 = ((bf16[8,64,6144]{2,1,0:T(8,128)(2,1)}), bf16[8,64,6144]{2,1,0:T(8,128)(2,1)}, u32[]{:S(2)}, u32[]{:S(2)}) async-start(bf16[8,64,6144]{2,1,0:T(8,128)(2,1)} %broadcast_select_fusion), calls=%async_computation.2 | async-start | bytes 12582912 | tf_op jit(solution)/shard_map/all_to_all | solution.py:43
  93.3 3.2 %slice.38 = bf16[8,64,6144]{2,1,0:T(8,128)(2,1)S(1)} slice(bf16[8,64,6528]{2,1,0:T(8,128)(2,1)} %all-to-all-done), slice={[0:8], [0:64], [0:6144]} | slice | bytes 12582912 | tf_op jit(solution)/shard_map/slice | solution.py:71
  99.9 4.6 %fusion.17 = (bf16[512,384]{1,0:T(8,128)(2,1)}, f32[512,384]{1,0:T(8,128)S(1)}) fusion(bf16[8,64,384]{2,1,0:T(8,128)(2,1)S(1)} %slice.37, bf16[1,6144,384]{2,1,0:T(8,128)(2,1)S(1)} %bitcast.90, bf16[512,3072]{1,0:T(8,128)(2,1)S(1)} %slice.50, bf16[512,3072]{1,0:T(8,128)(2,1)S(1)} %fusion.3), kind=kOutput, calls=%fused_computation.39 | convolution fusion | flops 2432434176 | bytes 12582912 | tf_op jit(solution)/shard_map/dot_general | solution.py:75
  104.5 4.1 %convolution_convert_fusion = bf16[512,6144]{1,0:T(8,128)(2,1)S(1)} fusion(bf16[1,6144,384]{2,1,0:T(8,128)(2,1)S(1)} %bitcast.90, f32[512,384]{1,0:T(8,128)S(1)} %get-tuple-element.24, bf16[512,384]{1,0:T(8,128)(2,1)S(1)} %bitcast.81), kind=kOutput, calls=%fused_computation.3 | convolution fusion | flops 2422996992 | bytes 12189696 | tf_op jit(solution)/shard_map/dot_general | solution.py:79
  110.2 2.1 fusion.54
  112.3 2.0 pad_maximum_fusion.2
  114.3 48.6 %all-to-all-done.2 = bf16[8,64,6144]{2,1,0:T(8,128)(2,1)} async-done(((bf16[8,64,6144]{2,1,0:T(8,128)(2,1)}), bf16[8,64,6144]{2,1,0:T(8,128)(2,1)}, u32[]{:S(2)}, u32[]{:S(2)}) %all-to-all-start.2) | async-done | bytes 6291488 | tf_op jit(solution)/shard_map/all_to_all | solution.py:43
  162.9 4.2 %all-to-all-start.1 = ((bf16[8,64,3200]{2,1,0:T(8,128)(2,1)}), bf16[8,64,3200]{2,1,0:T(8,128)(2,1)S(1)}, u32[]{:S(2)}, u32[]{:S(2)}) async-start(bf16[8,64,3200]{2,1,0:T(8,128)(2,1)} %pad_maximum_fusion.2), calls=%async_computation.1 | async-start | bytes 6553600 | tf_op jit(solution)/shard_map/all_to_all | solution.py:43
  167.1 7.8 %fusion.22 = bf16[512,384]{1,0:T(8,128)(2,1)S(1)} fusion(bf16[512,6144]{1,0:T(8,128)(2,1)} %bitcast.13, bf16[1,6144,384]{2,1,0:T(8,128)(2,1)} %param.10), kind=kOutput, calls=%fused_computation.44 | convolution fusion | flops 2417688576 | bytes 11403264 | tf_op jit(solution)/shard_map/dot_general | solution.py:107
  174.9 2.1 pad_maximum_fusion.1
  177.0 28.4 %all-to-all-done.1 = bf16[8,64,3200]{2,1,0:T(8,128)(2,1)S(1)} async-done(((bf16[8,64,3200]{2,1,0:T(8,128)(2,1)}), bf16[8,64,3200]{2,1,0:T(8,128)(2,1)S(1)}, u32[]{:S(2)}, u32[]{:S(2)}) %all-to-all-start.1) | async-done | bytes 3276832 | tf_op jit(solution)/shard_map/all_to_all | solution.py:43
  207.1 4.2 %all-to-all-start.3 = ((bf16[8,64,3456]{2,1,0:T(8,128)(2,1)}), bf16[8,64,3456]{2,1,0:T(8,128)(2,1)S(1)}, u32[]{:S(2)}, u32[]{:S(2)}) async-start(bf16[8,64,3456]{2,1,0:T(8,128)(2,1)} %pad_maximum_fusion.1), calls=%async_computation.3 | async-start | bytes 7077888 | tf_op jit(solution)/shard_map/all_to_all | solution.py:43
  211.3 2.6 convert_reduce_fusion
  216.8 7.2 %collective-permute-start.2 = (bf16[64,3072]{1,0:T(8,128)(2,1)S(1)}, bf16[64,3072]{1,0:T(8,128)(2,1)S(1)}, u32[]{:S(2)}, u32[]{:S(2)}) collective-permute-start(bf16[64,3072]{1,0:T(8,128)(2,1)S(1)} %fusion.29), channel_id=1, source_target_pairs={{8,0},{16,8},{24,16},{32,24},{40,32},{48,40},{56,48},{64,56},{72,6... | collective-permute-start | bytes 1179656 | tf_op jit(solution)/shard_map/ppermute | solution.py:14
  224.0 3.2 %pad_maximum_fusion = bf16[512,6144]{1,0:T(8,128)(2,1)} fusion(bf16[512,3072]{1,0:T(8,128)(2,1)S(1)} %copy-done.3, bf16[512,3072]{1,0:T(8,128)(2,1)S(1)} %copy-done.5), kind=kLoop, calls=%fused_computation.12 | loop fusion | flops 12582912 | bytes 12582912 | tf_op jit(solution)/shard_map/concatenate | solution.py:74
  228.9 28.9 %collective-permute-done.2 = bf16[64,3072]{1,0:T(8,128)(2,1)S(1)} collective-permute-done((bf16[64,3072]{1,0:T(8,128)(2,1)S(1)}, bf16[64,3072]{1,0:T(8,128)(2,1)S(1)}, u32[]{:S(2)}, u32[]{:S(2)}) %collective-permute-start.2) | collective-permute-done | bytes 393248 | tf_op jit(solution)/shard_map/ppermute | solution.py:14
  260.5 6.2 %collective-permute-start.1 = (bf16[64,3072]{1,0:T(8,128)(2,1)S(1)}, bf16[64,3072]{1,0:T(8,128)(2,1)S(1)}, u32[]{:S(2)}, u32[]{:S(2)}) collective-permute-start(bf16[64,3072]{1,0:T(8,128)(2,1)S(1)} %get-tuple-element.17), channel_id=1, source_target_pairs={{0,248},{8,240},{16,232},{24,224},{32,216},{40,208},{48,200},{56,1... | collective-permute-start | bytes 1179656 | tf_op jit(solution)/shard_map/ppermute | solution.py:120
  266.7 5.2 %fusion = bf16[1,6144,384]{2,1,0:T(8,128)(2,1)} fusion(bf16[512,6144]{1,0:T(8,128)(2,1)S(1)} %copy-done.6, bf16[512,384]{1,0:T(8,128)(2,1)S(1)} %copy-done.12), kind=kOutput, calls=%fused_computation.5 | convolution fusion | flops 2418278400 | bytes 11403264 | tf_op jit(solution)/shard_map/dot_general | solution.py:122
  271.9 13.2 %collective-permute-done.1 = bf16[64,3072]{1,0:T(8,128)(2,1)S(1)} collective-permute-done((bf16[64,3072]{1,0:T(8,128)(2,1)S(1)}, bf16[64,3072]{1,0:T(8,128)(2,1)S(1)}, u32[]{:S(2)}, u32[]{:S(2)}) %collective-permute-start.1) | collective-permute-done | bytes 393248 | tf_op jit(solution)/shard_map/ppermute | solution.py:120
  285.1 4.2 %collective-permute-done = bf16[64,3072]{1,0:T(8,128)(2,1)S(1)} collective-permute-done((bf16[64,3072]{1,0:T(8,128)(2,1)S(1)}, bf16[64,3072]{1,0:T(8,128)(2,1)S(1)}, u32[]{:S(2)}, u32[]{:S(2)}) %collective-permute-start) | collective-permute-done | bytes 393248 | tf_op jit(solution)/shard_map/ppermute | solution.py:14
  (66 shorter events, 19.9 us)
Async XLA Ops:
  6.3 6.7 %copy-start.7 = (bf16[1,64,3072]{2,1,0:T(8,128)(2,1)S(1)}, bf16[1,64,3072]{2,1,0:T(8,128)(2,1)}, u32[]{:S(2)}) copy-start(bf16[1,64,3072]{2,1,0:T(8,128)(2,1)} %param.7) | copy-start | bytes 1179652
  6.3 6.9 %copy-start.11 = (f32[1,3072]{1,0:T(1,128)S(1)}, f32[1,3072]{1,0:T(1,128)}, u32[]{:S(2)}) copy-start(f32[1,3072]{1,0:T(1,128)} %param.9) | copy-start | bytes 36868
  6.3 7.0 %copy-start.10 = (bf16[1,64,3072]{2,1,0:T(8,128)(2,1)S(1)}, bf16[1,64,3072]{2,1,0:T(8,128)(2,1)}, u32[]{:S(2)}) copy-start(bf16[1,64,3072]{2,1,0:T(8,128)(2,1)} %param.8) | copy-start | bytes 1179652
  6.3 80.6 %all-to-all-start = ((bf16[8,64,6528]{2,1,0:T(8,128)(2,1)}), bf16[8,64,6528]{2,1,0:T(8,128)(2,1)}, u32[]{:S(2)}, u32[]{:S(2)}) async-start(bf16[8,64,6528]{2,1,0:T(8,128)(2,1)} %pad_select_fusion), calls=%async_computation | async-start | bytes 13369344 | tf_op jit(solution)/shard_map/all_to_all | solution.py:43
  87.0 76.0 %all-to-all-start.2 = ((bf16[8,64,6144]{2,1,0:T(8,128)(2,1)}), bf16[8,64,6144]{2,1,0:T(8,128)(2,1)}, u32[]{:S(2)}, u32[]{:S(2)}) async-start(bf16[8,64,6144]{2,1,0:T(8,128)(2,1)} %broadcast_select_fusion), calls=%async_computation.2 | async-start | bytes 12582912 | tf_op jit(solution)/shard_map/all_to_all | solution.py:43
  96.5 3.3 %slice-start = ((s8[4718592]{0:T(1024)(128)(4,1)}), s8[4194304]{0:T(1024)(128)(4,1)S(1)}, s32[]{:S(2)}) async-start(s8[4718592]{0:T(1024)(128)(4,1)} %bitcast.89), calls=%async_computation.4 | async-start | bytes 8388608
  96.8 7.7 %copy-start.2 = (bf16[512,3072]{1,0:T(8,128)(2,1)}, bf16[512,3072]{1,0:T(8,128)(2,1)S(1)}, u32[]{:S(2)}) copy-start(bf16[512,3072]{1,0:T(8,128)(2,1)S(1)} %slice.50) | copy-start | bytes 9437188
  96.8 3.1 %slice-start.1 = ((s8[4718592]{0:T(1024)(128)(4,1)}), s8[524288]{0:T(1024)(128)(4,1)S(1)}, s32[]{:S(2)}) async-start(s8[4718592]{0:T(1024)(128)(4,1)} %bitcast.89), calls=%async_computation.5 | async-start | bytes 1048576
  99.9 4.6 %copy-start.4 = (bf16[512,3072]{1,0:T(8,128)(2,1)}, bf16[512,3072]{1,0:T(8,128)(2,1)S(1)}, u32[]{:S(2)}) copy-start(bf16[512,3072]{1,0:T(8,128)(2,1)S(1)} %fusion.3) | copy-start | bytes 9437188
  162.9 42.5 %all-to-all-start.1 = ((bf16[8,64,3200]{2,1,0:T(8,128)(2,1)}), bf16[8,64,3200]{2,1,0:T(8,128)(2,1)S(1)}, u32[]{:S(2)}, u32[]{:S(2)}) async-start(bf16[8,64,3200]{2,1,0:T(8,128)(2,1)} %pad_maximum_fusion.2), calls=%async_computation.1 | async-start | bytes 6553600 | tf_op jit(solution)/shard_map/all_to_all | solution.py:43
  167.1 7.8 %copy-start.1 = (bf16[512,3072]{1,0:T(8,128)(2,1)S(1)}, bf16[512,3072]{1,0:T(8,128)(2,1)}, u32[]{:S(2)}) copy-start(bf16[512,3072]{1,0:T(8,128)(2,1)} %get-tuple-element.21) | copy-start | bytes 9437188
  205.4 1.7 copy-start
  207.1 51.4 %all-to-all-start.3 = ((bf16[8,64,3456]{2,1,0:T(8,128)(2,1)}), bf16[8,64,3456]{2,1,0:T(8,128)(2,1)S(1)}, u32[]{:S(2)}, u32[]{:S(2)}) async-start(bf16[8,64,3456]{2,1,0:T(8,128)(2,1)} %pad_maximum_fusion.1), calls=%async_computation.3 | async-start | bytes 7077888 | tf_op jit(solution)/shard_map/all_to_all | solution.py:43
  211.3 12.7 %copy-start.3 = (bf16[512,3072]{1,0:T(8,128)(2,1)S(1)}, bf16[512,3072]{1,0:T(8,128)(2,1)}, u32[]{:S(2)}) copy-start(bf16[512,3072]{1,0:T(8,128)(2,1)} %copy-done.2) | copy-start | bytes 9437188
  211.3 12.7 %copy-start.5 = (bf16[512,3072]{1,0:T(8,128)(2,1)S(1)}, bf16[512,3072]{1,0:T(8,128)(2,1)}, u32[]{:S(2)}) copy-start(bf16[512,3072]{1,0:T(8,128)(2,1)} %copy-done.4) | copy-start | bytes 9437188
  216.8 41.0 %collective-permute-start.2 = (bf16[64,3072]{1,0:T(8,128)(2,1)S(1)}, bf16[64,3072]{1,0:T(8,128)(2,1)S(1)}, u32[]{:S(2)}, u32[]{:S(2)}) collective-permute-start(bf16[64,3072]{1,0:T(8,128)(2,1)S(1)} %fusion.29), channel_id=1, source_target_pairs={{8,0},{16,8},{24,16},{32,24},{40,32},{48,40},{56,48},{64,56},{72,6... | collective-permute-start | bytes 1179656 | tf_op jit(solution)/shard_map/ppermute | solution.py:14
  257.8 0.7 copy-start.8
  258.5 8.2 %copy-start.6 = (bf16[512,6144]{1,0:T(8,128)(2,1)S(1)}, bf16[512,6144]{1,0:T(8,128)(2,1)}, u32[]{:S(2)}) copy-start(bf16[512,6144]{1,0:T(8,128)(2,1)} %pad_maximum_fusion) | copy-start | bytes 18874372
  258.5 8.2 %copy-start.12 = (bf16[512,384]{1,0:T(8,128)(2,1)S(1)}, bf16[512,384]{1,0:T(8,128)(2,1)}, u32[]{:S(2)}) copy-start(bf16[512,384]{1,0:T(8,128)(2,1)} %get-tuple-element.14) | copy-start | bytes 1179652
  260.5 24.6 %collective-permute-start.1 = (bf16[64,3072]{1,0:T(8,128)(2,1)S(1)}, bf16[64,3072]{1,0:T(8,128)(2,1)S(1)}, u32[]{:S(2)}, u32[]{:S(2)}) collective-permute-start(bf16[64,3072]{1,0:T(8,128)(2,1)S(1)} %get-tuple-element.17), channel_id=1, source_target_pairs={{0,248},{8,240},{16,232},{24,224},{32,216},{40,208},{48,200},{56,1... | collective-permute-start | bytes 1179656 | tf_op jit(solution)/shard_map/ppermute | solution.py:120
  266.7 24.1 %copy-start.9 = (bf16[64,3072]{1,0:T(8,128)(2,1)S(1)}, bf16[64,3072]{1,0:T(8,128)(2,1)}, u32[]{:S(2)}) copy-start(bf16[64,3072]{1,0:T(8,128)(2,1)} %copy-done.8) | copy-start | bytes 1179652
  266.7 22.6 %collective-permute-start = (bf16[64,3072]{1,0:T(8,128)(2,1)S(1)}, bf16[64,3072]{1,0:T(8,128)(2,1)S(1)}, u32[]{:S(2)}, u32[]{:S(2)}) collective-permute-start(bf16[64,3072]{1,0:T(8,128)(2,1)S(1)} %get-tuple-element.18), channel_id=1, source_target_pairs={{248,0},{0,8},{8,16},{16,24},{24,32},{32,40},{40,48},{48,56},{56,6... | collective-permute-start | bytes 1179656 | tf_op jit(solution)/shard_map/ppermute | solution.py:14

commit v8 on v6

--- a/solution.py
+++ b/solution.py
@@ -90,7 +90,7 @@
 
     chunks_a = jnp.concatenate(
         [
-            term[:, :width].reshape(count, rows, width),
+            term.reshape(count, rows, 2 * width),
             jnp.broadcast_to(gain_tile[None], (count, rows, lanes)),
         ],
         axis=2,
@@ -98,7 +98,8 @@
     chunks_a, weight_grads = lax.optimization_barrier((chunks_a, weight_grads))
     got_a = exchange(chunks_a, "tensor")
     dnormed = jnp.sum(got_a[:, :, :width].astype(jnp.float32), axis=0)
-    shares = got_a[:, :gain_rows, width:].reshape(count, 2 * width).astype(jnp.float32)
+    dside = jnp.sum(got_a[:, :, width : 2 * width].astype(jnp.float32), axis=0).astype(jnp.bfloat16)
+    shares = got_a[:, :gain_rows, 2 * width :].reshape(count, 2 * width).astype(jnp.float32)
     gain_grad = jnp.sum(shares[:, :width] + shares[:, width:], axis=0)
     bfloat, brinv, _ = normalize(back_acts[0], gain)
     scaled = gain * dnormed
@@ -111,13 +112,10 @@
     hidden = jnp.dot(joined_all, weight_all, preferred_element_type=jnp.float32)
     update = gelu_value(hidden).astype(jnp.bfloat16)
 
-    chunks_b = jnp.concatenate(
-        [term[:, width:].reshape(count, rows, width), update.reshape(count, rows, block_cols)], axis=2
-    )
-    got_a, chunks_b = lax.optimization_barrier((got_a, chunks_b))
-    got_b2 = exchange(chunks_b, "tensor")
-    dside = jnp.sum(got_b2[:, :, :width].astype(jnp.float32), axis=0).astype(jnp.bfloat16)
-    update_rows = got_b2[:, :, width:].transpose(1, 0, 2).reshape(rows, width)
+    chunks_u = update.reshape(count, rows, block_cols)
+    got_a, chunks_u = lax.optimization_barrier((got_a, chunks_u))
+    got_u = exchange(chunks_u, "tensor")
+    update_rows = got_u.transpose(1, 0, 2).reshape(rows, width)
     out_rows = (xfloat + update_rows.astype(jnp.float32)).astype(jnp.bfloat16)
     received = shifted(out_rows, "section", 1)
     payload = jnp.where(section_idx < middle, out_rows, dside)

time: 292 us -> 290 us (level)
  waiting for transfers between devices: 195 us -> 202 us
  local copies, waits for them, and re-layouts: 13.4 us -> 8.18 us
    all_to_all x4, waiting for transfers between devices: 171 us -> 177 us  [exchange(): lax.all_to_all(chunks.reshape(count * rows, cols), axis, 0, 0, tiled=True)]
    ppermute x1, starting transfers between devices: 6.2 us -> 1.14 us  [on_device(): lax.ppermute(payload, 'section', [(s, sections - 1 - s) for s in range(se...]
    unnamed x25 -> x23, local copies, waits for them, and re-layouts: 6.67 us -> 3.54 us
  transfers between devices with their start and end apart: 7 -> 7, of which waited for: 6 -> 6; matrix products, arithmetic and copies ran while one was open for 17% -> 16% of each run, Pallas kernels for 0% -> 0%
where the time goes in v8:
time: 290 us; the launch traced here: 289 us
  waiting for transfers between devices  202 us (70%)
  starting transfers between devices  31.4 us (11%)
  matrix products  24.6 us (8%)
  other arithmetic  22 us (8%)
  local copies, waits for them, and re-layouts  8.18 us (3%)
    all_to_all x4, waiting for transfers between devices, exchange(): lax.all_to_all(chunks.reshape(count * rows, cols), axis, 0, 0, tiled=True)  177 us
    all_to_all x4, starting transfers between devices, exchange(): lax.all_to_all(chunks.reshape(count * rows, cols), axis, 0, 0, tiled=True)  21.3 us
    ppermute x1, waiting for transfers between devices, on_device(): lax.ppermute(payload, 'section', [(s, sections - 1 - s) for s in range(se...  18.4 us
    ppermute x2, starting transfers between devices, shifted(): return lax.ppermute(block, axis, route)  9.01 us
    dot_general x1, matrix products, on_device(): hidden = jnp.dot(joined_all, weight_all, preferred_element_type=jnp.float32)  8.5 us
    ppermute x2, waiting for transfers between devices, shifted(): return lax.ppermute(block, axis, route)  6.66 us
    dot_general x1, matrix products, on_device(): lax.dot_general(bfused_all, dhidden, contract, preferred_element_type=jnp...  6.42 us
    dot_general x1, matrix products, on_device(): lax.dot_general(dhidden, weight_all, across, preferred_element_type=jnp.f...  6.25 us
  transfers between devices with their start and end apart: 7, of which 6 were waited for; matrix products, arithmetic and copies ran while one was open for 16% of the time, Pallas kernels for 0%

profile of v8, /device:TPU:32, one launch (start us, length us, event | category | flops | bytes accessed | tf_op | source)
XLA Modules:
  0.0 289.4 jit_solution(15327874091288979122)
XLA Ops:
  1.8 1.3 maximum_maximum_fusion
  3.0 3.3 %pad_select_fusion = bf16[8,64,6528]{2,1,0:T(8,128)(2,1)} fusion(bf16[8,64,384]{2,1,0:T(8,128)(2,1)S(1)} %bitcast.65, pred[6528]{0:T(1024)(128)(4,1)S(1)} %iota_compare_fusion.1, bf16[64,6528]{1,0:T(8,128)(2,1)S(1)} %maximum_maximum_fusion), kind=kLoop, calls=%fused_computation.5 | loop fusion | flops 3342336 | bytes 7920000 | tf_op jit(solution)/shard_map/jit(_where)/select_n | solution.py:64
  6.4 6.6 %all-to-all-start = ((bf16[8,64,6528]{2,1,0:T(8,128)(2,1)}), bf16[8,64,6528]{2,1,0:T(8,128)(2,1)}, u32[]{:S(2)}, u32[]{:S(2)}) async-start(bf16[8,64,6528]{2,1,0:T(8,128)(2,1)} %pad_select_fusion), calls=%async_computation | async-start | bytes 13369344 | tf_op jit(solution)/shard_map/all_to_all | solution.py:43
  13.5 3.2 %broadcast_select_fusion = bf16[8,64,6144]{2,1,0:T(8,128)(2,1)} fusion(pred[8]{0:T(512)(128)(4,1)S(1)} %add_compare_fusion, bf16[64,6144]{1,0:T(8,128)(2,1)S(1)} %pad_maximum_fusion.4), kind=kLoop, calls=%fused_computation.14 | loop fusion | flops 3145728 | bytes 7077896 | tf_op jit(solution)/shard_map/jit(_where)/select_n | solution.py:67
  16.7 70.3 %all-to-all-done = bf16[8,64,6528]{2,1,0:T(8,128)(2,1)} async-done(((bf16[8,64,6528]{2,1,0:T(8,128)(2,1)}), bf16[8,64,6528]{2,1,0:T(8,128)(2,1)}, u32[]{:S(2)}, u32[]{:S(2)}) %all-to-all-start) | async-done | bytes 6684704 | tf_op jit(solution)/shard_map/all_to_all | solution.py:43
  87.0 5.3 %all-to-all-start.2 = ((bf16[8,64,6144]{2,1,0:T(8,128)(2,1)}), bf16[8,64,6144]{2,1,0:T(8,128)(2,1)}, u32[]{:S(2)}, u32[]{:S(2)}) async-start(bf16[8,64,6144]{2,1,0:T(8,128)(2,1)} %broadcast_select_fusion), calls=%async_computation.2 | async-start | bytes 12582912 | tf_op jit(solution)/shard_map/all_to_all | solution.py:43
  93.3 3.2 %slice.31 = bf16[8,64,6144]{2,1,0:T(8,128)(2,1)S(1)} slice(bf16[8,64,6528]{2,1,0:T(8,128)(2,1)} %all-to-all-done), slice={[0:8], [0:64], [0:6144]} | slice | bytes 12582912 | tf_op jit(solution)/shard_map/slice | solution.py:71
  98.9 3.4 %fusion.8 = f32[512,384]{1,0:T(8,128)S(1)} fusion(bf16[1,6144,384]{2,1,0:T(8,128)(2,1)S(1)} %bitcast.82, bf16[512,3072]{1,0:T(8,128)(2,1)S(1)} %slice.41, bf16[512,3072]{1,0:T(8,128)(2,1)S(1)} %fusion.2), kind=kOutput, calls=%fused_computation.18 | convolution fusion | flops 2428502016 | bytes 11796480 | tf_op jit(solution)/shard_map/dot_general | solution.py:75
  102.4 6.2 %convolution_convert_fusion = bf16[512,6144]{1,0:T(8,128)(2,1)S(1)} fusion(bf16[1,6144,384]{2,1,0:T(8,128)(2,1)} %param.10, f32[512,384]{1,0:T(8,128)S(1)} %fusion.8, bf16[512,384]{1,0:T(8,128)(2,1)S(1)} %bitcast.70), kind=kOutput, calls=%fused_computation.3 | convolution fusion | flops 2422996992 | bytes 12189696 | tf_op jit(solution)/shard_map/dot_general | solution.py:82
  108.6 1.4 fusion.4
  110.1 3.3 %pad_maximum_fusion = bf16[8,64,6272]{2,1,0:T(8,128)(2,1)} fusion(bf16[8,64,128]{2,1,0:T(8,128)(2,1)S(1)} %broadcast_in_dim.66, bf16[8,64,6144]{2,1,0:T(8,128)(2,1)S(1)} %bitcast.62), kind=kLoop, calls=%fused_computation.6 | loop fusion | flops 12845056 | bytes 12845056 | tf_op jit(solution)/shard_map/concatenate | solution.py:91
  113.3 6.4 %convolution_convert_fusion.1 = bf16[6144,384]{1,0:T(8,128)(2,1)} fusion(bf16[512,3072]{1,0:T(8,128)(2,1)S(1)} %slice.41, bf16[512,3072]{1,0:T(8,128)(2,1)S(1)} %copy-done.3, f32[512,384]{1,0:T(8,128)S(1)} %fusion.8, bf16[512,384]{1,0:T(8,128)(2,1)S(1)} %bitcast.71), kind=kOutput, calls=%fused_computation.4 | convolution fusion | flops 2434793472 | bytes 12189696 | tf_op jit(solution)/shard_map/dot_general | solution.py:78
  119.8 43.2 %all-to-all-done.2 = bf16[8,64,6144]{2,1,0:T(8,128)(2,1)} async-done(((bf16[8,64,6144]{2,1,0:T(8,128)(2,1)}), bf16[8,64,6144]{2,1,0:T(8,128)(2,1)}, u32[]{:S(2)}, u32[]{:S(2)}) %all-to-all-start.2) | async-done | bytes 6291488 | tf_op jit(solution)/shard_map/all_to_all | solution.py:43
  163.0 5.2 %all-to-all-start.1 = ((bf16[8,64,6272]{2,1,0:T(8,128)(2,1)}), bf16[8,64,6272]{2,1,0:T(8,128)(2,1)}, u32[]{:S(2)}, u32[]{:S(2)}) async-start(bf16[8,64,6272]{2,1,0:T(8,128)(2,1)} %pad_maximum_fusion), calls=%async_computation.1 | async-start | bytes 12845056 | tf_op jit(solution)/shard_map/all_to_all | solution.py:43
  168.2 8.5 %fusion.21 = bf16[512,384]{1,0:T(8,128)(2,1)} fusion(bf16[512,6144]{1,0:T(8,128)(2,1)} %bitcast.12, bf16[1,6144,384]{2,1,0:T(8,128)(2,1)} %param.10), kind=kOutput, calls=%fused_computation.42 | convolution fusion | flops 2417688576 | bytes 11403264 | tf_op jit(solution)/shard_map/dot_general | solution.py:112
  176.7 63.6 %all-to-all-done.1 = bf16[8,64,6272]{2,1,0:T(8,128)(2,1)} async-done(((bf16[8,64,6272]{2,1,0:T(8,128)(2,1)}), bf16[8,64,6272]{2,1,0:T(8,128)(2,1)}, u32[]{:S(2)}, u32[]{:S(2)}) %all-to-all-start.1) | async-done | bytes 6422560 | tf_op jit(solution)/shard_map/all_to_all | solution.py:43
  240.3 4.2 %all-to-all-start.3 = ((bf16[8,64,384]{2,1,0:T(8,128)(2,1)}), bf16[8,64,384]{2,1,0:T(8,128)(2,1)S(1)}, u32[]{:S(2)}, u32[]{:S(2)}) async-start(bf16[8,64,384]{2,1,0:T(8,128)(2,1)} %bitcast.13), calls=%async_computation.3 | async-start | bytes 786432 | tf_op jit(solution)/shard_map/all_to_all | solution.py:43
  244.5 2.5 convert_reduce_fusion
  247.6 7.2 %collective-permute-start.2 = (bf16[64,3072]{1,0:T(8,128)(2,1)S(1)}, bf16[64,3072]{1,0:T(8,128)(2,1)S(1)}, u32[]{:S(2)}, u32[]{:S(2)}) collective-permute-start(bf16[64,3072]{1,0:T(8,128)(2,1)S(1)} %fusion.28), channel_id=1, source_target_pairs={{8,0},{16,8},{24,16},{32,24},{40,32},{48,40},{56,48},{64,56},{72,6... | collective-permute-start | bytes 1179656 | tf_op jit(solution)/shard_map/ppermute | solution.py:14
  254.8 2.4 slice_reduce_fusion
  258.7 1.8 collective-permute-start
  262.1 2.4 collective-permute-done.2
  264.5 18.4 %collective-permute-done.1 = bf16[64,3072]{1,0:T(8,128)(2,1)S(1)} collective-permute-done((bf16[64,3072]{1,0:T(8,128)(2,1)S(1)}, bf16[64,3072]{1,0:T(8,128)(2,1)S(1)}, u32[]{:S(2)}, u32[]{:S(2)}) %collective-permute-start.1) | collective-permute-done | bytes 393248 | tf_op jit(solution)/shard_map/ppermute | solution.py:122
  283.0 4.2 %collective-permute-done = bf16[64,3072]{1,0:T(8,128)(2,1)S(1)} collective-permute-done((bf16[64,3072]{1,0:T(8,128)(2,1)S(1)}, bf16[64,3072]{1,0:T(8,128)(2,1)S(1)}, u32[]{:S(2)}, u32[]{:S(2)}) %collective-permute-start) | collective-permute-done | bytes 393248 | tf_op jit(solution)/shard_map/ppermute | solution.py:14
  (51 shorter events, 10.8 us)
Async XLA Ops:
  6.4 6.7 %copy-start.1 = (bf16[1,64,3072]{2,1,0:T(8,128)(2,1)S(1)}, bf16[1,64,3072]{2,1,0:T(8,128)(2,1)}, u32[]{:S(2)}) copy-start(bf16[1,64,3072]{2,1,0:T(8,128)(2,1)} %param.7) | copy-start | bytes 1179652
  6.4 6.9 %copy-start.6 = (f32[1,3072]{1,0:T(1,128)S(1)}, f32[1,3072]{1,0:T(1,128)}, u32[]{:S(2)}) copy-start(f32[1,3072]{1,0:T(1,128)} %param.9) | copy-start | bytes 36868
  6.4 7.0 %copy-start.5 = (bf16[1,64,3072]{2,1,0:T(8,128)(2,1)S(1)}, bf16[1,64,3072]{2,1,0:T(8,128)(2,1)}, u32[]{:S(2)}) copy-start(bf16[1,64,3072]{2,1,0:T(8,128)(2,1)} %param.8) | copy-start | bytes 1179652
  6.4 80.6 %all-to-all-start = ((bf16[8,64,6528]{2,1,0:T(8,128)(2,1)}), bf16[8,64,6528]{2,1,0:T(8,128)(2,1)}, u32[]{:S(2)}, u32[]{:S(2)}) async-start(bf16[8,64,6528]{2,1,0:T(8,128)(2,1)} %pad_select_fusion), calls=%async_computation | async-start | bytes 13369344 | tf_op jit(solution)/shard_map/all_to_all | solution.py:43
  87.0 76.0 %all-to-all-start.2 = ((bf16[8,64,6144]{2,1,0:T(8,128)(2,1)}), bf16[8,64,6144]{2,1,0:T(8,128)(2,1)}, u32[]{:S(2)}, u32[]{:S(2)}) async-start(bf16[8,64,6144]{2,1,0:T(8,128)(2,1)} %broadcast_select_fusion), calls=%async_computation.2 | async-start | bytes 12582912 | tf_op jit(solution)/shard_map/all_to_all | solution.py:43
  96.5 2.2 slice-start
  96.8 2.1 slice-start.1
  98.9 3.5 %copy-start.2 = (bf16[512,3072]{1,0:T(8,128)(2,1)}, bf16[512,3072]{1,0:T(8,128)(2,1)S(1)}, u32[]{:S(2)}) copy-start(bf16[512,3072]{1,0:T(8,128)(2,1)S(1)} %fusion.2) | copy-start | bytes 9437188
  110.0 3.3 %copy-start.3 = (bf16[512,3072]{1,0:T(8,128)(2,1)S(1)}, bf16[512,3072]{1,0:T(8,128)(2,1)}, u32[]{:S(2)}) copy-start(bf16[512,3072]{1,0:T(8,128)(2,1)} %copy-done.2) | copy-start | bytes 9437188
  163.0 77.3 %all-to-all-start.1 = ((bf16[8,64,6272]{2,1,0:T(8,128)(2,1)}), bf16[8,64,6272]{2,1,0:T(8,128)(2,1)}, u32[]{:S(2)}, u32[]{:S(2)}) async-start(bf16[8,64,6272]{2,1,0:T(8,128)(2,1)} %pad_maximum_fusion), calls=%async_computation.1 | async-start | bytes 12845056 | tf_op jit(solution)/shard_map/all_to_all | solution.py:43
  168.2 78.8 %copy-start = (bf16[1,64,3072]{2,1,0:T(8,128)(2,1)S(1)}, bf16[1,64,3072]{2,1,0:T(8,128)(2,1)}, u32[]{:S(2)}) copy-start(bf16[1,64,3072]{2,1,0:T(8,128)(2,1)} %param.11) | copy-start | bytes 1179652
  168.2 79.1 %copy-start.4 = (bf16[1,64,3072]{2,1,0:T(8,128)(2,1)S(1)}, bf16[1,64,3072]{2,1,0:T(8,128)(2,1)}, u32[]{:S(2)}) copy-start(bf16[1,64,3072]{2,1,0:T(8,128)(2,1)} %param.13) | copy-start | bytes 1179652
  240.3 16.9 %all-to-all-start.3 = ((bf16[8,64,384]{2,1,0:T(8,128)(2,1)}), bf16[8,64,384]{2,1,0:T(8,128)(2,1)S(1)}, u32[]{:S(2)}, u32[]{:S(2)}) async-start(bf16[8,64,384]{2,1,0:T(8,128)(2,1)} %bitcast.13), calls=%async_computation.3 | async-start | bytes 786432 | tf_op jit(solution)/shard_map/all_to_all | solution.py:43
  247.6 16.9 %collective-permute-start.2 = (bf16[64,3072]{1,0:T(8,128)(2,1)S(1)}, bf16[64,3072]{1,0:T(8,128)(2,1)S(1)}, u32[]{:S(2)}, u32[]{:S(2)}) collective-permute-start(bf16[64,3072]{1,0:T(8,128)(2,1)S(1)} %fusion.28), channel_id=1, source_target_pairs={{8,0},{16,8},{24,16},{32,24},{40,32},{48,40},{56,48},{64,56},{72,6... | collective-permute-start | bytes 1179656 | tf_op jit(solution)/shard_map/ppermute | solution.py:14
  257.5 25.4 %collective-permute-start.1 = (bf16[64,3072]{1,0:T(8,128)(2,1)S(1)}, bf16[64,3072]{1,0:T(8,128)(2,1)S(1)}, u32[]{:S(2)}, u32[]{:S(2)}) collective-permute-start(bf16[64,3072]{1,0:T(8,128)(2,1)S(1)} %get-tuple-element.17), channel_id=1, source_target_pairs={{0,248},{8,240},{16,232},{24,224},{32,216},{40,208},{48,200},{56,1... | collective-permute-start | bytes 1179656 | tf_op jit(solution)/shard_map/ppermute | solution.py:122
  258.7 28.5 %collective-permute-start = (bf16[64,3072]{1,0:T(8,128)(2,1)S(1)}, bf16[64,3072]{1,0:T(8,128)(2,1)S(1)}, u32[]{:S(2)}, u32[]{:S(2)}) collective-permute-start(bf16[64,3072]{1,0:T(8,128)(2,1)S(1)} %get-tuple-element.18), channel_id=1, source_target_pairs={{248,0},{0,8},{8,16},{16,24},{24,32},{32,40},{40,48},{48,56},{56,6... | collective-permute-start | bytes 1179656 | tf_op jit(solution)/shard_map/ppermute | solution.py:14

commit v9 on v8

--- a/solution.py
+++ b/solution.py
@@ -88,19 +88,11 @@
     gain_tile = jnp.concatenate([part_hi, part_lo]).reshape(gain_rows, lanes)
     gain_tile = jnp.pad(gain_tile, ((0, rows - gain_rows), (0, 0)))
 
-    chunks_a = jnp.concatenate(
-        [
-            term.reshape(count, rows, 2 * width),
-            jnp.broadcast_to(gain_tile[None], (count, rows, lanes)),
-        ],
-        axis=2,
-    )
+    chunks_a = term.reshape(count, rows, 2 * width)
     chunks_a, weight_grads = lax.optimization_barrier((chunks_a, weight_grads))
     got_a = exchange(chunks_a, "tensor")
     dnormed = jnp.sum(got_a[:, :, :width].astype(jnp.float32), axis=0)
     dside = jnp.sum(got_a[:, :, width : 2 * width].astype(jnp.float32), axis=0).astype(jnp.bfloat16)
-    shares = got_a[:, :gain_rows, 2 * width :].reshape(count, 2 * width).astype(jnp.float32)
-    gain_grad = jnp.sum(shares[:, :width] + shares[:, width:], axis=0)
     bfloat, brinv, _ = normalize(back_acts[0], gain)
     scaled = gain * dnormed
     dnorm_in = brinv * scaled - bfloat * brinv * brinv * brinv * jnp.mean(
@@ -112,10 +104,15 @@
     hidden = jnp.dot(joined_all, weight_all, preferred_element_type=jnp.float32)
     update = gelu_value(hidden).astype(jnp.bfloat16)
 
-    chunks_u = update.reshape(count, rows, block_cols)
+    chunks_u = jnp.concatenate(
+        [update.reshape(count, rows, block_cols), jnp.broadcast_to(gain_tile[None], (count, rows, lanes))],
+        axis=2,
+    )
     got_a, chunks_u = lax.optimization_barrier((got_a, chunks_u))
     got_u = exchange(chunks_u, "tensor")
-    update_rows = got_u.transpose(1, 0, 2).reshape(rows, width)
+    update_rows = got_u[:, :, :block_cols].transpose(1, 0, 2).reshape(rows, width)
+    shares = got_u[:, :gain_rows, block_cols:].reshape(count, 2 * width).astype(jnp.float32)
+    gain_grad = jnp.sum(shares[:, :width] + shares[:, width:], axis=0)
     out_rows = (xfloat + update_rows.astype(jnp.float32)).astype(jnp.bfloat16)
     received = shifted(out_rows, "section", 1)
     payload = jnp.where(section_idx < middle, out_rows, dside)

time: 290 us -> 290 us (level)
  no operation moved by 1% of the time
where the time goes in v9:
time: 290 us; the launch traced here: 289 us
  waiting for transfers between devices  200 us (69%)
  starting transfers between devices  32.7 us (11%)
  matrix products  23.4 us (8%)
  other arithmetic  21.5 us (7%)
  local copies, waits for them, and re-layouts  10.3 us (4%)
    all_to_all x4, waiting for transfers between devices, exchange(): lax.all_to_all(chunks.reshape(count * rows, cols), axis, 0, 0, tiled=True)  174 us
    all_to_all x4, starting transfers between devices, exchange(): lax.all_to_all(chunks.reshape(count * rows, cols), axis, 0, 0, tiled=True)  21.2 us
    ppermute x1, waiting for transfers between devices, on_device(): lax.ppermute(payload, 'section', [(s, sections - 1 - s) for s in range(se...  20.8 us
    ppermute x2, starting transfers between devices, shifted(): return lax.ppermute(block, axis, route)  8.01 us
    dot_general x1, matrix products, on_device(): hidden = jnp.dot(joined_all, weight_all, preferred_element_type=jnp.float32)  7.68 us
    dot_general x1, matrix products, on_device(): lax.dot_general(bfused_all, dhidden, contract, preferred_element_type=jnp...  6.5 us
    dot_general x1, matrix products, on_device(): lax.dot_general(dhidden, weight_all, across, preferred_element_type=jnp.f...  5.85 us
  transfers between devices with their start and end apart: 7, of which 6 were waited for; matrix products, arithmetic and copies ran while one was open for 16% of the time, Pallas kernels for 0%

profile of v9, /device:TPU:32, one launch (start us, length us, event | category | flops | bytes accessed | tf_op | source)
XLA Modules:
  0.0 289.3 jit_solution(5515450746024619602)
XLA Ops:
  1.8 1.3 maximum_maximum_fusion
  3.0 3.3 %pad_select_fusion = bf16[8,64,6528]{2,1,0:T(8,128)(2,1)} fusion(bf16[8,64,384]{2,1,0:T(8,128)(2,1)S(1)} %bitcast.65, pred[6528]{0:T(1024)(128)(4,1)S(1)} %iota_compare_fusion.1, bf16[64,6528]{1,0:T(8,128)(2,1)S(1)} %maximum_maximum_fusion), kind=kLoop, calls=%fused_computation.5 | loop fusion | flops 3342336 | bytes 7920000 | tf_op jit(solution)/shard_map/jit(_where)/select_n | solution.py:64
  6.4 6.6 %all-to-all-start = ((bf16[8,64,6528]{2,1,0:T(8,128)(2,1)}), bf16[8,64,6528]{2,1,0:T(8,128)(2,1)}, u32[]{:S(2)}, u32[]{:S(2)}) async-start(bf16[8,64,6528]{2,1,0:T(8,128)(2,1)} %pad_select_fusion), calls=%async_computation | async-start | bytes 13369344 | tf_op jit(solution)/shard_map/all_to_all | solution.py:43
  13.5 3.2 %broadcast_select_fusion = bf16[8,64,6144]{2,1,0:T(8,128)(2,1)} fusion(pred[8]{0:T(512)(128)(4,1)S(1)} %add_compare_fusion, bf16[64,6144]{1,0:T(8,128)(2,1)S(1)} %pad_maximum_fusion.3), kind=kLoop, calls=%fused_computation.13 | loop fusion | flops 3145728 | bytes 7077896 | tf_op jit(solution)/shard_map/jit(_where)/select_n | solution.py:67
  16.6 70.3 %all-to-all-done = bf16[8,64,6528]{2,1,0:T(8,128)(2,1)} async-done(((bf16[8,64,6528]{2,1,0:T(8,128)(2,1)}), bf16[8,64,6528]{2,1,0:T(8,128)(2,1)}, u32[]{:S(2)}, u32[]{:S(2)}) %all-to-all-start) | async-done | bytes 6684704 | tf_op jit(solution)/shard_map/all_to_all | solution.py:43
  87.0 5.2 %all-to-all-start.2 = ((bf16[8,64,6144]{2,1,0:T(8,128)(2,1)}), bf16[8,64,6144]{2,1,0:T(8,128)(2,1)}, u32[]{:S(2)}, u32[]{:S(2)}) async-start(bf16[8,64,6144]{2,1,0:T(8,128)(2,1)} %broadcast_select_fusion), calls=%async_computation.2 | async-start | bytes 12582912 | tf_op jit(solution)/shard_map/all_to_all | solution.py:43
  93.2 3.2 %slice.34 = bf16[8,64,6144]{2,1,0:T(8,128)(2,1)S(1)} slice(bf16[8,64,6528]{2,1,0:T(8,128)(2,1)} %all-to-all-done), slice={[0:8], [0:64], [0:6144]} | slice | bytes 12582912 | tf_op jit(solution)/shard_map/slice | solution.py:71
  97.4 1.3 fusion.2
  98.7 2.2 slice-done
  101.0 3.4 %fusion.8 = f32[512,384]{1,0:T(8,128)S(1)} fusion(bf16[1,6144,384]{2,1,0:T(8,128)(2,1)S(1)} %bitcast.83, bf16[512,3072]{1,0:T(8,128)(2,1)S(1)} %slice.45, bf16[512,3072]{1,0:T(8,128)(2,1)S(1)} %fusion.2), kind=kOutput, calls=%fused_computation.17 | convolution fusion | flops 2428502016 | bytes 11796480 | tf_op jit(solution)/shard_map/dot_general | solution.py:75
  104.4 5.9 %convolution_convert_fusion = bf16[512,6144]{1,0:T(8,128)(2,1)} fusion(bf16[1,6144,384]{2,1,0:T(8,128)(2,1)S(1)} %bitcast.83, f32[512,384]{1,0:T(8,128)S(1)} %fusion.8, bf16[512,384]{1,0:T(8,128)(2,1)S(1)} %bitcast.72), kind=kOutput, calls=%fused_computation.3 | convolution fusion | flops 2422996992 | bytes 12189696 | tf_op jit(solution)/shard_map/dot_general | solution.py:82
  110.3 6.5 %convolution_convert_fusion.1 = bf16[6144,384]{1,0:T(8,128)(2,1)} fusion(bf16[512,3072]{1,0:T(8,128)(2,1)S(1)} %slice.45, bf16[512,3072]{1,0:T(8,128)(2,1)S(1)} %fusion.2, f32[512,384]{1,0:T(8,128)S(1)} %fusion.8, bf16[512,384]{1,0:T(8,128)(2,1)S(1)} %bitcast.73), kind=kOutput, calls=%fused_computation.4 | convolution fusion | flops 2434793472 | bytes 12189696 | tf_op jit(solution)/shard_map/dot_general | solution.py:78
  116.8 46.1 %all-to-all-done.2 = bf16[8,64,6144]{2,1,0:T(8,128)(2,1)} async-done(((bf16[8,64,6144]{2,1,0:T(8,128)(2,1)}), bf16[8,64,6144]{2,1,0:T(8,128)(2,1)}, u32[]{:S(2)}, u32[]{:S(2)}) %all-to-all-start.2) | async-done | bytes 6291488 | tf_op jit(solution)/shard_map/all_to_all | solution.py:43
  162.9 5.2 %all-to-all-start.1 = ((bf16[8,64,6144]{2,1,0:T(8,128)(2,1)}), bf16[8,64,6144]{2,1,0:T(8,128)(2,1)}, u32[]{:S(2)}, u32[]{:S(2)}) async-start(bf16[8,64,6144]{2,1,0:T(8,128)(2,1)} %bitcast.62), calls=%async_computation.1 | async-start | bytes 12582912 | tf_op jit(solution)/shard_map/all_to_all | solution.py:43
  168.1 4.2 %fusion.4 = f32[3072]{0:T(1024)S(1)} fusion(bf16[512,6144]{1,0:T(8,128)(2,1)} %convolution_convert_fusion, f32[512]{0:T(512)S(1)} %add_rsqrt_fusion, bf16[512,6144]{1,0:T(8,128)(2,1)} %bitcast.61), kind=kLoop, calls=%fused_computation.10 | loop fusion | flops 7861248 | bytes 6305792 | tf_op jit(solution)/shard_map/reduce_sum | solution.py:85
  172.3 7.7 %fusion.21 = bf16[512,384]{1,0:T(8,128)(2,1)S(1)} fusion(bf16[512,6144]{1,0:T(8,128)(2,1)} %bitcast.11, bf16[1,6144,384]{2,1,0:T(8,128)(2,1)} %param.10), kind=kOutput, calls=%fused_computation.41 | convolution fusion | flops 2417688576 | bytes 11403264 | tf_op jit(solution)/shard_map/dot_general | solution.py:104
  180.9 57.9 %all-to-all-done.1 = bf16[8,64,6144]{2,1,0:T(8,128)(2,1)} async-done(((bf16[8,64,6144]{2,1,0:T(8,128)(2,1)}), bf16[8,64,6144]{2,1,0:T(8,128)(2,1)}, u32[]{:S(2)}, u32[]{:S(2)}) %all-to-all-start.1) | async-done | bytes 6291488 | tf_op jit(solution)/shard_map/all_to_all | solution.py:43
  238.8 4.2 %all-to-all-start.3 = ((bf16[8,64,512]{2,1,0:T(8,128)(2,1)}), bf16[8,64,512]{2,1,0:T(8,128)(2,1)S(1)}, u32[]{:S(2)}, u32[]{:S(2)}) async-start(bf16[8,64,512]{2,1,0:T(8,128)(2,1)} %pad_maximum_fusion.4), calls=%async_computation.3 | async-start | bytes 1048576 | tf_op jit(solution)/shard_map/all_to_all | solution.py:43
  243.0 2.5 convert_reduce_fusion
  246.1 7.2 %collective-permute-start.2 = (bf16[64,3072]{1,0:T(8,128)(2,1)S(1)}, bf16[64,3072]{1,0:T(8,128)(2,1)S(1)}, u32[]{:S(2)}, u32[]{:S(2)}) collective-permute-start(bf16[64,3072]{1,0:T(8,128)(2,1)S(1)} %fusion.28), channel_id=1, source_target_pairs={{8,0},{16,8},{24,16},{32,24},{40,32},{48,40},{56,48},{64,56},{72,6... | collective-permute-start | bytes 1179656 | tf_op jit(solution)/shard_map/ppermute | solution.py:14
  253.4 2.4 slice_reduce_fusion
  256.0 3.5 %collective-permute-start.1 = (bf16[64,3072]{1,0:T(8,128)(2,1)S(1)}, bf16[64,3072]{1,0:T(8,128)(2,1)S(1)}, u32[]{:S(2)}, u32[]{:S(2)}) collective-permute-start(bf16[64,3072]{1,0:T(8,128)(2,1)S(1)} %get-tuple-element.17), channel_id=1, source_target_pairs={{0,248},{8,240},{16,232},{24,224},{32,216},{40,208},{48,200},{56,1... | collective-permute-start | bytes 1179656 | tf_op jit(solution)/shard_map/ppermute | solution.py:119
  262.0 20.8 %collective-permute-done.1 = bf16[64,3072]{1,0:T(8,128)(2,1)S(1)} collective-permute-done((bf16[64,3072]{1,0:T(8,128)(2,1)S(1)}, bf16[64,3072]{1,0:T(8,128)(2,1)S(1)}, u32[]{:S(2)}, u32[]{:S(2)}) %collective-permute-start.1) | collective-permute-done | bytes 393248 | tf_op jit(solution)/shard_map/ppermute | solution.py:119
  282.8 4.2 %collective-permute-done = bf16[64,3072]{1,0:T(8,128)(2,1)S(1)} collective-permute-done((bf16[64,3072]{1,0:T(8,128)(2,1)S(1)}, bf16[64,3072]{1,0:T(8,128)(2,1)S(1)}, u32[]{:S(2)}, u32[]{:S(2)}) %collective-permute-start) | collective-permute-done | bytes 393248 | tf_op jit(solution)/shard_map/ppermute | solution.py:14
  (49 shorter events, 10.1 us)
Async XLA Ops:
  6.3 6.7 %copy-start.2 = (bf16[1,64,3072]{2,1,0:T(8,128)(2,1)S(1)}, bf16[1,64,3072]{2,1,0:T(8,128)(2,1)}, u32[]{:S(2)}) copy-start(bf16[1,64,3072]{2,1,0:T(8,128)(2,1)} %param.7) | copy-start | bytes 1179652
  6.4 6.9 %copy-start.5 = (f32[1,3072]{1,0:T(1,128)S(1)}, f32[1,3072]{1,0:T(1,128)}, u32[]{:S(2)}) copy-start(f32[1,3072]{1,0:T(1,128)} %param.9) | copy-start | bytes 36868
  6.4 7.0 %copy-start.4 = (bf16[1,64,3072]{2,1,0:T(8,128)(2,1)S(1)}, bf16[1,64,3072]{2,1,0:T(8,128)(2,1)}, u32[]{:S(2)}) copy-start(bf16[1,64,3072]{2,1,0:T(8,128)(2,1)} %param.8) | copy-start | bytes 1179652
  6.4 80.6 %all-to-all-start = ((bf16[8,64,6528]{2,1,0:T(8,128)(2,1)}), bf16[8,64,6528]{2,1,0:T(8,128)(2,1)}, u32[]{:S(2)}, u32[]{:S(2)}) async-start(bf16[8,64,6528]{2,1,0:T(8,128)(2,1)} %pad_select_fusion), calls=%async_computation | async-start | bytes 13369344 | tf_op jit(solution)/shard_map/all_to_all | solution.py:43
  87.0 75.9 %all-to-all-start.2 = ((bf16[8,64,6144]{2,1,0:T(8,128)(2,1)}), bf16[8,64,6144]{2,1,0:T(8,128)(2,1)}, u32[]{:S(2)}, u32[]{:S(2)}) async-start(bf16[8,64,6144]{2,1,0:T(8,128)(2,1)} %broadcast_select_fusion), calls=%async_computation.2 | async-start | bytes 12582912 | tf_op jit(solution)/shard_map/all_to_all | solution.py:43
  96.4 13.9 %copy-start = (bf16[8,64,6144]{2,1,0:T(8,128)(2,1)}, bf16[8,64,6144]{2,1,0:T(8,128)(2,1)S(1)}, u32[]{:S(2)}) copy-start(bf16[8,64,6144]{2,1,0:T(8,128)(2,1)S(1)} %slice.34) | copy-start | bytes 18874372
  96.4 4.5 %slice-start = ((s8[4718592]{0:T(1024)(128)(4,1)}), s8[4194304]{0:T(1024)(128)(4,1)S(1)}, s32[]{:S(2)}) async-start(s8[4718592]{0:T(1024)(128)(4,1)} %bitcast.82), calls=%async_computation.4 | async-start | bytes 8388608
  96.7 4.3 %slice-start.1 = ((s8[4718592]{0:T(1024)(128)(4,1)}), s8[524288]{0:T(1024)(128)(4,1)S(1)}, s32[]{:S(2)}) async-start(s8[4718592]{0:T(1024)(128)(4,1)} %bitcast.82), calls=%async_computation.5 | async-start | bytes 1048576
  162.9 75.9 %all-to-all-start.1 = ((bf16[8,64,6144]{2,1,0:T(8,128)(2,1)}), bf16[8,64,6144]{2,1,0:T(8,128)(2,1)}, u32[]{:S(2)}, u32[]{:S(2)}) async-start(bf16[8,64,6144]{2,1,0:T(8,128)(2,1)} %bitcast.62), calls=%async_computation.1 | async-start | bytes 12582912 | tf_op jit(solution)/shard_map/all_to_all | solution.py:43
  180.0 65.5 %copy-start.1 = (bf16[1,64,3072]{2,1,0:T(8,128)(2,1)S(1)}, bf16[1,64,3072]{2,1,0:T(8,128)(2,1)}, u32[]{:S(2)}) copy-start(bf16[1,64,3072]{2,1,0:T(8,128)(2,1)} %param.11) | copy-start | bytes 1179652
  180.0 65.8 %copy-start.3 = (bf16[1,64,3072]{2,1,0:T(8,128)(2,1)S(1)}, bf16[1,64,3072]{2,1,0:T(8,128)(2,1)}, u32[]{:S(2)}) copy-start(bf16[1,64,3072]{2,1,0:T(8,128)(2,1)} %param.13) | copy-start | bytes 1179652
  238.8 16.9 %all-to-all-start.3 = ((bf16[8,64,512]{2,1,0:T(8,128)(2,1)}), bf16[8,64,512]{2,1,0:T(8,128)(2,1)S(1)}, u32[]{:S(2)}, u32[]{:S(2)}) async-start(bf16[8,64,512]{2,1,0:T(8,128)(2,1)} %pad_maximum_fusion.4), calls=%async_computation.3 | async-start | bytes 1048576 | tf_op jit(solution)/shard_map/all_to_all | solution.py:43
  246.1 15.2 %collective-permute-start.2 = (bf16[64,3072]{1,0:T(8,128)(2,1)S(1)}, bf16[64,3072]{1,0:T(8,128)(2,1)S(1)}, u32[]{:S(2)}, u32[]{:S(2)}) collective-permute-start(bf16[64,3072]{1,0:T(8,128)(2,1)S(1)} %fusion.28), channel_id=1, source_target_pairs={{8,0},{16,8},{24,16},{32,24},{40,32},{48,40},{56,48},{64,56},{72,6... | collective-permute-start | bytes 1179656 | tf_op jit(solution)/shard_map/ppermute | solution.py:14
  256.0 26.8 %collective-permute-start.1 = (bf16[64,3072]{1,0:T(8,128)(2,1)S(1)}, bf16[64,3072]{1,0:T(8,128)(2,1)S(1)}, u32[]{:S(2)}, u32[]{:S(2)}) collective-permute-start(bf16[64,3072]{1,0:T(8,128)(2,1)S(1)} %get-tuple-element.17), channel_id=1, source_target_pairs={{0,248},{8,240},{16,232},{24,224},{32,216},{40,208},{48,200},{56,1... | collective-permute-start | bytes 1179656 | tf_op jit(solution)/shard_map/ppermute | solution.py:119
  259.6 27.5 %collective-permute-start = (bf16[64,3072]{1,0:T(8,128)(2,1)S(1)}, bf16[64,3072]{1,0:T(8,128)(2,1)S(1)}, u32[]{:S(2)}, u32[]{:S(2)}) collective-permute-start(bf16[64,3072]{1,0:T(8,128)(2,1)S(1)} %get-tuple-element.18), channel_id=1, source_target_pairs={{248,0},{0,8},{8,16},{16,24},{24,32},{32,40},{40,48},{48,56},{56,6... | collective-permute-start | bytes 1179656 | tf_op jit(solution)/shard_map/ppermute | solution.py:14
